TPU v7x, 256 devices: a whole 4x4x8 slice. The times are simulated.
256 devices in a mesh: gx: 8 (over z), gy: 32 (over y, x, core).
Axes of the slice: x: 4, y: 4, z: 8, core: 2. Of those that a mesh axis runs over, the one named last changes fastest.
Arguments:
- saved_pops: bfloat16 [4, 19, 128, 16384], P(None, None, 'gx', 'gy'), may hold values from 0.099609375 to 1.8984375
- seed_adjoint: float32 [19, 128, 16384], P(None, 'gx', 'gy'), may hold values from -6 to 6
- solid_label: int32 [128, 16384], P('gx', 'gy'), may hold values 0 or 1
- design_mask: int32 [128, 16384], P('gx', 'gy'), may hold values 0 or 1
- design_field: float32 [128, 16384], P('gx', 'gy'), may hold values from 0 to 1
Outputs:
- adjoint_out: float32 [19, 128, 16384], P(None, 'gx', 'gy')
- sensitivity: float32 [128, 16384], P('gx', 'gy')
All inputs are finite; a program needn't handle non-finite values. No bound on the sum of `solid_label` or of `design_mask` on one device may be relied on, other than what follows from the above.
Results may differ from a plain program's by a relative error of at most 0.0003.
Values sent between devices are 32-bit elements; how exact they have to be, the bound alone decides.
No kernel may reach another device: no remote copies, remote signals or barrier semaphores. Data moves between devices by JAX's collectives and lax.ppermute only.
A program may use at most 64 MiB of HBM per device.

v0:
```python
import jax
import jax.numpy as jnp
import numpy as np
from jax import lax
from jax.experimental import pallas as pl
from jax.experimental.pallas import tpu as pltpu
from jax.sharding import PartitionSpec as P

NZ = 32


VELOCITIES = np.array(
    [
        [0, 0, 0],
        [1, 0, 0],
        [-1, 0, 0],
        [0, 1, 0],
        [0, -1, 0],
        [0, 0, 1],
        [0, 0, -1],
        [1, 1, 0],
        [1, -1, 0],
        [-1, 1, 0],
        [-1, -1, 0],
        [1, 0, 1],
        [1, 0, -1],
        [-1, 0, 1],
        [-1, 0, -1],
        [0, 1, 1],
        [0, 1, -1],
        [0, -1, 1],
        [0, -1, -1],
    ]
)
LATTICE_WEIGHTS = np.array([1.0 / 3.0] + [1.0 / 18.0] * 6 + [1.0 / 36.0] * 12)
OPPOSITE = np.array([0, 2, 1, 4, 3, 6, 5, 10, 9, 8, 7, 14, 13, 12, 11, 18, 17, 16, 15])
OMEGA_BASE = 1.0
OMEGA_SPAN = 0.8
SENS_SCALE = 10.0

W32 = [float(np.float32(w)) for w in LATTICE_WEIGHTS]
XP = [i for i in range(19) if VELOCITIES[i, 0] == 1]
XM = [i for i in range(19) if VELOCITIES[i, 0] == -1]
YP = [i for i in range(19) if VELOCITIES[i, 1] == 1]
YM = [i for i in range(19) if VELOCITIES[i, 1] == -1]
LANES = 128


def _collide_vjp(f, g, rate, solid):
    rho = f[0]
    for i in range(1, 19):
        rho = rho + f[i]
    mom = []
    for a in range(3):
        pos = [f[i] for i in range(19) if VELOCITIES[i, a] > 0]
        neg = [f[i] for i in range(19) if VELOCITIES[i, a] < 0]
        acc = pos[0]
        for x in pos[1:]:
            acc = acc + x
        for x in neg:
            acc = acc - x
        mom.append(acc)
    u = [m / rho for m in mom]
    usq = u[0] * u[0] + u[1] * u[1] + u[2] * u[2]
    base = 1.0 - 1.5 * usq
    fluid = solid == 0
    one_minus = 1.0 - rate
    rbar = None
    esum = None
    easum = None
    mb = [None, None, None]
    proj = []
    amp = []
    gf = []
    for i in range(19):
        cvec = [int(c) for c in VELOCITIES[i]]
        p = None
        for a in range(3):
            if cvec[a] == 0:
                continue
            term = u[a] if cvec[a] > 0 else -u[a]
            p = term if p is None else p + term
        if p is None:
            amp_i = base
        else:
            amp_i = base + (3.0 + 4.5 * p) * p
        proj.append(p)
        amp.append(amp_i)
        gi = jnp.where(fluid, g[i], 0.0)
        gf.append(gi)
        feq = W32[i] * rho * amp_i
        t = gi * (feq - f[i])
        rbar = t if rbar is None else rbar + t
        e = (rate * W32[i]) * gi
        esum = e if esum is None else esum + e
        ea = e * amp_i
        easum = ea if easum is None else easum + ea
        if p is not None:
            ep = e * (3.0 + 9.0 * p)
            for a in range(3):
                if cvec[a] == 0:
                    continue
                if mb[a] is None:
                    mb[a] = ep if cvec[a] > 0 else -ep
                else:
                    mb[a] = mb[a] + ep if cvec[a] > 0 else mb[a] - ep
    mb = [mb[a] - 3.0 * u[a] * esum for a in range(3)]
    rhobar = easum - (mb[0] * u[0] + mb[1] * u[1] + mb[2] * u[2])
    out = []
    for i in range(19):
        cvec = [int(c) for c in VELOCITIES[i]]
        val = one_minus * gf[i] + rhobar
        for a in range(3):
            if cvec[a] > 0:
                val = val + mb[a]
            elif cvec[a] < 0:
                val = val - mb[a]
        out.append(jnp.where(fluid, val, g[int(OPPOSITE[i])]))
    return out, rbar


DEPTH = 4


def _pull_all(a_ref, p_ref):
    _, rows, flat = a_ref.shape
    zl = lax.broadcasted_iota(jnp.int32, (rows, flat), 1) % NZ
    for i in range(19):
        cx, cy, cz = (int(c) for c in VELOCITIES[i])
        v = a_ref[i]
        if cx != 0:
            v = pltpu.roll(v, (rows - cx) % rows, 0)
        if cy != 0:
            v = pltpu.roll(v, (flat - cy * NZ) % flat, 1)
        if cz == 1:
            v = jnp.where(zl == NZ - 1, pltpu.roll(v, NZ - 1, 1), pltpu.roll(v, flat - 1, 1))
        elif cz == -1:
            v = jnp.where(zl == 0, pltpu.roll(v, flat - NZ + 1, 1), pltpu.roll(v, 1, 1))
        p_ref[i] = v


def _fill_ext(dst, own, hxp, hxm, hyp, hym, rows, flat):
    dst[0:rows, 0:flat] = own
    dst[rows : rows + DEPTH, 0:flat] = hxp
    dst[rows + DEPTH : rows + 2 * DEPTH, 0:flat] = hxm
    dst[:, flat : flat + DEPTH * NZ] = hyp
    dst[:, flat + DEPTH * NZ : flat + 2 * DEPTH * NZ] = hym


def _fused_kernel(pops_ref, seed_ref, solid_ref, mask_ref, field_ref, hxp, hxm, hyp, hym,
                  adj_out, sens_out, a_ref, p_ref, f_ref, rate_ref, solid_ext):
    steps = pops_ref.shape[0]
    _, rows, flat = seed_ref.shape
    erows, eflat = a_ref.shape[1], a_ref.shape[2]
    nfield = hxp.shape[0]
    mask_all = mask_ref[...].astype(jnp.float32)
    rate_own = OMEGA_BASE + OMEGA_SPAN * field_ref[...] * mask_all
    _fill_ext(rate_ref, rate_own, hxp[nfield - 2], hxm[nfield - 2], hyp[nfield - 2],
              hym[nfield - 2], rows, flat)
    _fill_ext(solid_ext, solid_ref[...].astype(jnp.float32), hxp[nfield - 1], hxm[nfield - 1],
              hyp[nfield - 1], hym[nfield - 1], rows, flat)
    for i in range(19):
        _fill_ext(a_ref.at[i], seed_ref[i], hxp[i], hxm[i], hyp[i], hym[i], rows, flat)
    sens_out[...] = jnp.zeros(sens_out.shape, jnp.float32)
    row_tiles = rows // 8
    lane_tiles = flat // LANES
    ext_lane_tiles = eflat // LANES
    n_own = row_tiles * lane_tiles
    n_halo_rows = (erows - rows) // 8 * lane_tiles
    n_halo = n_halo_rows + (erows // 8) * (ext_lane_tiles - lane_tiles)

    def chunk(r0, l0, write_ref, own):
        rs = pl.ds(r0, 8)
        ls = pl.ds(l0, LANES)
        f = [f_ref[i, rs, ls] for i in range(19)]
        g = [p_ref[i, rs, ls] for i in range(19)]
        solid = solid_ext[rs, ls]
        solid_i = jnp.where(solid > 0.5, 1, 0)
        new, rbar = _collide_vjp(f, g, rate_ref[rs, ls], solid_i)
        for i in range(19):
            write_ref[i, rs, ls] = new[i]
        if own:
            mask = mask_ref[rs, ls].astype(jnp.float32)
            contrib = SENS_SCALE * OMEGA_SPAN * mask * jnp.where(solid_i == 0, rbar, 0.0)
            sens_out[rs, ls] = sens_out[rs, ls] + contrib

    for n, step in enumerate(reversed(range(steps))):
        last = step == 0
        for i in range(19):
            own = pops_ref[step, i].astype(jnp.float32) * W32[i]
            if last:
                f_ref[i, 0:rows, 0:flat] = own
            else:
                k = 19 + 19 * (steps - 1 - step) + i
                _fill_ext(f_ref.at[i], own, hxp[k] * W32[i], hxm[k] * W32[i], hyp[k] * W32[i],
                          hym[k] * W32[i], rows, flat)
        _pull_all(a_ref, p_ref)
        write_ref = adj_out if last else a_ref

        def own_body(c, carry, write_ref=write_ref):
            r0 = pl.multiple_of((c // lane_tiles) * 8, 8)
            l0 = pl.multiple_of((c % lane_tiles) * LANES, LANES)
            chunk(r0, l0, write_ref, True)
            return carry

        lax.fori_loop(0, n_own, own_body, 0)
        if not last:

            def halo_body(c, carry):
                c2 = c - n_halo_rows
                ext_w = ext_lane_tiles - lane_tiles
                r = jnp.where(c < n_halo_rows, rows // 8 + c // lane_tiles, c2 // ext_w)
                t = jnp.where(c < n_halo_rows, c % lane_tiles, lane_tiles + c2 % ext_w)
                chunk(pl.multiple_of(r * 8, 8), pl.multiple_of(t * LANES, LANES), a_ref, False)
                return carry

            lax.fori_loop(0, n_halo, halo_body, 0)


def _messages(saved_pops, seed, solid, mask, field):
    steps = saved_pops.shape[0]
    rate = OMEGA_BASE + OMEGA_SPAN * field * mask.astype(jnp.float32)
    parts = [seed] + [saved_pops[s].astype(jnp.float32) for s in reversed(range(1, steps))]
    parts += [rate[None], solid.astype(jnp.float32)[None]]
    return jnp.concatenate(parts, axis=0)


def _shift(n, d):
    return [(i, (i + d) % n) for i in range(n)]


def body(saved_pops, seed_adjoint, solid_label, design_mask, design_field):
    nx = lax.axis_size("gx")
    ny = lax.axis_size("gy")
    _, rows, flat = seed_adjoint.shape
    yw = DEPTH * NZ
    fields = _messages(saved_pops, seed_adjoint, solid_label, design_mask, design_field)
    hxp = lax.ppermute(fields[:, 0:DEPTH, :], "gx", _shift(nx, -1))
    hxm = lax.ppermute(fields[:, rows - DEPTH : rows, :], "gx", _shift(nx, 1))
    col_lo = jnp.concatenate([fields[:, :, 0:yw], hxp[:, :, 0:yw], hxm[:, :, 0:yw]], axis=1)
    col_hi = jnp.concatenate(
        [fields[:, :, flat - yw : flat], hxp[:, :, flat - yw : flat], hxm[:, :, flat - yw : flat]],
        axis=1,
    )
    hyp = lax.ppermute(col_lo, "gy", _shift(ny, -1))
    hym = lax.ppermute(col_hi, "gy", _shift(ny, 1))
    erows = rows + 2 * DEPTH
    eflat = flat + 2 * yw
    ext = (19, erows, eflat)
    args = [saved_pops, seed_adjoint, solid_label, design_mask, design_field, hxp, hxm, hyp, hym]

    def full(shape):
        nd = len(shape)
        return pl.BlockSpec(shape, lambda i, _n=nd: (0,) * _n)

    adjoint, sensitivity = pl.pallas_call(
        _fused_kernel,
        grid=(1,),
        in_specs=[full(a.shape) for a in args],
        out_specs=[full(seed_adjoint.shape), full((rows, flat))],
        out_shape=[
            jax.ShapeDtypeStruct(seed_adjoint.shape, jnp.float32),
            jax.ShapeDtypeStruct((rows, flat), jnp.float32),
        ],
        scratch_shapes=[
            pltpu.VMEM(ext, jnp.float32),
            pltpu.VMEM(ext, jnp.float32),
            pltpu.VMEM(ext, jnp.float32),
            pltpu.VMEM((erows, eflat), jnp.float32),
            pltpu.VMEM((erows, eflat), jnp.float32),
        ],
    )(*args)
    return (adjoint, sensitivity)


def solution(mesh):
    in_specs = (
        P(None, None, "gx", "gy"),
        P(None, "gx", "gy"),
        P("gx", "gy"),
        P("gx", "gy"),
        P("gx", "gy"),
    )
    out_specs = (P(None, "gx", "gy"), P("gx", "gy"))
    return jax.shard_map(body, mesh=mesh, in_specs=in_specs, out_specs=out_specs, check_vma=False)
```

profile of v0, /device:TPU:0, one launch (start us, length us, event | category | flops | bytes accessed | tf_op | source)
XLA Modules:
  0.0 58.8 jit_solution(9434129184865612523)
XLA Ops:
  0.6 0.0 copy-start.5
  0.6 0.0 copy-start.4
  0.7 0.0 copy-start.6
  0.7 1.1 %constant_dynamic-update-slice_fusion = f32[78,16,512]{2,1,0:T(8,128)S(1)} fusion(f32[19,16,512]{2,1,0:T(8,128)} %seed_ref.1), kind=kLoop, calls=%fused_computation.7 | loop fusion | bytes 1245184
  1.8 1.0 %convert_dynamic-update-slice_fusion.2 = f32[78,16,512]{2,1,0:T(8,128)S(1)} fusion(f32[78,16,512]{2,1,0:T(8,128)S(1)} %constant_dynamic-update-slice_fusion, bf16[4,19,16,512]{3,2,1,0:T(8,128)(2,1)} %pops_ref.1), kind=kLoop, calls=%fused_computation.4 | loop fusion | flops 155648 | bytes 933888
  2.8 1.0 %convert_dynamic-update-slice_fusion.1 = f32[78,16,512]{2,1,0:T(8,128)S(1)} fusion(f32[78,16,512]{2,1,0:T(8,128)S(1)} %convert_dynamic-update-slice_fusion.2, bf16[4,19,16,512]{3,2,1,0:T(8,128)(2,1)} %pops_ref.1), kind=kLoop, calls=%fused_computation.3 | loop fusion | flops 155648 | bytes 933888
  3.9 1.0 %convert_dynamic-update-slice_fusion = f32[78,16,512]{2,1,0:T(8,128)S(1)} fusion(f32[78,16,512]{2,1,0:T(8,128)S(1)} %convert_dynamic-update-slice_fusion.1, bf16[4,19,16,512]{3,2,1,0:T(8,128)(2,1)} %pops_ref.1), kind=kLoop, calls=%fused_computation.2 | loop fusion | flops 155648 | bytes 933888
  5.0 0.3 fusion.1
  5.3 0.3 collective-permute-start.1
  5.5 4.0 %collective-permute-start = (f32[78,4,512]{2,1,0:T(4,128)S(1)}, f32[78,4,512]{2,1,0:T(4,128)S(1)}, u32[]{:S(2)}, u32[]{:S(2)}) collective-permute-start(f32[78,4,512]{2,1,0:T(4,128)S(1)} %get-tuple-element.5), channel_id=1, source_target_pairs={{0,224},{32,0},{64,32},{96,64},{128,96},{160,128},{192,160},{224,1... | collective-permute-start | bytes 1916936 | tf_op jit(solution)/shard_map/ppermute | solution.py:238
  9.6 0.1 fusion
  9.7 14.2 %collective-permute-done.1.hxm = f32[78,4,512]{2,1,0:T(4,128)S(1)} collective-permute-done((f32[78,4,512]{2,1,0:T(4,128)S(1)}, f32[78,4,512]{2,1,0:T(4,128)S(1)}, u32[]{:S(2)}, u32[]{:S(2)}) %collective-permute-start.1) | collective-permute-done | bytes 639008 | tf_op jit(solution)/shard_map/ppermute | solution.py:239
  23.9 0.1 fusion.3
  23.9 0.0 collective-permute-done.hxp
  23.9 0.0 copy-start.1
  24.0 0.1 fusion.2
  24.0 0.1 pad_maximum_fusion
  24.1 4.2 %collective-permute-start.2 = (f32[78,24,128]{2,1,0:T(8,128)S(1)}, f32[78,24,128]{2,1,0:T(8,128)S(1)}, u32[]{:S(2)}, u32[]{:S(2)}) collective-permute-start(f32[78,24,128]{2,1,0:T(8,128)S(1)} %pad_maximum_fusion), channel_id=1, source_target_pairs={{0,31},{1,0},{2,1},{3,2},{4,3},{5,4},{6,5},{7,6},{8,7},{9,8},{10,9... | collective-permute-start | bytes 2875400 | tf_op jit(solution)/shard_map/ppermute | solution.py:245
  28.3 0.1 pad_maximum_fusion.1
  28.4 0.1 collective-permute-start.3
  28.5 11.1 %collective-permute-done.2.hyp = f32[78,24,128]{2,1,0:T(8,128)S(1)} collective-permute-done((f32[78,24,128]{2,1,0:T(8,128)S(1)}, f32[78,24,128]{2,1,0:T(8,128)S(1)}, u32[]{:S(2)}, u32[]{:S(2)}) %collective-permute-start.2) | collective-permute-done | bytes 958496 | tf_op jit(solution)/shard_map/ppermute | solution.py:245
  39.6 5.4 %collective-permute-done.3.hym = f32[78,24,128]{2,1,0:T(8,128)S(1)} collective-permute-done((f32[78,24,128]{2,1,0:T(8,128)S(1)}, f32[78,24,128]{2,1,0:T(8,128)S(1)}, u32[]{:S(2)}, u32[]{:S(2)}) %collective-permute-start.3) | collective-permute-done | bytes 958496 | tf_op jit(solution)/shard_map/ppermute | solution.py:246
  45.1 1.0 %copy-done.3 = f32[78,24,128]{2,1,0:T(8,128)} copy-done((f32[78,24,128]{2,1,0:T(8,128)}, f32[78,24,128]{2,1,0:T(8,128)S(1)}, u32[]{:S(2)}) %copy-start.3) | copy-done | bytes 958488
  46.1 12.7 %shard_map.68 = (f32[19,16,512]{2,1,0:T(8,128)}, f32[16,512]{1,0:T(8,128)}) custom-call(bf16[4,19,16,512]{3,2,1,0:T(8,128)(2,1)} %pops_ref.1, f32[19,16,512]{2,1,0:T(8,128)} %seed_ref.1, s32[16,512]{1,0:T(8,128)} %solid_ref.1, s32[16,512]{1,0:T(8,128)} %mask_ref.1, f32[16,512]{1,0:T(8,128)} %field_ref.1, f32[78,4,512]{2,1,0:T(4,128)} %copy-done.1, ...), custom_call_target="tpu_custom_call" | custom-call | tf_op jit(solution)/shard_map/pallas_call | solution.py:256
  (11 shorter events, 0.0 us)
Async XLA Ops:
  0.6 4.3 %copy-start.5 = (f32[16,512]{1,0:T(8,128)S(1)}, f32[16,512]{1,0:T(8,128)}, u32[]{:S(2)}) copy-start(f32[16,512]{1,0:T(8,128)} %field_ref.1) | copy-start | bytes 98308
  0.6 4.3 %copy-start.4 = (s32[16,512]{1,0:T(8,128)S(1)}, s32[16,512]{1,0:T(8,128)}, u32[]{:S(2)}) copy-start(s32[16,512]{1,0:T(8,128)} %mask_ref.1) | copy-start | bytes 98308
  0.7 4.3 %copy-start.6 = (s32[16,512]{1,0:T(8,128)S(1)}, s32[16,512]{1,0:T(8,128)}, u32[]{:S(2)}) copy-start(s32[16,512]{1,0:T(8,128)} %solid_ref.1) | copy-start | bytes 98308
  5.3 18.6 %collective-permute-start.1 = (f32[78,4,512]{2,1,0:T(4,128)S(1)}, f32[78,4,512]{2,1,0:T(4,128)S(1)}, u32[]{:S(2)}, u32[]{:S(2)}) collective-permute-start(f32[78,4,512]{2,1,0:T(4,128)S(1)} %get-tuple-element.4), channel_id=1, source_target_pairs={{0,32},{32,64},{64,96},{96,128},{128,160},{160,192},{192,224},{224... | collective-permute-start | bytes 1916936 | tf_op jit(solution)/shard_map/ppermute | solution.py:239
  5.5 18.4 %collective-permute-start = (f32[78,4,512]{2,1,0:T(4,128)S(1)}, f32[78,4,512]{2,1,0:T(4,128)S(1)}, u32[]{:S(2)}, u32[]{:S(2)}) collective-permute-start(f32[78,4,512]{2,1,0:T(4,128)S(1)} %get-tuple-element.5), channel_id=1, source_target_pairs={{0,224},{32,0},{64,32},{96,64},{128,96},{160,128},{192,160},{224,1... | collective-permute-start | bytes 1916936 | tf_op jit(solution)/shard_map/ppermute | solution.py:238
  23.9 4.5 %copy-start = (f32[78,4,512]{2,1,0:T(4,128)}, f32[78,4,512]{2,1,0:T(4,128)S(1)}, u32[]{:S(2)}) copy-start(f32[78,4,512]{2,1,0:T(4,128)S(1)} %collective-permute-done.1.hxm) | copy-start | bytes 1916932
  23.9 21.1 %copy-start.1 = (f32[78,4,512]{2,1,0:T(4,128)}, f32[78,4,512]{2,1,0:T(4,128)S(1)}, u32[]{:S(2)}) copy-start(f32[78,4,512]{2,1,0:T(4,128)S(1)} %collective-permute-done.hxp) | copy-start | bytes 1916932
  24.1 15.5 %collective-permute-start.2 = (f32[78,24,128]{2,1,0:T(8,128)S(1)}, f32[78,24,128]{2,1,0:T(8,128)S(1)}, u32[]{:S(2)}, u32[]{:S(2)}) collective-permute-start(f32[78,24,128]{2,1,0:T(8,128)S(1)} %pad_maximum_fusion), channel_id=1, source_target_pairs={{0,31},{1,0},{2,1},{3,2},{4,3},{5,4},{6,5},{7,6},{8,7},{9,8},{10,9... | collective-permute-start | bytes 2875400 | tf_op jit(solution)/shard_map/ppermute | solution.py:245
  28.4 16.7 %collective-permute-start.3 = (f32[78,24,128]{2,1,0:T(8,128)S(1)}, f32[78,24,128]{2,1,0:T(8,128)S(1)}, u32[]{:S(2)}, u32[]{:S(2)}) collective-permute-start(f32[78,24,128]{2,1,0:T(8,128)S(1)} %pad_maximum_fusion.1), channel_id=1, source_target_pairs={{0,1},{1,2},{2,3},{3,4},{4,5},{5,6},{6,7},{7,8},{8,9},{9,10},{10,1... | collective-permute-start | bytes 2875400 | tf_op jit(solution)/shard_map/ppermute | solution.py:246
  39.6 5.4 %copy-start.2 = (f32[78,24,128]{2,1,0:T(8,128)}, f32[78,24,128]{2,1,0:T(8,128)S(1)}, u32[]{:S(2)}) copy-start(f32[78,24,128]{2,1,0:T(8,128)S(1)} %collective-permute-done.2.hyp) | copy-start | bytes 2875396
  45.1 1.0 %copy-start.3 = (f32[78,24,128]{2,1,0:T(8,128)}, f32[78,24,128]{2,1,0:T(8,128)S(1)}, u32[]{:S(2)}) copy-start(f32[78,24,128]{2,1,0:T(8,128)S(1)} %collective-permute-done.3.hym) | copy-start | bytes 2875396
where the time goes:
time: 60 us; the launch traced here: 58.8 us
  waiting for transfers between devices  30.7 us (51%)
  Pallas kernels  12.7 us (21%)
  starting transfers between devices  8.54 us (14%)
  other arithmetic  3.3 us (6%)
  local copies, waits for them, and re-layouts  2.68 us (4%)
  between operations  0.8 us (1%)
    ppermute x1, waiting for transfers between devices, body(): hxm = lax.ppermute(fields[:, rows - DEPTH:rows, :], 'gx', _shift(nx, 1))  14.2 us
    pallas_call x1, Pallas kernels, body(): pl.pallas_call(_fused_kernel, grid=(1,), in_specs=[full(a.shape) for a in...  12.7 us
    ppermute x1, waiting for transfers between devices, body(): hyp = lax.ppermute(col_lo, 'gy', _shift(ny, -1))  11.1 us
    ppermute x1, waiting for transfers between devices, body(): hym = lax.ppermute(col_hi, 'gy', _shift(ny, 1))  5.42 us
    ppermute x1, starting transfers between devices, body(): hyp = lax.ppermute(col_lo, 'gy', _shift(ny, -1))  4.17 us
    ppermute x1, starting transfers between devices, body(): hxp = lax.ppermute(fields[:, 0:DEPTH, :], 'gx', _shift(nx, -1))  4.03 us
    unnamed x4, other arithmetic  3.1 us
    unnamed x15, local copies, waits for them, and re-layouts  2.15 us
  transfers between devices with their start and end apart: 4, of which 3 were waited for; matrix products, arithmetic and copies ran while one was open for 0% of the time, Pallas kernels for 0%

commit v1 on v0

--- a/solution.py
+++ b/solution.py
@@ -139,15 +139,18 @@
         p_ref[i] = v
 
 
-def _fill_ext(dst, own, hxp, hxm, hyp, hym, rows, flat):
+def _fill_ext(dst, own, hxp, hxm, hyp, hym, cp, cm, rows, flat):
+    yw = DEPTH * NZ
     dst[0:rows, 0:flat] = own
     dst[rows : rows + DEPTH, 0:flat] = hxp
     dst[rows + DEPTH : rows + 2 * DEPTH, 0:flat] = hxm
-    dst[:, flat : flat + DEPTH * NZ] = hyp
-    dst[:, flat + DEPTH * NZ : flat + 2 * DEPTH * NZ] = hym
-
-
-def _fused_kernel(pops_ref, seed_ref, solid_ref, mask_ref, field_ref, hxp, hxm, hyp, hym,
+    dst[0:rows, flat : flat + yw] = hyp
+    dst[rows : rows + 2 * DEPTH, flat : flat + yw] = cp
+    dst[0:rows, flat + yw : flat + 2 * yw] = hym
+    dst[rows : rows + 2 * DEPTH, flat + yw : flat + 2 * yw] = cm
+
+
+def _fused_kernel(pops_ref, seed_ref, solid_ref, mask_ref, field_ref, hxp, hxm, hyp, hym, cp, cm,
                   adj_out, sens_out, a_ref, p_ref, f_ref, rate_ref, solid_ext):
     steps = pops_ref.shape[0]
     _, rows, flat = seed_ref.shape
@@ -155,12 +158,13 @@
     nfield = hxp.shape[0]
     mask_all = mask_ref[...].astype(jnp.float32)
     rate_own = OMEGA_BASE + OMEGA_SPAN * field_ref[...] * mask_all
-    _fill_ext(rate_ref, rate_own, hxp[nfield - 2], hxm[nfield - 2], hyp[nfield - 2],
-              hym[nfield - 2], rows, flat)
-    _fill_ext(solid_ext, solid_ref[...].astype(jnp.float32), hxp[nfield - 1], hxm[nfield - 1],
-              hyp[nfield - 1], hym[nfield - 1], rows, flat)
-    for i in range(19):
-        _fill_ext(a_ref.at[i], seed_ref[i], hxp[i], hxm[i], hyp[i], hym[i], rows, flat)
+    halo = lambda k, scale=None: [
+        h[k] if scale is None else h[k] * scale for h in (hxp, hxm, hyp, hym, cp, cm)
+    ]
+    _fill_ext(rate_ref, rate_own, *halo(nfield - 2), rows, flat)
+    _fill_ext(solid_ext, solid_ref[...].astype(jnp.float32), *halo(nfield - 1), rows, flat)
+    for i in range(19):
+        _fill_ext(a_ref.at[i], seed_ref[i], *halo(i), rows, flat)
     sens_out[...] = jnp.zeros(sens_out.shape, jnp.float32)
     row_tiles = rows // 8
     lane_tiles = flat // LANES
@@ -192,8 +196,7 @@
                 f_ref[i, 0:rows, 0:flat] = own
             else:
                 k = 19 + 19 * (steps - 1 - step) + i
-                _fill_ext(f_ref.at[i], own, hxp[k] * W32[i], hxm[k] * W32[i], hyp[k] * W32[i],
-                          hym[k] * W32[i], rows, flat)
+                _fill_ext(f_ref.at[i], own, *halo(k, W32[i]), rows, flat)
         _pull_all(a_ref, p_ref)
         write_ref = adj_out if last else a_ref
 
@@ -217,11 +220,12 @@
             lax.fori_loop(0, n_halo, halo_body, 0)
 
 
-def _messages(saved_pops, seed, solid, mask, field):
+def _message(saved_pops, seed, solid, mask, field, rs, ls):
     steps = saved_pops.shape[0]
-    rate = OMEGA_BASE + OMEGA_SPAN * field * mask.astype(jnp.float32)
-    parts = [seed] + [saved_pops[s].astype(jnp.float32) for s in reversed(range(1, steps))]
-    parts += [rate[None], solid.astype(jnp.float32)[None]]
+    rate = OMEGA_BASE + OMEGA_SPAN * field[rs, ls] * mask[rs, ls].astype(jnp.float32)
+    parts = [seed[:, rs, ls]]
+    parts += [saved_pops[s][:, rs, ls].astype(jnp.float32) for s in reversed(range(1, steps))]
+    parts += [rate[None], solid[rs, ls].astype(jnp.float32)[None]]
     return jnp.concatenate(parts, axis=0)
 
 
@@ -234,20 +238,21 @@
     ny = lax.axis_size("gy")
     _, rows, flat = seed_adjoint.shape
     yw = DEPTH * NZ
-    fields = _messages(saved_pops, seed_adjoint, solid_label, design_mask, design_field)
-    hxp = lax.ppermute(fields[:, 0:DEPTH, :], "gx", _shift(nx, -1))
-    hxm = lax.ppermute(fields[:, rows - DEPTH : rows, :], "gx", _shift(nx, 1))
-    col_lo = jnp.concatenate([fields[:, :, 0:yw], hxp[:, :, 0:yw], hxm[:, :, 0:yw]], axis=1)
-    col_hi = jnp.concatenate(
-        [fields[:, :, flat - yw : flat], hxp[:, :, flat - yw : flat], hxm[:, :, flat - yw : flat]],
-        axis=1,
-    )
-    hyp = lax.ppermute(col_lo, "gy", _shift(ny, -1))
-    hym = lax.ppermute(col_hi, "gy", _shift(ny, 1))
+    ins = (saved_pops, seed_adjoint, solid_label, design_mask, design_field)
+    full_r, full_l = slice(0, rows), slice(0, flat)
+    lo_l, hi_l = slice(0, yw), slice(flat - yw, flat)
+    hxp = lax.ppermute(_message(*ins, slice(0, DEPTH), full_l), "gx", _shift(nx, -1))
+    hxm = lax.ppermute(_message(*ins, slice(rows - DEPTH, rows), full_l), "gx", _shift(nx, 1))
+    hyp = lax.ppermute(_message(*ins, full_r, lo_l), "gy", _shift(ny, -1))
+    hym = lax.ppermute(_message(*ins, full_r, hi_l), "gy", _shift(ny, 1))
+    c_lo = jnp.concatenate([hxp[:, :, lo_l], hxm[:, :, lo_l]], axis=1)
+    c_hi = jnp.concatenate([hxp[:, :, hi_l], hxm[:, :, hi_l]], axis=1)
+    cp = lax.ppermute(c_lo, "gy", _shift(ny, -1))
+    cm = lax.ppermute(c_hi, "gy", _shift(ny, 1))
     erows = rows + 2 * DEPTH
     eflat = flat + 2 * yw
     ext = (19, erows, eflat)
-    args = [saved_pops, seed_adjoint, solid_label, design_mask, design_field, hxp, hxm, hyp, hym]
+    args = [saved_pops, seed_adjoint, solid_label, design_mask, design_field, hxp, hxm, hyp, hym, cp, cm]
 
     def full(shape):
         nd = len(shape)

time: 60 us -> 51.9 us (0.86); the launches traced: 58.8 us -> 51.8 us
  waiting for transfers between devices: 30.7 us -> 22.1 us
  starting transfers between devices: 8.54 us -> 12.3 us
  other arithmetic: 3.3 us -> 0.48 us
  local copies, waits for them, and re-layouts: 2.68 us -> 3.32 us
    ppermute x4 -> x6, waiting for transfers between devices: 30.7 us -> 22.1 us  [the longest x1 12.4 us: body(): lax.ppermute(_message(*ins, slice(rows - DEPTH, rows), full_l), 'gx', _sh...]
    ppermute x4 -> x6, starting transfers between devices: 8.54 us -> 12.3 us  [the longest x1 4.45 us: body(): hyp = lax.ppermute(_message(*ins, full_r, lo_l), 'gy', _shift(ny, -1))]
    unnamed x4 -> x8, other arithmetic: 3.1 us -> 0.33 us
    squeeze x0 -> x1, local copies, waits for them, and re-layouts: none -> 1.28 us  [_message(): saved_pops[s][:, rs, ls].astype(jnp.float32)]
    unnamed x15 -> x22, local copies, waits for them, and re-layouts: 2.15 us -> 1.92 us
  transfers between devices with their start and end apart: 4 -> 6, of which waited for: 3 -> 3; matrix products, arithmetic and copies ran while one was open for 0% -> 1% of each run, Pallas kernels for 0% -> 0%
where the time goes in v1:
time: 51.9 us; the launch traced here: 51.8 us
  waiting for transfers between devices  22.1 us (43%)
  Pallas kernels  12.7 us (24%)
  starting transfers between devices  12.3 us (24%)
  local copies, waits for them, and re-layouts  3.32 us (6%)
  between operations  0.86 us (2%)
    pallas_call x1, Pallas kernels, body(): pl.pallas_call(_fused_kernel, grid=(1,), in_specs=[full(a.shape) for a in...  12.7 us
    ppermute x1, waiting for transfers between devices, body(): lax.ppermute(_message(*ins, slice(rows - DEPTH, rows), full_l), 'gx', _sh...  12.4 us
    ppermute x1, waiting for transfers between devices, body(): cm = lax.ppermute(c_hi, 'gy', _shift(ny, 1))  5.38 us
    ppermute x1, starting transfers between devices, body(): hyp = lax.ppermute(_message(*ins, full_r, lo_l), 'gy', _shift(ny, -1))  4.45 us
    ppermute x1, waiting for transfers between devices, body(): cp = lax.ppermute(c_lo, 'gy', _shift(ny, -1))  4.29 us
    ppermute x1, starting transfers between devices, body(): lax.ppermute(_message(*ins, slice(0, DEPTH), full_l), 'gx', _shift(nx, -1))  4.2 us
    ppermute x1, starting transfers between devices, body(): cp = lax.ppermute(c_lo, 'gy', _shift(ny, -1))  3.54 us
    unnamed x22, local copies, waits for them, and re-layouts  1.92 us
  transfers between devices with their start and end apart: 6, of which 3 were waited for; matrix products, arithmetic and copies ran while one was open for 1% of the time, Pallas kernels for 0%

profile of v1, /device:TPU:0, one launch (start us, length us, event | category | flops | bytes accessed | tf_op | source)
XLA Modules:
  0.0 51.8 jit_solution(7662827103014188730)
XLA Ops:
  0.6 1.1 %slice_dynamic-update-slice_fusion.2 = (f32[78,4,512]{2,1,0:T(4,128)S(1)}, f32[78,4,512]{2,1,0:T(4,128)S(1)}) fusion(f32[19,16,512]{2,1,0:T(8,128)} %seed_ref.1), kind=kLoop, calls=%fused_computation.16 | loop fusion | bytes 622592
  1.8 0.0 copy-start.7
  1.8 0.0 copy-start.8
  1.8 0.0 copy-start.9
  1.8 0.0 copy-start
  1.8 1.3 %slice_bitcast_fusion = (bf16[19,16,512]{2,1,0:T(8,128)(2,1)S(1)}, bf16[19,16,512]{2,1,0:T(8,128)(2,1)S(1)}, bf16[19,16,512]{2,1,0:T(8,128)(2,1)S(1)}) fusion(bf16[4,19,16,512]{3,2,1,0:T(8,128)(2,1)} %pops_ref.1), kind=kLoop, calls=%fused_computation.2 | loop fusion | bytes 1867776 | tf_op jit(solution)/shard_map/squeeze | solution.py:227
  3.1 0.1 convert_dynamic-update-slice_fusion.8
  3.2 0.1 convert_dynamic-update-slice_fusion.7
  3.3 0.1 convert_dynamic-update-slice_fusion.6
  3.4 4.2 %collective-permute-start = (f32[78,4,512]{2,1,0:T(4,128)S(1)}, f32[78,4,512]{2,1,0:T(4,128)S(1)}, u32[]{:S(2)}, u32[]{:S(2)}) collective-permute-start(f32[78,4,512]{2,1,0:T(4,128)S(1)} %get-tuple-element.32), channel_id=1, source_target_pairs={{0,224},{32,0},{64,32},{96,64},{128,96},{160,128},{192,160},{224,1... | collective-permute-start | bytes 1916936 | tf_op jit(solution)/shard_map/ppermute | solution.py:244
  7.6 0.0 collective-permute-start.1
  7.8 4.4 %collective-permute-start.2 = (f32[78,16,128]{2,1,0:T(8,128)S(1)}, f32[78,16,128]{2,1,0:T(8,128)S(1)}, u32[]{:S(2)}, u32[]{:S(2)}) collective-permute-start(f32[78,16,128]{2,1,0:T(8,128)S(1)} %get-tuple-element.30), channel_id=1, source_target_pairs={{0,31},{1,0},{2,1},{3,2},{4,3},{5,4},{6,5},{7,6},{8,7},{9,8},{10,9... | collective-permute-start | bytes 1916936 | tf_op jit(solution)/shard_map/ppermute | solution.py:246
  12.2 12.4 %collective-permute-done.1.hxm = f32[78,4,512]{2,1,0:T(4,128)S(1)} collective-permute-done((f32[78,4,512]{2,1,0:T(4,128)S(1)}, f32[78,4,512]{2,1,0:T(4,128)S(1)}, u32[]{:S(2)}, u32[]{:S(2)}) %collective-permute-start.1) | collective-permute-done | bytes 639008 | tf_op jit(solution)/shard_map/ppermute | solution.py:245
  24.7 0.1 fusion.1
  24.7 0.1 fusion
  24.8 0.1 pad_maximum_fusion
  24.9 3.5 %collective-permute-start.4 = (f32[78,8,128]{2,1,0:T(8,128)S(1)}, f32[78,8,128]{2,1,0:T(8,128)S(1)}, u32[]{:S(2)}, u32[]{:S(2)}) collective-permute-start(f32[78,8,128]{2,1,0:T(8,128)S(1)} %pad_maximum_fusion), channel_id=1, source_target_pairs={{0,31},{1,0},{2,1},{3,2},{4,3},{5,4},{6,5},{7,6},{8,7},{9,8},{10,9... | collective-permute-start | bytes 958472 | tf_op jit(solution)/shard_map/ppermute | solution.py:250
  28.4 0.1 pad_maximum_fusion.1
  28.5 0.1 collective-permute-start.5
  28.6 0.0 collective-permute-done.2.hyp
  28.6 4.3 %collective-permute-done.4.cp = f32[78,8,128]{2,1,0:T(8,128)S(1)} collective-permute-done((f32[78,8,128]{2,1,0:T(8,128)S(1)}, f32[78,8,128]{2,1,0:T(8,128)S(1)}, u32[]{:S(2)}, u32[]{:S(2)}) %collective-permute-start.4) | collective-permute-done | bytes 319520 | tf_op jit(solution)/shard_map/ppermute | solution.py:250
  32.9 5.4 %collective-permute-done.5.cm = f32[78,8,128]{2,1,0:T(8,128)S(1)} collective-permute-done((f32[78,8,128]{2,1,0:T(8,128)S(1)}, f32[78,8,128]{2,1,0:T(8,128)S(1)}, u32[]{:S(2)}, u32[]{:S(2)}) %collective-permute-start.5) | collective-permute-done | bytes 319520 | tf_op jit(solution)/shard_map/ppermute | solution.py:251
  38.3 0.7 %copy-done.6 = f32[78,8,128]{2,1,0:T(8,128)} copy-done((f32[78,8,128]{2,1,0:T(8,128)}, f32[78,8,128]{2,1,0:T(8,128)S(1)}, u32[]{:S(2)}) %copy-start.6) | copy-done | bytes 319512
  39.1 12.7 %shard_map.68 = (f32[19,16,512]{2,1,0:T(8,128)}, f32[16,512]{1,0:T(8,128)}) custom-call(bf16[4,19,16,512]{3,2,1,0:T(8,128)(2,1)} %pops_ref.1, f32[19,16,512]{2,1,0:T(8,128)} %seed_ref.1, s32[16,512]{1,0:T(8,128)} %solid_ref.1, s32[16,512]{1,0:T(8,128)} %mask_ref.1, f32[16,512]{1,0:T(8,128)} %field_ref.1, f32[78,4,512]{2,1,0:T(4,128)} %copy-done.1, ...), custom_call_target="tpu_custom_call" | custom-call | tf_op jit(solution)/shard_map/pallas_call | solution.py:261
  (26 shorter events, 0.2 us)
Async XLA Ops:
  1.8 1.6 %copy-start.7 = (s32[16,512]{1,0:T(8,128)S(1)}, s32[16,512]{1,0:T(8,128)}, u32[]{:S(2)}) copy-start(s32[16,512]{1,0:T(8,128)} %mask_ref.1) | copy-start | bytes 98308
  1.8 1.6 %copy-start.8 = (f32[16,512]{1,0:T(8,128)S(1)}, f32[16,512]{1,0:T(8,128)}, u32[]{:S(2)}) copy-start(f32[16,512]{1,0:T(8,128)} %field_ref.1) | copy-start | bytes 98308
  1.8 1.6 %copy-start.9 = (s32[16,512]{1,0:T(8,128)S(1)}, s32[16,512]{1,0:T(8,128)}, u32[]{:S(2)}) copy-start(s32[16,512]{1,0:T(8,128)} %solid_ref.1) | copy-start | bytes 98308
  1.8 5.8 %copy-start = (f32[19,16,512]{2,1,0:T(8,128)S(1)}, f32[19,16,512]{2,1,0:T(8,128)}, u32[]{:S(2)}) copy-start(f32[19,16,512]{2,1,0:T(8,128)} %seed_ref.1) | copy-start | bytes 1867780
  3.4 21.3 %collective-permute-start = (f32[78,4,512]{2,1,0:T(4,128)S(1)}, f32[78,4,512]{2,1,0:T(4,128)S(1)}, u32[]{:S(2)}, u32[]{:S(2)}) collective-permute-start(f32[78,4,512]{2,1,0:T(4,128)S(1)} %get-tuple-element.32), channel_id=1, source_target_pairs={{0,224},{32,0},{64,32},{96,64},{128,96},{160,128},{192,160},{224,1... | collective-permute-start | bytes 1916936 | tf_op jit(solution)/shard_map/ppermute | solution.py:244
  7.6 17.1 %collective-permute-start.1 = (f32[78,4,512]{2,1,0:T(4,128)S(1)}, f32[78,4,512]{2,1,0:T(4,128)S(1)}, u32[]{:S(2)}, u32[]{:S(2)}) collective-permute-start(f32[78,4,512]{2,1,0:T(4,128)S(1)} %get-tuple-element.31), channel_id=1, source_target_pairs={{0,32},{32,64},{64,96},{96,128},{128,160},{160,192},{192,224},{224... | collective-permute-start | bytes 1916936 | tf_op jit(solution)/shard_map/ppermute | solution.py:245
  7.8 20.8 %collective-permute-start.2 = (f32[78,16,128]{2,1,0:T(8,128)S(1)}, f32[78,16,128]{2,1,0:T(8,128)S(1)}, u32[]{:S(2)}, u32[]{:S(2)}) collective-permute-start(f32[78,16,128]{2,1,0:T(8,128)S(1)} %get-tuple-element.30), channel_id=1, source_target_pairs={{0,31},{1,0},{2,1},{3,2},{4,3},{5,4},{6,5},{7,6},{8,7},{9,8},{10,9... | collective-permute-start | bytes 1916936 | tf_op jit(solution)/shard_map/ppermute | solution.py:246
  12.2 16.4 %collective-permute-start.3 = (f32[78,16,128]{2,1,0:T(8,128)S(1)}, f32[78,16,128]{2,1,0:T(8,128)S(1)}, u32[]{:S(2)}, u32[]{:S(2)}) collective-permute-start(f32[78,16,128]{2,1,0:T(8,128)S(1)} %get-tuple-element.29), channel_id=1, source_target_pairs={{0,1},{1,2},{2,3},{3,4},{4,5},{5,6},{6,7},{7,8},{8,9},{9,10},{10,1... | collective-permute-start | bytes 1916936 | tf_op jit(solution)/shard_map/ppermute | solution.py:247
  24.7 3.8 %copy-start.2 = (f32[78,4,512]{2,1,0:T(4,128)}, f32[78,4,512]{2,1,0:T(4,128)S(1)}, u32[]{:S(2)}) copy-start(f32[78,4,512]{2,1,0:T(4,128)S(1)} %collective-permute-done.1.hxm) | copy-start | bytes 1916932
  24.7 13.6 %copy-start.1 = (f32[78,4,512]{2,1,0:T(4,128)}, f32[78,4,512]{2,1,0:T(4,128)S(1)}, u32[]{:S(2)}) copy-start(f32[78,4,512]{2,1,0:T(4,128)S(1)} %collective-permute-done.hxp) | copy-start | bytes 1916932
  24.9 8.0 %collective-permute-start.4 = (f32[78,8,128]{2,1,0:T(8,128)S(1)}, f32[78,8,128]{2,1,0:T(8,128)S(1)}, u32[]{:S(2)}, u32[]{:S(2)}) collective-permute-start(f32[78,8,128]{2,1,0:T(8,128)S(1)} %pad_maximum_fusion), channel_id=1, source_target_pairs={{0,31},{1,0},{2,1},{3,2},{4,3},{5,4},{6,5},{7,6},{8,7},{9,8},{10,9... | collective-permute-start | bytes 958472 | tf_op jit(solution)/shard_map/ppermute | solution.py:250
  28.5 9.8 %collective-permute-start.5 = (f32[78,8,128]{2,1,0:T(8,128)S(1)}, f32[78,8,128]{2,1,0:T(8,128)S(1)}, u32[]{:S(2)}, u32[]{:S(2)}) collective-permute-start(f32[78,8,128]{2,1,0:T(8,128)S(1)} %pad_maximum_fusion.1), channel_id=1, source_target_pairs={{0,1},{1,2},{2,3},{3,4},{4,5},{5,6},{6,7},{7,8},{8,9},{9,10},{10,1... | collective-permute-start | bytes 958472 | tf_op jit(solution)/shard_map/ppermute | solution.py:251
  28.6 9.7 %copy-start.3 = (f32[78,16,128]{2,1,0:T(8,128)}, f32[78,16,128]{2,1,0:T(8,128)S(1)}, u32[]{:S(2)}) copy-start(f32[78,16,128]{2,1,0:T(8,128)S(1)} %collective-permute-done.2.hyp) | copy-start | bytes 1916932
  28.6 9.7 %copy-start.4 = (f32[78,16,128]{2,1,0:T(8,128)}, f32[78,16,128]{2,1,0:T(8,128)S(1)}, u32[]{:S(2)}) copy-start(f32[78,16,128]{2,1,0:T(8,128)S(1)} %collective-permute-done.3.hym) | copy-start | bytes 1916932
  32.9 5.4 %copy-start.5 = (f32[78,8,128]{2,1,0:T(8,128)}, f32[78,8,128]{2,1,0:T(8,128)S(1)}, u32[]{:S(2)}) copy-start(f32[78,8,128]{2,1,0:T(8,128)S(1)} %collective-permute-done.4.cp) | copy-start | bytes 958468
  38.3 0.7 %copy-start.6 = (f32[78,8,128]{2,1,0:T(8,128)}, f32[78,8,128]{2,1,0:T(8,128)S(1)}, u32[]{:S(2)}) copy-start(f32[78,8,128]{2,1,0:T(8,128)S(1)} %collective-permute-done.5.cm) | copy-start | bytes 958468

commit v2 on v1

--- a/solution.py
+++ b/solution.py
@@ -46,7 +46,7 @@
 LANES = 128
 
 
-def _collide_vjp(f, g, rate, solid):
+def _velocity(f):
     rho = f[0]
     for i in range(1, 19):
         rho = rho + f[i]
@@ -60,16 +60,17 @@
         for x in neg:
             acc = acc - x
         mom.append(acc)
-    u = [m / rho for m in mom]
+    return rho, [m / rho for m in mom]
+
+
+def _vjp_core(u, g, rate, solid):
     usq = u[0] * u[0] + u[1] * u[1] + u[2] * u[2]
     base = 1.0 - 1.5 * usq
     fluid = solid == 0
     one_minus = 1.0 - rate
-    rbar = None
     esum = None
     easum = None
     mb = [None, None, None]
-    proj = []
     amp = []
     gf = []
     for i in range(19):
@@ -84,13 +85,9 @@
             amp_i = base
         else:
             amp_i = base + (3.0 + 4.5 * p) * p
-        proj.append(p)
         amp.append(amp_i)
         gi = jnp.where(fluid, g[i], 0.0)
         gf.append(gi)
-        feq = W32[i] * rho * amp_i
-        t = gi * (feq - f[i])
-        rbar = t if rbar is None else rbar + t
         e = (rate * W32[i]) * gi
         esum = e if esum is None else esum + e
         ea = e * amp_i
@@ -116,6 +113,17 @@
             elif cvec[a] < 0:
                 val = val - mb[a]
         out.append(jnp.where(fluid, val, g[int(OPPOSITE[i])]))
+    return out, amp, gf
+
+
+def _collide_vjp(f, g, rate, solid):
+    rho, u = _velocity(f)
+    out, amp, gf = _vjp_core(u, g, rate, solid)
+    rbar = None
+    for i in range(19):
+        feq = W32[i] * rho * amp[i]
+        t = gf[i] * (feq - f[i])
+        rbar = t if rbar is None else rbar + t
     return out, rbar
 
 
@@ -141,7 +149,8 @@
 
 def _fill_ext(dst, own, hxp, hxm, hyp, hym, cp, cm, rows, flat):
     yw = DEPTH * NZ
-    dst[0:rows, 0:flat] = own
+    if own is not None:
+        dst[0:rows, 0:flat] = own
     dst[rows : rows + DEPTH, 0:flat] = hxp
     dst[rows + DEPTH : rows + 2 * DEPTH, 0:flat] = hxm
     dst[0:rows, flat : flat + yw] = hyp
@@ -151,7 +160,7 @@
 
 
 def _fused_kernel(pops_ref, seed_ref, solid_ref, mask_ref, field_ref, hxp, hxm, hyp, hym, cp, cm,
-                  adj_out, sens_out, a_ref, p_ref, f_ref, rate_ref, solid_ext):
+                  adj_out, sens_out, a_ref, p_ref, u_ref, rate_ref, solid_ext):
     steps = pops_ref.shape[0]
     _, rows, flat = seed_ref.shape
     erows, eflat = a_ref.shape[1], a_ref.shape[2]
@@ -173,37 +182,37 @@
     n_halo_rows = (erows - rows) // 8 * lane_tiles
     n_halo = n_halo_rows + (erows // 8) * (ext_lane_tiles - lane_tiles)
 
-    def chunk(r0, l0, write_ref, own):
+    def chunk(step, r0, l0, write_ref, own):
         rs = pl.ds(r0, 8)
         ls = pl.ds(l0, LANES)
-        f = [f_ref[i, rs, ls] for i in range(19)]
         g = [p_ref[i, rs, ls] for i in range(19)]
         solid = solid_ext[rs, ls]
         solid_i = jnp.where(solid > 0.5, 1, 0)
-        new, rbar = _collide_vjp(f, g, rate_ref[rs, ls], solid_i)
-        for i in range(19):
-            write_ref[i, rs, ls] = new[i]
+        rate = rate_ref[rs, ls]
         if own:
+            f = [pops_ref[step, i, rs, ls].astype(jnp.float32) * W32[i] for i in range(19)]
+            new, rbar = _collide_vjp(f, g, rate, solid_i)
             mask = mask_ref[rs, ls].astype(jnp.float32)
             contrib = SENS_SCALE * OMEGA_SPAN * mask * jnp.where(solid_i == 0, rbar, 0.0)
             sens_out[rs, ls] = sens_out[rs, ls] + contrib
+        else:
+            u = [u_ref[a, rs, ls] for a in range(3)]
+            new, _, _ = _vjp_core(u, g, rate, solid_i)
+        for i in range(19):
+            write_ref[i, rs, ls] = new[i]
 
     for n, step in enumerate(reversed(range(steps))):
         last = step == 0
-        for i in range(19):
-            own = pops_ref[step, i].astype(jnp.float32) * W32[i]
-            if last:
-                f_ref[i, 0:rows, 0:flat] = own
-            else:
-                k = 19 + 19 * (steps - 1 - step) + i
-                _fill_ext(f_ref.at[i], own, *halo(k, W32[i]), rows, flat)
+        if not last:
+            for a in range(3):
+                _fill_ext(u_ref.at[a], None, *halo(19 + 3 * n + a), rows, flat)
         _pull_all(a_ref, p_ref)
         write_ref = adj_out if last else a_ref
 
         def own_body(c, carry, write_ref=write_ref):
             r0 = pl.multiple_of((c // lane_tiles) * 8, 8)
             l0 = pl.multiple_of((c % lane_tiles) * LANES, LANES)
-            chunk(r0, l0, write_ref, True)
+            chunk(step, r0, l0, write_ref, True)
             return carry
 
         lax.fori_loop(0, n_own, own_body, 0)
@@ -214,7 +223,7 @@
                 ext_w = ext_lane_tiles - lane_tiles
                 r = jnp.where(c < n_halo_rows, rows // 8 + c // lane_tiles, c2 // ext_w)
                 t = jnp.where(c < n_halo_rows, c % lane_tiles, lane_tiles + c2 % ext_w)
-                chunk(pl.multiple_of(r * 8, 8), pl.multiple_of(t * LANES, LANES), a_ref, False)
+                chunk(step, pl.multiple_of(r * 8, 8), pl.multiple_of(t * LANES, LANES), a_ref, False)
                 return carry
 
             lax.fori_loop(0, n_halo, halo_body, 0)
@@ -224,7 +233,9 @@
     steps = saved_pops.shape[0]
     rate = OMEGA_BASE + OMEGA_SPAN * field[rs, ls] * mask[rs, ls].astype(jnp.float32)
     parts = [seed[:, rs, ls]]
-    parts += [saved_pops[s][:, rs, ls].astype(jnp.float32) for s in reversed(range(1, steps))]
+    for s in reversed(range(1, steps)):
+        f = [saved_pops[s, i][rs, ls].astype(jnp.float32) * W32[i] for i in range(19)]
+        parts += [u[None] for u in _velocity(f)[1]]
     parts += [rate[None], solid[rs, ls].astype(jnp.float32)[None]]
     return jnp.concatenate(parts, axis=0)
 
@@ -270,7 +281,7 @@
         scratch_shapes=[
             pltpu.VMEM(ext, jnp.float32),
             pltpu.VMEM(ext, jnp.float32),
-            pltpu.VMEM(ext, jnp.float32),
+            pltpu.VMEM((3, erows, eflat), jnp.float32),
             pltpu.VMEM((erows, eflat), jnp.float32),
             pltpu.VMEM((erows, eflat), jnp.float32),
         ],

time: 51.9 us -> 47.4 us (0.913); the launches traced: 51.8 us -> 46.6 us
  waiting for transfers between devices: 22.1 us -> 11 us
  other arithmetic: 0.48 us -> 9.05 us
  Pallas kernels: 12.7 us -> 11.3 us
  local copies, waits for them, and re-layouts: 3.32 us -> 2.05 us
    ppermute x1, waiting for transfers between devices: 12.4 us -> 3.38 us  [body(): lax.ppermute(_message(*ins, slice(rows - DEPTH, rows), full_l), 'gx', _sh...]
    unnamed x8 -> x38, other arithmetic: 0.33 us -> 8.98 us
    ppermute x1, waiting for transfers between devices: 4.29 us -> 0.54 us  [body(): cp = lax.ppermute(c_lo, 'gy', _shift(ny, -1))]
    ppermute x1, waiting for transfers between devices: 0.01 us -> 1.76 us  [body(): hym = lax.ppermute(_message(*ins, full_r, hi_l), 'gy', _shift(ny, 1))]
    pallas_call x1, Pallas kernels: 12.7 us -> 11.3 us  [body(): pl.pallas_call(_fused_kernel, grid=(1,), in_specs=[full(a.shape) for a in...]
    squeeze x1 -> x3, local copies, waits for them, and re-layouts: 1.28 us -> 0.07 us  [_message(): saved_pops[s, i][rs, ls].astype(jnp.float32) * W32[i]]
    unnamed x22 -> x24, local copies, waits for them, and re-layouts: 1.92 us -> 1.93 us
  transfers between devices with their start and end apart: 6 -> 6, of which waited for: 3 -> 4; matrix products, arithmetic and copies ran while one was open for 1% -> 1% of each run, Pallas kernels for 0% -> 0%
where the time goes in v2:
time: 47.4 us; the launch traced here: 46.6 us
  starting transfers between devices  12.3 us (26%)
  Pallas kernels  11.3 us (24%)
  waiting for transfers between devices  11 us (23%)
  other arithmetic  9.05 us (19%)
  local copies, waits for them, and re-layouts  2.05 us (4%)
  between operations  0.97 us (2%)
    pallas_call x1, Pallas kernels, body(): pl.pallas_call(_fused_kernel, grid=(1,), in_specs=[full(a.shape) for a in...  11.3 us
    unnamed x38, other arithmetic  8.98 us
    ppermute x1, waiting for transfers between devices, body(): cm = lax.ppermute(c_hi, 'gy', _shift(ny, 1))  5.29 us
    ppermute x1, starting transfers between devices, body(): hyp = lax.ppermute(_message(*ins, full_r, lo_l), 'gy', _shift(ny, -1))  4.45 us
    ppermute x1, starting transfers between devices, body(): lax.ppermute(_message(*ins, slice(0, DEPTH), full_l), 'gx', _shift(nx, -1))  4.2 us
    ppermute x1, starting transfers between devices, body(): cp = lax.ppermute(c_lo, 'gy', _shift(ny, -1))  3.54 us
    ppermute x1, waiting for transfers between devices, body(): lax.ppermute(_message(*ins, slice(rows - DEPTH, rows), full_l), 'gx', _sh...  3.38 us
    unnamed x24, local copies, waits for them, and re-layouts  1.93 us
  transfers between devices with their start and end apart: 6, of which 4 were waited for; matrix products, arithmetic and copies ran while one was open for 1% of the time, Pallas kernels for 0%

profile of v2, /device:TPU:0, one launch (start us, length us, event | category | flops | bytes accessed | tf_op | source)
XLA Modules:
  0.0 46.6 jit_solution(3018694122353092033)
XLA Ops:
  0.7 1.2 %slice_dynamic-update-slice_fusion.2 = (f32[30,4,512]{2,1,0:T(4,128)S(1)}, f32[30,4,512]{2,1,0:T(4,128)S(1)}) fusion(f32[19,16,512]{2,1,0:T(8,128)} %seed_ref.1), kind=kLoop, calls=%fused_computation.2 | loop fusion | bytes 622592
  1.9 0.9 %constant_dynamic-update-slice_fusion.10 = (f32[30,4,512]{2,1,0:T(4,128)S(1)}, f32[1,4,512]{2,1,0:T(4,128)S(1)}) fusion(f32[30,4,512]{2,1,0:T(4,128)S(1)} %get-tuple-element.86, bf16[4,19,16,512]{3,2,1,0:T(8,128)(2,1)} %pops_ref.1), kind=kLoop, calls=%fused_computation.16 | loop fusion | flops 135168 | bytes 94208
  2.8 0.9 %constant_dynamic-update-slice_fusion.9 = f32[30,4,512]{2,1,0:T(4,128)S(1)} fusion(f32[30,4,512]{2,1,0:T(4,128)S(1)} %get-tuple-element.24, f32[1,4,512]{2,1,0:T(4,128)S(1)} %get-tuple-element.25, bf16[4,19,16,512]{3,2,1,0:T(8,128)(2,1)} %pops_ref.1), kind=kLoop, calls=%fused_computation.15 | loop fusion | flops 61440 | bytes 57344
  3.7 0.9 %constant_dynamic-update-slice_fusion.8 = f32[30,4,512]{2,1,0:T(4,128)S(1)} fusion(f32[30,4,512]{2,1,0:T(4,128)S(1)} %constant_dynamic-update-slice_fusion.9, f32[1,4,512]{2,1,0:T(4,128)S(1)} %get-tuple-element.25, bf16[4,19,16,512]{3,2,1,0:T(8,128)(2,1)} %pops_ref.1), kind=kLoop, calls=%fused_computation.14 | loop fusion | flops 61440 | bytes 57344
  4.6 0.9 %constant_dynamic-update-slice_fusion.7 = (f32[30,4,512]{2,1,0:T(4,128)S(1)}, f32[1,4,512]{2,1,0:T(4,128)S(1)}) fusion(f32[30,4,512]{2,1,0:T(4,128)S(1)} %constant_dynamic-update-slice_fusion.8, bf16[4,19,16,512]{3,2,1,0:T(8,128)(2,1)} %pops_ref.1), kind=kLoop, calls=%fused_computation.13 | loop fusion | flops 135168 | bytes 94208
  5.5 0.9 %constant_dynamic-update-slice_fusion.6 = f32[30,4,512]{2,1,0:T(4,128)S(1)} fusion(f32[30,4,512]{2,1,0:T(4,128)S(1)} %get-tuple-element.22, f32[1,4,512]{2,1,0:T(4,128)S(1)} %get-tuple-element.23, bf16[4,19,16,512]{3,2,1,0:T(8,128)(2,1)} %pops_ref.1), kind=kLoop, calls=%fused_computation.12 | loop fusion | flops 61440 | bytes 57344
  6.4 0.9 %constant_dynamic-update-slice_fusion.5 = f32[30,4,512]{2,1,0:T(4,128)S(1)} fusion(f32[30,4,512]{2,1,0:T(4,128)S(1)} %constant_dynamic-update-slice_fusion.6, f32[1,4,512]{2,1,0:T(4,128)S(1)} %get-tuple-element.23, bf16[4,19,16,512]{3,2,1,0:T(8,128)(2,1)} %pops_ref.1), kind=kLoop, calls=%fused_computation.11 | loop fusion | flops 61440 | bytes 57344
  7.2 0.9 %constant_dynamic-update-slice_fusion.4 = (f32[30,4,512]{2,1,0:T(4,128)S(1)}, f32[1,4,512]{2,1,0:T(4,128)S(1)}) fusion(f32[30,4,512]{2,1,0:T(4,128)S(1)} %constant_dynamic-update-slice_fusion.5, bf16[4,19,16,512]{3,2,1,0:T(8,128)(2,1)} %pops_ref.1), kind=kLoop, calls=%fused_computation.10 | loop fusion | flops 135168 | bytes 94208
  8.2 0.9 %constant_dynamic-update-slice_fusion.3 = f32[30,4,512]{2,1,0:T(4,128)S(1)} fusion(f32[30,4,512]{2,1,0:T(4,128)S(1)} %get-tuple-element.20, f32[1,4,512]{2,1,0:T(4,128)S(1)} %get-tuple-element.21, bf16[4,19,16,512]{3,2,1,0:T(8,128)(2,1)} %pops_ref.1), kind=kLoop, calls=%fused_computation.9 | loop fusion | flops 61440 | bytes 57344
  9.1 0.9 %constant_dynamic-update-slice_fusion.2 = f32[30,4,512]{2,1,0:T(4,128)S(1)} fusion(f32[30,4,512]{2,1,0:T(4,128)S(1)} %constant_dynamic-update-slice_fusion.3, f32[1,4,512]{2,1,0:T(4,128)S(1)} %get-tuple-element.21, bf16[4,19,16,512]{3,2,1,0:T(8,128)(2,1)} %pops_ref.1), kind=kLoop, calls=%fused_computation.8 | loop fusion | flops 61440 | bytes 57344
  9.9 0.1 constant_dynamic-update-slice_fusion.21
  10.1 0.1 constant_dynamic-update-slice_fusion.18
  10.3 0.1 constant_dynamic-update-slice_fusion.15
  10.5 4.2 %collective-permute-start = (f32[30,4,512]{2,1,0:T(4,128)S(1)}, f32[30,4,512]{2,1,0:T(4,128)S(1)}, u32[]{:S(2)}, u32[]{:S(2)}) collective-permute-start(f32[30,4,512]{2,1,0:T(4,128)S(1)} %get-tuple-element.98), channel_id=1, source_target_pairs={{0,224},{32,0},{64,32},{96,64},{128,96},{160,128},{192,160},{224,1... | collective-permute-start | bytes 737288 | tf_op jit(solution)/shard_map/ppermute | solution.py:255
  15.4 4.4 %collective-permute-start.2 = (f32[30,16,128]{2,1,0:T(8,128)S(1)}, f32[30,16,128]{2,1,0:T(8,128)S(1)}, u32[]{:S(2)}, u32[]{:S(2)}) collective-permute-start(f32[30,16,128]{2,1,0:T(8,128)S(1)} %get-tuple-element.96), channel_id=1, source_target_pairs={{0,31},{1,0},{2,1},{3,2},{4,3},{5,4},{6,5},{7,6},{8,7},{9,8},{10,9... | collective-permute-start | bytes 737288 | tf_op jit(solution)/shard_map/ppermute | solution.py:257
  19.9 0.0 collective-permute-done.hxp
  19.9 3.4 %collective-permute-done.1.hxm = f32[30,4,512]{2,1,0:T(4,128)S(1)} collective-permute-done((f32[30,4,512]{2,1,0:T(4,128)S(1)}, f32[30,4,512]{2,1,0:T(4,128)S(1)}, u32[]{:S(2)}, u32[]{:S(2)}) %collective-permute-start.1) | collective-permute-done | bytes 245792 | tf_op jit(solution)/shard_map/ppermute | solution.py:256
  23.4 3.5 %collective-permute-start.4 = (f32[30,8,128]{2,1,0:T(8,128)S(1)}, f32[30,8,128]{2,1,0:T(8,128)S(1)}, u32[]{:S(2)}, u32[]{:S(2)}) collective-permute-start(f32[30,8,128]{2,1,0:T(8,128)S(1)} %pad_maximum_fusion), channel_id=1, source_target_pairs={{0,31},{1,0},{2,1},{3,2},{4,3},{5,4},{6,5},{7,6},{8,7},{9,8},{10,9... | collective-permute-start | bytes 368648 | tf_op jit(solution)/shard_map/ppermute | solution.py:261
  27.0 0.1 collective-permute-start.5
  27.1 1.8 %collective-permute-done.3.hym = f32[30,16,128]{2,1,0:T(8,128)S(1)} collective-permute-done((f32[30,16,128]{2,1,0:T(8,128)S(1)}, f32[30,16,128]{2,1,0:T(8,128)S(1)}, u32[]{:S(2)}, u32[]{:S(2)}) %collective-permute-start.3) | collective-permute-done | bytes 245792 | tf_op jit(solution)/shard_map/ppermute | solution.py:258
  28.8 0.5 %collective-permute-done.4.cp = f32[30,8,128]{2,1,0:T(8,128)S(1)} collective-permute-done((f32[30,8,128]{2,1,0:T(8,128)S(1)}, f32[30,8,128]{2,1,0:T(8,128)S(1)}, u32[]{:S(2)}, u32[]{:S(2)}) %collective-permute-start.4) | collective-permute-done | bytes 122912 | tf_op jit(solution)/shard_map/ppermute | solution.py:261
  29.4 5.3 %collective-permute-done.5.cm = f32[30,8,128]{2,1,0:T(8,128)S(1)} collective-permute-done((f32[30,8,128]{2,1,0:T(8,128)S(1)}, f32[30,8,128]{2,1,0:T(8,128)S(1)}, u32[]{:S(2)}, u32[]{:S(2)}) %collective-permute-start.5) | collective-permute-done | bytes 122912 | tf_op jit(solution)/shard_map/ppermute | solution.py:262
  34.7 0.6 %copy-done.10 = f32[30,8,128]{2,1,0:T(8,128)} copy-done((f32[30,8,128]{2,1,0:T(8,128)}, f32[30,8,128]{2,1,0:T(8,128)S(1)}, u32[]{:S(2)}) %copy-start.10) | copy-done | bytes 122904
  35.3 11.3 %shard_map.68 = (f32[19,16,512]{2,1,0:T(8,128)}, f32[16,512]{1,0:T(8,128)}) custom-call(bf16[4,19,16,512]{3,2,1,0:T(8,128)(2,1)} %pops_ref.1, f32[19,16,512]{2,1,0:T(8,128)} %seed_ref.1, s32[16,512]{1,0:T(8,128)} %solid_ref.1, s32[16,512]{1,0:T(8,128)} %mask_ref.1, f32[16,512]{1,0:T(8,128)} %field_ref.1, f32[30,4,512]{2,1,0:T(4,128)} %copy-done.2, ...), custom_call_target="tpu_custom_call" | custom-call | tf_op jit(solution)/shard_map/pallas_call | solution.py:272
  (60 shorter events, 1.0 us)
Async XLA Ops:
  0.6 9.3 %copy-start = (bf16[4,19,16,512]{3,2,1,0:T(8,128)(2,1)S(1)}, bf16[4,19,16,512]{3,2,1,0:T(8,128)(2,1)}, u32[]{:S(2)}) copy-start(bf16[4,19,16,512]{3,2,1,0:T(8,128)(2,1)} %pops_ref.1) | copy-start | bytes 3735556
  0.6 9.8 %copy-start.6 = (s32[16,512]{1,0:T(8,128)S(1)}, s32[16,512]{1,0:T(8,128)}, u32[]{:S(2)}) copy-start(s32[16,512]{1,0:T(8,128)} %mask_ref.1) | copy-start | bytes 98308
  0.7 9.8 %copy-start.7 = (f32[16,512]{1,0:T(8,128)S(1)}, f32[16,512]{1,0:T(8,128)}, u32[]{:S(2)}) copy-start(f32[16,512]{1,0:T(8,128)} %field_ref.1) | copy-start | bytes 98308
  0.7 9.8 %copy-start.8 = (s32[16,512]{1,0:T(8,128)S(1)}, s32[16,512]{1,0:T(8,128)}, u32[]{:S(2)}) copy-start(s32[16,512]{1,0:T(8,128)} %solid_ref.1) | copy-start | bytes 98308
  10.0 4.8 %copy-start.1 = (f32[19,16,512]{2,1,0:T(8,128)S(1)}, f32[19,16,512]{2,1,0:T(8,128)}, u32[]{:S(2)}) copy-start(f32[19,16,512]{2,1,0:T(8,128)} %seed_ref.1) | copy-start | bytes 1867780
  10.5 9.4 %collective-permute-start = (f32[30,4,512]{2,1,0:T(4,128)S(1)}, f32[30,4,512]{2,1,0:T(4,128)S(1)}, u32[]{:S(2)}, u32[]{:S(2)}) collective-permute-start(f32[30,4,512]{2,1,0:T(4,128)S(1)} %get-tuple-element.98), channel_id=1, source_target_pairs={{0,224},{32,0},{64,32},{96,64},{128,96},{160,128},{192,160},{224,1... | collective-permute-start | bytes 737288 | tf_op jit(solution)/shard_map/ppermute | solution.py:255
  14.7 8.6 %collective-permute-start.1 = (f32[30,4,512]{2,1,0:T(4,128)S(1)}, f32[30,4,512]{2,1,0:T(4,128)S(1)}, u32[]{:S(2)}, u32[]{:S(2)}) collective-permute-start(f32[30,4,512]{2,1,0:T(4,128)S(1)} %get-tuple-element.97), channel_id=1, source_target_pairs={{0,32},{32,64},{64,96},{96,128},{128,160},{160,192},{192,224},{224... | collective-permute-start | bytes 737288 | tf_op jit(solution)/shard_map/ppermute | solution.py:256
  15.4 11.6 %collective-permute-start.2 = (f32[30,16,128]{2,1,0:T(8,128)S(1)}, f32[30,16,128]{2,1,0:T(8,128)S(1)}, u32[]{:S(2)}, u32[]{:S(2)}) collective-permute-start(f32[30,16,128]{2,1,0:T(8,128)S(1)} %get-tuple-element.96), channel_id=1, source_target_pairs={{0,31},{1,0},{2,1},{3,2},{4,3},{5,4},{6,5},{7,6},{8,7},{9,8},{10,9... | collective-permute-start | bytes 737288 | tf_op jit(solution)/shard_map/ppermute | solution.py:257
  19.9 8.9 %collective-permute-start.3 = (f32[30,16,128]{2,1,0:T(8,128)S(1)}, f32[30,16,128]{2,1,0:T(8,128)S(1)}, u32[]{:S(2)}, u32[]{:S(2)}) collective-permute-start(f32[30,16,128]{2,1,0:T(8,128)S(1)} %get-tuple-element.95), channel_id=1, source_target_pairs={{0,1},{1,2},{2,3},{3,4},{4,5},{5,6},{6,7},{7,8},{8,9},{9,10},{10,1... | collective-permute-start | bytes 737288 | tf_op jit(solution)/shard_map/ppermute | solution.py:258
  19.9 14.7 %copy-start.2 = (f32[30,4,512]{2,1,0:T(4,128)}, f32[30,4,512]{2,1,0:T(4,128)S(1)}, u32[]{:S(2)}) copy-start(f32[30,4,512]{2,1,0:T(4,128)S(1)} %collective-permute-done.hxp) | copy-start | bytes 737284
  23.3 11.3 %copy-start.3 = (f32[30,4,512]{2,1,0:T(4,128)}, f32[30,4,512]{2,1,0:T(4,128)S(1)}, u32[]{:S(2)}) copy-start(f32[30,4,512]{2,1,0:T(4,128)S(1)} %collective-permute-done.1.hxm) | copy-start | bytes 737284
  23.4 6.0 %collective-permute-start.4 = (f32[30,8,128]{2,1,0:T(8,128)S(1)}, f32[30,8,128]{2,1,0:T(8,128)S(1)}, u32[]{:S(2)}, u32[]{:S(2)}) collective-permute-start(f32[30,8,128]{2,1,0:T(8,128)S(1)} %pad_maximum_fusion), channel_id=1, source_target_pairs={{0,31},{1,0},{2,1},{3,2},{4,3},{5,4},{6,5},{7,6},{8,7},{9,8},{10,9... | collective-permute-start | bytes 368648 | tf_op jit(solution)/shard_map/ppermute | solution.py:261
  27.0 7.7 %collective-permute-start.5 = (f32[30,8,128]{2,1,0:T(8,128)S(1)}, f32[30,8,128]{2,1,0:T(8,128)S(1)}, u32[]{:S(2)}, u32[]{:S(2)}) collective-permute-start(f32[30,8,128]{2,1,0:T(8,128)S(1)} %pad_maximum_fusion.1), channel_id=1, source_target_pairs={{0,1},{1,2},{2,3},{3,4},{4,5},{5,6},{6,7},{7,8},{8,9},{9,10},{10,1... | collective-permute-start | bytes 368648 | tf_op jit(solution)/shard_map/ppermute | solution.py:262
  27.1 7.6 %copy-start.4 = (f32[30,16,128]{2,1,0:T(8,128)}, f32[30,16,128]{2,1,0:T(8,128)S(1)}, u32[]{:S(2)}) copy-start(f32[30,16,128]{2,1,0:T(8,128)S(1)} %collective-permute-done.2.hyp) | copy-start | bytes 737284
  28.8 5.8 %copy-start.5 = (f32[30,16,128]{2,1,0:T(8,128)}, f32[30,16,128]{2,1,0:T(8,128)S(1)}, u32[]{:S(2)}) copy-start(f32[30,16,128]{2,1,0:T(8,128)S(1)} %collective-permute-done.3.hym) | copy-start | bytes 737284
  29.4 5.3 %copy-start.9 = (f32[30,8,128]{2,1,0:T(8,128)}, f32[30,8,128]{2,1,0:T(8,128)S(1)}, u32[]{:S(2)}) copy-start(f32[30,8,128]{2,1,0:T(8,128)S(1)} %collective-permute-done.4.cp) | copy-start | bytes 368644
  34.7 0.6 %copy-start.10 = (f32[30,8,128]{2,1,0:T(8,128)}, f32[30,8,128]{2,1,0:T(8,128)S(1)}, u32[]{:S(2)}) copy-start(f32[30,8,128]{2,1,0:T(8,128)S(1)} %collective-permute-done.5.cm) | copy-start | bytes 368644

commit v3 on v2

--- a/solution.py
+++ b/solution.py
@@ -229,15 +229,50 @@
             lax.fori_loop(0, n_halo, halo_body, 0)
 
 
-def _message(saved_pops, seed, solid, mask, field, rs, ls):
+def _prep_kernel(pops_ref, seed_ref, solid_ref, mask_ref, field_ref, x_lo, x_hi, y_lo, y_hi, u_ref):
+    steps = pops_ref.shape[0]
+    _, rows, flat = seed_ref.shape
+    yw = DEPTH * NZ
+    for n, step in enumerate(reversed(range(1, steps))):
+        for t in range(flat // LANES):
+            sl = slice(LANES * t, LANES * (t + 1))
+            f = [pops_ref[step, i, :, sl].astype(jnp.float32) * W32[i] for i in range(19)]
+            _, u = _velocity(f)
+            for a in range(3):
+                u_ref[3 * n + a, :, sl] = u[a]
+    nu = 3 * (steps - 1)
+    rate = OMEGA_BASE + OMEGA_SPAN * field_ref[...] * mask_ref[...].astype(jnp.float32)
+    solid = solid_ref[...].astype(jnp.float32)
+    fields = [lambda rs, ls, i=i: seed_ref[i, rs, ls] for i in range(19)]
+    fields += [lambda rs, ls, k=k: u_ref[k, rs, ls] for k in range(nu)]
+    fields += [lambda rs, ls: rate[rs, ls], lambda rs, ls: solid[rs, ls]]
+    for k, get in enumerate(fields):
+        x_lo[k] = get(slice(0, DEPTH), slice(0, flat))
+        x_hi[k] = get(slice(rows - DEPTH, rows), slice(0, flat))
+        y_lo[k] = get(slice(0, rows), slice(0, yw))
+        y_hi[k] = get(slice(0, rows), slice(flat - yw, flat))
+
+
+def _messages(saved_pops, seed, solid, mask, field):
     steps = saved_pops.shape[0]
-    rate = OMEGA_BASE + OMEGA_SPAN * field[rs, ls] * mask[rs, ls].astype(jnp.float32)
-    parts = [seed[:, rs, ls]]
-    for s in reversed(range(1, steps)):
-        f = [saved_pops[s, i][rs, ls].astype(jnp.float32) * W32[i] for i in range(19)]
-        parts += [u[None] for u in _velocity(f)[1]]
-    parts += [rate[None], solid[rs, ls].astype(jnp.float32)[None]]
-    return jnp.concatenate(parts, axis=0)
+    _, rows, flat = seed.shape
+    nfield = 19 + 3 * (steps - 1) + 2
+    yw = DEPTH * NZ
+    shapes = [(nfield, DEPTH, flat), (nfield, DEPTH, flat), (nfield, rows, yw), (nfield, rows, yw)]
+    args = [saved_pops, seed, solid, mask, field]
+
+    def full(shape):
+        nd = len(shape)
+        return pl.BlockSpec(shape, lambda i, _n=nd: (0,) * _n)
+
+    return pl.pallas_call(
+        _prep_kernel,
+        grid=(1,),
+        in_specs=[full(a.shape) for a in args],
+        out_specs=[full(sh) for sh in shapes],
+        out_shape=[jax.ShapeDtypeStruct(sh, jnp.float32) for sh in shapes],
+        scratch_shapes=[pltpu.VMEM((3 * (steps - 1), rows, flat), jnp.float32)],
+    )(*args)
 
 
 def _shift(n, d):
@@ -249,13 +284,12 @@
     ny = lax.axis_size("gy")
     _, rows, flat = seed_adjoint.shape
     yw = DEPTH * NZ
-    ins = (saved_pops, seed_adjoint, solid_label, design_mask, design_field)
-    full_r, full_l = slice(0, rows), slice(0, flat)
     lo_l, hi_l = slice(0, yw), slice(flat - yw, flat)
-    hxp = lax.ppermute(_message(*ins, slice(0, DEPTH), full_l), "gx", _shift(nx, -1))
-    hxm = lax.ppermute(_message(*ins, slice(rows - DEPTH, rows), full_l), "gx", _shift(nx, 1))
-    hyp = lax.ppermute(_message(*ins, full_r, lo_l), "gy", _shift(ny, -1))
-    hym = lax.ppermute(_message(*ins, full_r, hi_l), "gy", _shift(ny, 1))
+    x_lo, x_hi, y_lo, y_hi = _messages(saved_pops, seed_adjoint, solid_label, design_mask, design_field)
+    hxp = lax.ppermute(x_lo, "gx", _shift(nx, -1))
+    hxm = lax.ppermute(x_hi, "gx", _shift(nx, 1))
+    hyp = lax.ppermute(y_lo, "gy", _shift(ny, -1))
+    hym = lax.ppermute(y_hi, "gy", _shift(ny, 1))
     c_lo = jnp.concatenate([hxp[:, :, lo_l], hxm[:, :, lo_l]], axis=1)
     c_hi = jnp.concatenate([hxp[:, :, hi_l], hxm[:, :, hi_l]], axis=1)
     cp = lax.ppermute(c_lo, "gy", _shift(ny, -1))

time: 47.4 us -> 39.7 us (0.84); the launches traced: 46.6 us -> 39.6 us
  other arithmetic: 9.05 us -> 0.06 us
  Pallas kernels: 11.3 us -> 14 us
  local copies, waits for them, and re-layouts: 2.05 us -> 0.72 us
  waiting for transfers between devices: 11 us -> 12 us
    unnamed x38 -> x0, other arithmetic: 8.98 us -> none
    pallas_call x0 -> x1, Pallas kernels: none -> 2.67 us  [_messages(): pl.pallas_call(_prep_kernel, grid=(1,), in_specs=[full(a.shape) for a in...]
    unnamed x24 -> x12, local copies, waits for them, and re-layouts: 1.93 us -> 0.68 us
    ppermute x1, waiting for transfers between devices: 0.54 us -> 1.35 us  [body(): cp = lax.ppermute(c_lo, 'gy', _shift(ny, -1))]
  transfers between devices with their start and end apart: 6 -> 6, of which waited for: 4 -> 5; matrix products, arithmetic and copies ran while one was open for 1% -> 0% of each run, Pallas kernels for 0% -> 0%
where the time goes in v3:
time: 39.7 us; the launch traced here: 39.6 us
  Pallas kernels  14 us (35%)
  starting transfers between devices  12.1 us (30%)
  waiting for transfers between devices  12 us (30%)
  local copies, waits for them, and re-layouts  0.72 us (2%)
  between operations  0.71 us (2%)
    pallas_call x1, Pallas kernels, body(): pl.pallas_call(_fused_kernel, grid=(1,), in_specs=[full(a.shape) for a in...  11.3 us
    ppermute x1, waiting for transfers between devices, body(): cm = lax.ppermute(c_hi, 'gy', _shift(ny, 1))  5.29 us
    ppermute x1, starting transfers between devices, body(): hyp = lax.ppermute(y_lo, 'gy', _shift(ny, -1))  4.37 us
    ppermute x1, starting transfers between devices, body(): hxp = lax.ppermute(x_lo, 'gx', _shift(nx, -1))  4.12 us
    ppermute x1, starting transfers between devices, body(): cp = lax.ppermute(c_lo, 'gy', _shift(ny, -1))  3.54 us
    ppermute x1, waiting for transfers between devices, body(): hxm = lax.ppermute(x_hi, 'gx', _shift(nx, 1))  3.28 us
    pallas_call x1, Pallas kernels, _messages(): pl.pallas_call(_prep_kernel, grid=(1,), in_specs=[full(a.shape) for a in...  2.67 us
    ppermute x1, waiting for transfers between devices, body(): cp = lax.ppermute(c_lo, 'gy', _shift(ny, -1))  1.35 us
  transfers between devices with their start and end apart: 6, of which 5 were waited for; matrix products, arithmetic and copies ran while one was open for 0% of the time, Pallas kernels for 0%

profile of v3, /device:TPU:0, one launch (start us, length us, event | category | flops | bytes accessed | tf_op | source)
XLA Modules:
  0.0 39.6 jit_solution(2459028131251878016)
XLA Ops:
  0.6 2.7 %shard_map.68 = (f32[30,4,512]{2,1,0:T(4,128)}, f32[30,4,512]{2,1,0:T(4,128)}, f32[30,16,128]{2,1,0:T(8,128)}, f32[30,16,128]{2,1,0:T(8,128)}) custom-call(bf16[4,19,16,512]{3,2,1,0:T(8,128)(2,1)} %pops_ref.3, f32[19,16,512]{2,1,0:T(8,128)} %seed_ref.3, s32[16,512]{1,0:T(8,128)} %solid_ref.3, s32[16,512]{1,0:T(8,128)} %mask_ref.3, f32[16,512]{1,0:T(8,128)} %field_ref.3), custom_call_target="tpu_custom_call" | custom-call | tf_op jit(solution)/shard_map/pallas_call | solution.py:268
  3.3 4.1 %collective-permute-start = (f32[30,4,512]{2,1,0:T(4,128)}, f32[30,4,512]{2,1,0:T(4,128)S(1)}, u32[]{:S(2)}, u32[]{:S(2)}) collective-permute-start(f32[30,4,512]{2,1,0:T(4,128)} %get-tuple-element.6), channel_id=1, source_target_pairs={{0,224},{32,0},{64,32},{96,64},{128,96},{160,128},{192,160},{224,1... | collective-permute-start | bytes 737288 | tf_op jit(solution)/shard_map/ppermute | solution.py:289
  7.4 0.0 collective-permute-start.1
  7.4 4.4 %collective-permute-start.2 = (f32[30,16,128]{2,1,0:T(8,128)}, f32[30,16,128]{2,1,0:T(8,128)S(1)}, u32[]{:S(2)}, u32[]{:S(2)}) collective-permute-start(f32[30,16,128]{2,1,0:T(8,128)} %get-tuple-element.8), channel_id=1, source_target_pairs={{0,31},{1,0},{2,1},{3,2},{4,3},{5,4},{6,5},{7,6},{8,7},{9,8},{10,9... | collective-permute-start | bytes 737288 | tf_op jit(solution)/shard_map/ppermute | solution.py:291
  11.8 0.0 collective-permute-start.3
  11.8 1.2 %collective-permute-done.hxp = f32[30,4,512]{2,1,0:T(4,128)S(1)} collective-permute-done((f32[30,4,512]{2,1,0:T(4,128)}, f32[30,4,512]{2,1,0:T(4,128)S(1)}, u32[]{:S(2)}, u32[]{:S(2)}) %collective-permute-start) | collective-permute-done | bytes 245792 | tf_op jit(solution)/shard_map/ppermute | solution.py:289
  12.9 0.0 copy-start
  13.0 3.3 %collective-permute-done.1.hxm = f32[30,4,512]{2,1,0:T(4,128)S(1)} collective-permute-done((f32[30,4,512]{2,1,0:T(4,128)}, f32[30,4,512]{2,1,0:T(4,128)S(1)}, u32[]{:S(2)}, u32[]{:S(2)}) %collective-permute-start.1) | collective-permute-done | bytes 245792 | tf_op jit(solution)/shard_map/ppermute | solution.py:290
  16.3 0.0 copy-start.1
  16.3 3.5 %collective-permute-start.4 = (f32[30,8,128]{2,1,0:T(8,128)S(1)}, f32[30,8,128]{2,1,0:T(8,128)S(1)}, u32[]{:S(2)}, u32[]{:S(2)}) collective-permute-start(f32[30,8,128]{2,1,0:T(8,128)S(1)} %pad_maximum_fusion), channel_id=1, source_target_pairs={{0,31},{1,0},{2,1},{3,2},{4,3},{5,4},{6,5},{7,6},{8,7},{9,8},{10,9... | collective-permute-start | bytes 368648 | tf_op jit(solution)/shard_map/ppermute | solution.py:295
  19.9 0.1 collective-permute-start.5
  20.0 0.0 collective-permute-done.2.hyp
  20.0 0.0 copy-start.2
  20.0 0.9 %collective-permute-done.3.hym = f32[30,16,128]{2,1,0:T(8,128)S(1)} collective-permute-done((f32[30,16,128]{2,1,0:T(8,128)}, f32[30,16,128]{2,1,0:T(8,128)S(1)}, u32[]{:S(2)}, u32[]{:S(2)}) %collective-permute-start.3) | collective-permute-done | bytes 245792 | tf_op jit(solution)/shard_map/ppermute | solution.py:292
  20.9 1.4 %collective-permute-done.4.cp = f32[30,8,128]{2,1,0:T(8,128)S(1)} collective-permute-done((f32[30,8,128]{2,1,0:T(8,128)S(1)}, f32[30,8,128]{2,1,0:T(8,128)S(1)}, u32[]{:S(2)}, u32[]{:S(2)}) %collective-permute-start.4) | collective-permute-done | bytes 122912 | tf_op jit(solution)/shard_map/ppermute | solution.py:295
  22.3 5.3 %collective-permute-done.5.cm = f32[30,8,128]{2,1,0:T(8,128)S(1)} collective-permute-done((f32[30,8,128]{2,1,0:T(8,128)S(1)}, f32[30,8,128]{2,1,0:T(8,128)S(1)}, u32[]{:S(2)}, u32[]{:S(2)}) %collective-permute-start.5) | collective-permute-done | bytes 122912 | tf_op jit(solution)/shard_map/ppermute | solution.py:296
  27.6 0.0 copy-done
  27.6 0.0 copy-done.1
  27.6 0.0 copy-done.2
  27.6 0.0 copy-done.3
  27.6 0.0 copy-done.4
  27.6 0.0 copy-start.5
  27.6 0.7 %copy-done.5 = f32[30,8,128]{2,1,0:T(8,128)} copy-done((f32[30,8,128]{2,1,0:T(8,128)}, f32[30,8,128]{2,1,0:T(8,128)S(1)}, u32[]{:S(2)}) %copy-start.5) | copy-done | bytes 122904
  28.3 11.3 %shard_map.69 = (f32[19,16,512]{2,1,0:T(8,128)}, f32[16,512]{1,0:T(8,128)}) custom-call(bf16[4,19,16,512]{3,2,1,0:T(8,128)(2,1)} %pops_ref.3, f32[19,16,512]{2,1,0:T(8,128)} %seed_ref.3, s32[16,512]{1,0:T(8,128)} %solid_ref.3, s32[16,512]{1,0:T(8,128)} %mask_ref.3, f32[16,512]{1,0:T(8,128)} %field_ref.3, f32[30,4,512]{2,1,0:T(4,128)} %copy-done, ...), custom_call_target="tpu_custom_call" | custom-call | tf_op jit(solution)/shard_map/pallas_call | solution.py:306
  (6 shorter events, 0.1 us)
Async XLA Ops:
  3.3 9.7 %collective-permute-start = (f32[30,4,512]{2,1,0:T(4,128)}, f32[30,4,512]{2,1,0:T(4,128)S(1)}, u32[]{:S(2)}, u32[]{:S(2)}) collective-permute-start(f32[30,4,512]{2,1,0:T(4,128)} %get-tuple-element.6), channel_id=1, source_target_pairs={{0,224},{32,0},{64,32},{96,64},{128,96},{160,128},{192,160},{224,1... | collective-permute-start | bytes 737288 | tf_op jit(solution)/shard_map/ppermute | solution.py:289
  7.4 8.8 %collective-permute-start.1 = (f32[30,4,512]{2,1,0:T(4,128)}, f32[30,4,512]{2,1,0:T(4,128)S(1)}, u32[]{:S(2)}, u32[]{:S(2)}) collective-permute-start(f32[30,4,512]{2,1,0:T(4,128)} %get-tuple-element.7), channel_id=1, source_target_pairs={{0,32},{32,64},{64,96},{96,128},{128,160},{160,192},{192,224},{224... | collective-permute-start | bytes 737288 | tf_op jit(solution)/shard_map/ppermute | solution.py:290
  7.4 12.6 %collective-permute-start.2 = (f32[30,16,128]{2,1,0:T(8,128)}, f32[30,16,128]{2,1,0:T(8,128)S(1)}, u32[]{:S(2)}, u32[]{:S(2)}) collective-permute-start(f32[30,16,128]{2,1,0:T(8,128)} %get-tuple-element.8), channel_id=1, source_target_pairs={{0,31},{1,0},{2,1},{3,2},{4,3},{5,4},{6,5},{7,6},{8,7},{9,8},{10,9... | collective-permute-start | bytes 737288 | tf_op jit(solution)/shard_map/ppermute | solution.py:291
  11.8 9.2 %collective-permute-start.3 = (f32[30,16,128]{2,1,0:T(8,128)}, f32[30,16,128]{2,1,0:T(8,128)S(1)}, u32[]{:S(2)}, u32[]{:S(2)}) collective-permute-start(f32[30,16,128]{2,1,0:T(8,128)} %get-tuple-element.9), channel_id=1, source_target_pairs={{0,1},{1,2},{2,3},{3,4},{4,5},{5,6},{6,7},{7,8},{8,9},{9,10},{10,1... | collective-permute-start | bytes 737288 | tf_op jit(solution)/shard_map/ppermute | solution.py:292
  12.9 14.6 %copy-start = (f32[30,4,512]{2,1,0:T(4,128)}, f32[30,4,512]{2,1,0:T(4,128)S(1)}, u32[]{:S(2)}) copy-start(f32[30,4,512]{2,1,0:T(4,128)S(1)} %collective-permute-done.hxp) | copy-start | bytes 737284
  16.3 11.3 %copy-start.1 = (f32[30,4,512]{2,1,0:T(4,128)}, f32[30,4,512]{2,1,0:T(4,128)S(1)}, u32[]{:S(2)}) copy-start(f32[30,4,512]{2,1,0:T(4,128)S(1)} %collective-permute-done.1.hxm) | copy-start | bytes 737284
  16.3 6.0 %collective-permute-start.4 = (f32[30,8,128]{2,1,0:T(8,128)S(1)}, f32[30,8,128]{2,1,0:T(8,128)S(1)}, u32[]{:S(2)}, u32[]{:S(2)}) collective-permute-start(f32[30,8,128]{2,1,0:T(8,128)S(1)} %pad_maximum_fusion), channel_id=1, source_target_pairs={{0,31},{1,0},{2,1},{3,2},{4,3},{5,4},{6,5},{7,6},{8,7},{9,8},{10,9... | collective-permute-start | bytes 368648 | tf_op jit(solution)/shard_map/ppermute | solution.py:295
  19.9 7.7 %collective-permute-start.5 = (f32[30,8,128]{2,1,0:T(8,128)S(1)}, f32[30,8,128]{2,1,0:T(8,128)S(1)}, u32[]{:S(2)}, u32[]{:S(2)}) collective-permute-start(f32[30,8,128]{2,1,0:T(8,128)S(1)} %pad_maximum_fusion.1), channel_id=1, source_target_pairs={{0,1},{1,2},{2,3},{3,4},{4,5},{5,6},{6,7},{7,8},{8,9},{9,10},{10,1... | collective-permute-start | bytes 368648 | tf_op jit(solution)/shard_map/ppermute | solution.py:296
  20.0 7.6 %copy-start.2 = (f32[30,16,128]{2,1,0:T(8,128)}, f32[30,16,128]{2,1,0:T(8,128)S(1)}, u32[]{:S(2)}) copy-start(f32[30,16,128]{2,1,0:T(8,128)S(1)} %collective-permute-done.2.hyp) | copy-start | bytes 737284
  20.9 6.7 %copy-start.3 = (f32[30,16,128]{2,1,0:T(8,128)}, f32[30,16,128]{2,1,0:T(8,128)S(1)}, u32[]{:S(2)}) copy-start(f32[30,16,128]{2,1,0:T(8,128)S(1)} %collective-permute-done.3.hym) | copy-start | bytes 737284
  22.3 5.3 %copy-start.4 = (f32[30,8,128]{2,1,0:T(8,128)}, f32[30,8,128]{2,1,0:T(8,128)S(1)}, u32[]{:S(2)}) copy-start(f32[30,8,128]{2,1,0:T(8,128)S(1)} %collective-permute-done.4.cp) | copy-start | bytes 368644
  27.6 0.7 %copy-start.5 = (f32[30,8,128]{2,1,0:T(8,128)}, f32[30,8,128]{2,1,0:T(8,128)S(1)}, u32[]{:S(2)}) copy-start(f32[30,8,128]{2,1,0:T(8,128)S(1)} %collective-permute-done.5.cm) | copy-start | bytes 368644

commit v4 on v3

--- a/solution.py
+++ b/solution.py
@@ -147,19 +147,17 @@
         p_ref[i] = v
 
 
-def _fill_ext(dst, own, hxp, hxm, hyp, hym, cp, cm, rows, flat):
+def _fill_ext(dst, own, hxp, hxm, hyp, hym, rows, flat):
     yw = DEPTH * NZ
     if own is not None:
         dst[0:rows, 0:flat] = own
     dst[rows : rows + DEPTH, 0:flat] = hxp
     dst[rows + DEPTH : rows + 2 * DEPTH, 0:flat] = hxm
-    dst[0:rows, flat : flat + yw] = hyp
-    dst[rows : rows + 2 * DEPTH, flat : flat + yw] = cp
-    dst[0:rows, flat + yw : flat + 2 * yw] = hym
-    dst[rows : rows + 2 * DEPTH, flat + yw : flat + 2 * yw] = cm
-
-
-def _fused_kernel(pops_ref, seed_ref, solid_ref, mask_ref, field_ref, hxp, hxm, hyp, hym, cp, cm,
+    dst[:, flat : flat + yw] = hyp
+    dst[:, flat + yw : flat + 2 * yw] = hym
+
+
+def _fused_kernel(pops_ref, seed_ref, solid_ref, mask_ref, field_ref, hxp, hxm, hyp, hym,
                   adj_out, sens_out, a_ref, p_ref, u_ref, rate_ref, solid_ext):
     steps = pops_ref.shape[0]
     _, rows, flat = seed_ref.shape
@@ -168,7 +166,7 @@
     mask_all = mask_ref[...].astype(jnp.float32)
     rate_own = OMEGA_BASE + OMEGA_SPAN * field_ref[...] * mask_all
     halo = lambda k, scale=None: [
-        h[k] if scale is None else h[k] * scale for h in (hxp, hxm, hyp, hym, cp, cm)
+        h[k] if scale is None else h[k] * scale for h in (hxp, hxm, hyp, hym)
     ]
     _fill_ext(rate_ref, rate_own, *halo(nfield - 2), rows, flat)
     _fill_ext(solid_ext, solid_ref[...].astype(jnp.float32), *halo(nfield - 1), rows, flat)
@@ -288,16 +286,14 @@
     x_lo, x_hi, y_lo, y_hi = _messages(saved_pops, seed_adjoint, solid_label, design_mask, design_field)
     hxp = lax.ppermute(x_lo, "gx", _shift(nx, -1))
     hxm = lax.ppermute(x_hi, "gx", _shift(nx, 1))
-    hyp = lax.ppermute(y_lo, "gy", _shift(ny, -1))
-    hym = lax.ppermute(y_hi, "gy", _shift(ny, 1))
-    c_lo = jnp.concatenate([hxp[:, :, lo_l], hxm[:, :, lo_l]], axis=1)
-    c_hi = jnp.concatenate([hxp[:, :, hi_l], hxm[:, :, hi_l]], axis=1)
-    cp = lax.ppermute(c_lo, "gy", _shift(ny, -1))
-    cm = lax.ppermute(c_hi, "gy", _shift(ny, 1))
+    col_lo = jnp.concatenate([y_lo, hxp[:, :, lo_l], hxm[:, :, lo_l]], axis=1)
+    col_hi = jnp.concatenate([y_hi, hxp[:, :, hi_l], hxm[:, :, hi_l]], axis=1)
+    hyp = lax.ppermute(col_lo, "gy", _shift(ny, -1))
+    hym = lax.ppermute(col_hi, "gy", _shift(ny, 1))
     erows = rows + 2 * DEPTH
     eflat = flat + 2 * yw
     ext = (19, erows, eflat)
-    args = [saved_pops, seed_adjoint, solid_label, design_mask, design_field, hxp, hxm, hyp, hym, cp, cm]
+    args = [saved_pops, seed_adjoint, solid_label, design_mask, design_field, hxp, hxm, hyp, hym]
 
     def full(shape):
         nd = len(shape)

time: 39.7 us -> 43.5 us (1.096)
  waiting for transfers between devices: 12 us -> 19 us
  starting transfers between devices: 12.1 us -> 7.74 us
  other arithmetic: 0.06 us -> 1.12 us
    ppermute x1, waiting for transfers between devices: 1.15 us -> 5.53 us  [body(): hxp = lax.ppermute(x_lo, 'gx', _shift(nx, -1))]
    ppermute x4 -> x2, starting transfers between devices: 7.99 us -> 3.62 us  [the longest x1 3.54 us: body(): hyp = lax.ppermute(col_lo, 'gy', _shift(ny, -1))]
    ppermute x4 -> x2, waiting for transfers between devices: 7.59 us -> 10.2 us  [the longest x1 5.35 us: body(): hym = lax.ppermute(col_hi, 'gy', _shift(ny, 1))]
    concatenate x2, other arithmetic: 0.06 us -> 1.12 us  [the longest x1 1.07 us: body(): col_lo = jnp.concatenate([y_lo, hxp[:, :, lo_l], hxm[:, :, lo_l]], axis=1)]
  transfers between devices with their start and end apart: 6 -> 4, of which waited for: 5 -> 4; matrix products, arithmetic and copies ran while one was open for 0% -> 0% of each run, Pallas kernels for 0% -> 0%
where the time goes in v4:
time: 43.5 us; the launch traced here: 43.4 us
  waiting for transfers between devices  19 us (44%)
  Pallas kernels  14 us (32%)
  starting transfers between devices  7.74 us (18%)
  other arithmetic  1.12 us (3%)
  local copies, waits for them, and re-layouts  0.79 us (2%)
  between operations  0.67 us (2%)
    pallas_call x1, Pallas kernels, body(): pl.pallas_call(_fused_kernel, grid=(1,), in_specs=[full(a.shape) for a in...  11.3 us
    ppermute x1, waiting for transfers between devices, body(): hxp = lax.ppermute(x_lo, 'gx', _shift(nx, -1))  5.53 us
    ppermute x1, waiting for transfers between devices, body(): hym = lax.ppermute(col_hi, 'gy', _shift(ny, 1))  5.35 us
    ppermute x1, waiting for transfers between devices, body(): hyp = lax.ppermute(col_lo, 'gy', _shift(ny, -1))  4.89 us
    ppermute x1, starting transfers between devices, body(): hxp = lax.ppermute(x_lo, 'gx', _shift(nx, -1))  4.12 us
    ppermute x1, starting transfers between devices, body(): hyp = lax.ppermute(col_lo, 'gy', _shift(ny, -1))  3.54 us
    ppermute x1, waiting for transfers between devices, body(): hxm = lax.ppermute(x_hi, 'gx', _shift(nx, 1))  3.28 us
    pallas_call x1, Pallas kernels, _messages(): pl.pallas_call(_prep_kernel, grid=(1,), in_specs=[full(a.shape) for a in...  2.67 us
  transfers between devices with their start and end apart: 4, of which 4 were waited for; matrix products, arithmetic and copies ran while one was open for 0% of the time, Pallas kernels for 0%

profile of v4, /device:TPU:0, one launch (start us, length us, event | category | flops | bytes accessed | tf_op | source)
XLA Modules:
  0.0 43.4 jit_solution(1465965561267867148)
XLA Ops:
  0.6 2.7 %shard_map.68 = (f32[30,4,512]{2,1,0:T(4,128)}, f32[30,4,512]{2,1,0:T(4,128)}, f32[30,16,128]{2,1,0:T(8,128)}, f32[30,16,128]{2,1,0:T(8,128)}) custom-call(bf16[4,19,16,512]{3,2,1,0:T(8,128)(2,1)} %pops_ref.3, f32[19,16,512]{2,1,0:T(8,128)} %seed_ref.3, s32[16,512]{1,0:T(8,128)} %solid_ref.3, s32[16,512]{1,0:T(8,128)} %mask_ref.3, f32[16,512]{1,0:T(8,128)} %field_ref.3), custom_call_target="tpu_custom_call" | custom-call | tf_op jit(solution)/shard_map/pallas_call | solution.py:266
  3.3 0.0 copy-start.4
  3.3 4.1 %collective-permute-start = (f32[30,4,512]{2,1,0:T(4,128)}, f32[30,4,512]{2,1,0:T(4,128)S(1)}, u32[]{:S(2)}, u32[]{:S(2)}) collective-permute-start(f32[30,4,512]{2,1,0:T(4,128)} %get-tuple-element.6), channel_id=1, source_target_pairs={{0,224},{32,0},{64,32},{96,64},{128,96},{160,128},{192,160},{224,1... | collective-permute-start | bytes 737288 | tf_op jit(solution)/shard_map/ppermute | solution.py:287
  7.4 0.0 collective-permute-start.1
  7.4 5.5 %collective-permute-done.hxp = f32[30,4,512]{2,1,0:T(4,128)S(1)} collective-permute-done((f32[30,4,512]{2,1,0:T(4,128)}, f32[30,4,512]{2,1,0:T(4,128)S(1)}, u32[]{:S(2)}, u32[]{:S(2)}) %collective-permute-start) | collective-permute-done | bytes 245792 | tf_op jit(solution)/shard_map/ppermute | solution.py:287
  12.9 0.0 copy-start
  13.0 3.3 %collective-permute-done.1.hxm = f32[30,4,512]{2,1,0:T(4,128)S(1)} collective-permute-done((f32[30,4,512]{2,1,0:T(4,128)}, f32[30,4,512]{2,1,0:T(4,128)S(1)}, u32[]{:S(2)}, u32[]{:S(2)}) %collective-permute-start.1) | collective-permute-done | bytes 245792 | tf_op jit(solution)/shard_map/ppermute | solution.py:288
  16.3 0.0 copy-start.1
  16.3 1.1 %pad_maximum_fusion = f32[30,24,128]{2,1,0:T(8,128)S(1)} fusion(f32[30,4,128]{2,1,0:T(4,128)S(1)} %get-tuple-element.13, f32[30,4,128]{2,1,0:T(4,128)S(1)} %get-tuple-element.11, f32[30,16,128]{2,1,0:T(8,128)} %get-tuple-element.8), kind=kLoop, calls=%fused_computation | loop fusion | flops 184320 | bytes 737280 | tf_op jit(solution)/shard_map/concatenate | solution.py:289
  17.4 3.5 %collective-permute-start.2 = (f32[30,24,128]{2,1,0:T(8,128)S(1)}, f32[30,24,128]{2,1,0:T(8,128)S(1)}, u32[]{:S(2)}, u32[]{:S(2)}) collective-permute-start(f32[30,24,128]{2,1,0:T(8,128)S(1)} %pad_maximum_fusion), channel_id=1, source_target_pairs={{0,31},{1,0},{2,1},{3,2},{4,3},{5,4},{6,5},{7,6},{8,7},{9,8},{10,9... | collective-permute-start | bytes 1105928 | tf_op jit(solution)/shard_map/ppermute | solution.py:291
  20.9 0.0 copy-done.4
  20.9 0.1 collective-permute-start.3
  21.0 4.9 %collective-permute-done.2.hyp = f32[30,24,128]{2,1,0:T(8,128)S(1)} collective-permute-done((f32[30,24,128]{2,1,0:T(8,128)S(1)}, f32[30,24,128]{2,1,0:T(8,128)S(1)}, u32[]{:S(2)}, u32[]{:S(2)}) %collective-permute-start.2) | collective-permute-done | bytes 368672 | tf_op jit(solution)/shard_map/ppermute | solution.py:291
  25.9 0.0 copy-start.2
  25.9 5.4 %collective-permute-done.3.hym = f32[30,24,128]{2,1,0:T(8,128)S(1)} collective-permute-done((f32[30,24,128]{2,1,0:T(8,128)S(1)}, f32[30,24,128]{2,1,0:T(8,128)S(1)}, u32[]{:S(2)}, u32[]{:S(2)}) %collective-permute-start.3) | collective-permute-done | bytes 368672 | tf_op jit(solution)/shard_map/ppermute | solution.py:292
  31.3 0.0 copy-done
  31.3 0.0 copy-done.1
  31.3 0.0 copy-done.2
  31.3 0.0 copy-start.3
  31.3 0.7 %copy-done.3 = f32[30,24,128]{2,1,0:T(8,128)} copy-done((f32[30,24,128]{2,1,0:T(8,128)}, f32[30,24,128]{2,1,0:T(8,128)S(1)}, u32[]{:S(2)}) %copy-start.3) | copy-done | bytes 368664
  32.0 11.3 %shard_map.69 = (f32[19,16,512]{2,1,0:T(8,128)}, f32[16,512]{1,0:T(8,128)}) custom-call(bf16[4,19,16,512]{3,2,1,0:T(8,128)(2,1)} %pops_ref.3, f32[19,16,512]{2,1,0:T(8,128)} %seed_ref.3, s32[16,512]{1,0:T(8,128)} %solid_ref.3, s32[16,512]{1,0:T(8,128)} %mask_ref.3, f32[16,512]{1,0:T(8,128)} %field_ref.3, f32[30,4,512]{2,1,0:T(4,128)} %copy-done, ...), custom_call_target="tpu_custom_call" | custom-call | tf_op jit(solution)/shard_map/pallas_call | solution.py:302
  (3 shorter events, 0.1 us)
Async XLA Ops:
  3.3 17.6 %copy-start.4 = (f32[30,16,128]{2,1,0:T(8,128)S(1)}, f32[30,16,128]{2,1,0:T(8,128)}, u32[]{:S(2)}) copy-start(f32[30,16,128]{2,1,0:T(8,128)} %get-tuple-element.9) | copy-start | bytes 737284
  3.3 9.7 %collective-permute-start = (f32[30,4,512]{2,1,0:T(4,128)}, f32[30,4,512]{2,1,0:T(4,128)S(1)}, u32[]{:S(2)}, u32[]{:S(2)}) collective-permute-start(f32[30,4,512]{2,1,0:T(4,128)} %get-tuple-element.6), channel_id=1, source_target_pairs={{0,224},{32,0},{64,32},{96,64},{128,96},{160,128},{192,160},{224,1... | collective-permute-start | bytes 737288 | tf_op jit(solution)/shard_map/ppermute | solution.py:287
  7.4 8.8 %collective-permute-start.1 = (f32[30,4,512]{2,1,0:T(4,128)}, f32[30,4,512]{2,1,0:T(4,128)S(1)}, u32[]{:S(2)}, u32[]{:S(2)}) collective-permute-start(f32[30,4,512]{2,1,0:T(4,128)} %get-tuple-element.7), channel_id=1, source_target_pairs={{0,32},{32,64},{64,96},{96,128},{128,160},{160,192},{192,224},{224... | collective-permute-start | bytes 737288 | tf_op jit(solution)/shard_map/ppermute | solution.py:288
  12.9 18.3 %copy-start = (f32[30,4,512]{2,1,0:T(4,128)}, f32[30,4,512]{2,1,0:T(4,128)S(1)}, u32[]{:S(2)}) copy-start(f32[30,4,512]{2,1,0:T(4,128)S(1)} %collective-permute-done.hxp) | copy-start | bytes 737284
  16.3 15.0 %copy-start.1 = (f32[30,4,512]{2,1,0:T(4,128)}, f32[30,4,512]{2,1,0:T(4,128)S(1)}, u32[]{:S(2)}) copy-start(f32[30,4,512]{2,1,0:T(4,128)S(1)} %collective-permute-done.1.hxm) | copy-start | bytes 737284
  17.4 8.6 %collective-permute-start.2 = (f32[30,24,128]{2,1,0:T(8,128)S(1)}, f32[30,24,128]{2,1,0:T(8,128)S(1)}, u32[]{:S(2)}, u32[]{:S(2)}) collective-permute-start(f32[30,24,128]{2,1,0:T(8,128)S(1)} %pad_maximum_fusion), channel_id=1, source_target_pairs={{0,31},{1,0},{2,1},{3,2},{4,3},{5,4},{6,5},{7,6},{8,7},{9,8},{10,9... | collective-permute-start | bytes 1105928 | tf_op jit(solution)/shard_map/ppermute | solution.py:291
  20.9 10.3 %collective-permute-start.3 = (f32[30,24,128]{2,1,0:T(8,128)S(1)}, f32[30,24,128]{2,1,0:T(8,128)S(1)}, u32[]{:S(2)}, u32[]{:S(2)}) collective-permute-start(f32[30,24,128]{2,1,0:T(8,128)S(1)} %pad_maximum_fusion.1), channel_id=1, source_target_pairs={{0,1},{1,2},{2,3},{3,4},{4,5},{5,6},{6,7},{7,8},{8,9},{9,10},{10,1... | collective-permute-start | bytes 1105928 | tf_op jit(solution)/shard_map/ppermute | solution.py:292
  25.9 5.4 %copy-start.2 = (f32[30,24,128]{2,1,0:T(8,128)}, f32[30,24,128]{2,1,0:T(8,128)S(1)}, u32[]{:S(2)}) copy-start(f32[30,24,128]{2,1,0:T(8,128)S(1)} %collective-permute-done.2.hyp) | copy-start | bytes 1105924
  31.3 0.7 %copy-start.3 = (f32[30,24,128]{2,1,0:T(8,128)}, f32[30,24,128]{2,1,0:T(8,128)S(1)}, u32[]{:S(2)}) copy-start(f32[30,24,128]{2,1,0:T(8,128)S(1)} %collective-permute-done.3.hym) | copy-start | bytes 1105924

commit v5 on v3

--- a/solution.py
+++ b/solution.py
@@ -164,12 +164,19 @@
     steps = pops_ref.shape[0]
     _, rows, flat = seed_ref.shape
     erows, eflat = a_ref.shape[1], a_ref.shape[2]
-    nfield = hxp.shape[0]
+    nfield = hyp.shape[0]
     mask_all = mask_ref[...].astype(jnp.float32)
     rate_own = OMEGA_BASE + OMEGA_SPAN * field_ref[...] * mask_all
-    halo = lambda k, scale=None: [
-        h[k] if scale is None else h[k] * scale for h in (hxp, hxm, hyp, hym, cp, cm)
-    ]
+    def halo(k, scale=None):
+        parts = [
+            hxp[DEPTH * k : DEPTH * (k + 1), :],
+            hxm[DEPTH * k : DEPTH * (k + 1), :],
+            hyp[k],
+            hym[k],
+            cp[2 * DEPTH * k : 2 * DEPTH * (k + 1), :],
+            cm[2 * DEPTH * k : 2 * DEPTH * (k + 1), :],
+        ]
+        return parts if scale is None else [p * scale for p in parts]
     _fill_ext(rate_ref, rate_own, *halo(nfield - 2), rows, flat)
     _fill_ext(solid_ext, solid_ref[...].astype(jnp.float32), *halo(nfield - 1), rows, flat)
     for i in range(19):
@@ -247,8 +254,8 @@
     fields += [lambda rs, ls, k=k: u_ref[k, rs, ls] for k in range(nu)]
     fields += [lambda rs, ls: rate[rs, ls], lambda rs, ls: solid[rs, ls]]
     for k, get in enumerate(fields):
-        x_lo[k] = get(slice(0, DEPTH), slice(0, flat))
-        x_hi[k] = get(slice(rows - DEPTH, rows), slice(0, flat))
+        x_lo[DEPTH * k : DEPTH * (k + 1), :] = get(slice(0, DEPTH), slice(0, flat))
+        x_hi[DEPTH * k : DEPTH * (k + 1), :] = get(slice(rows - DEPTH, rows), slice(0, flat))
         y_lo[k] = get(slice(0, rows), slice(0, yw))
         y_hi[k] = get(slice(0, rows), slice(flat - yw, flat))
 
@@ -258,7 +265,7 @@
     _, rows, flat = seed.shape
     nfield = 19 + 3 * (steps - 1) + 2
     yw = DEPTH * NZ
-    shapes = [(nfield, DEPTH, flat), (nfield, DEPTH, flat), (nfield, rows, yw), (nfield, rows, yw)]
+    shapes = [(nfield * DEPTH, flat), (nfield * DEPTH, flat), (nfield, rows, yw), (nfield, rows, yw)]
     args = [saved_pops, seed, solid, mask, field]
 
     def full(shape):
@@ -290,8 +297,11 @@
     hxm = lax.ppermute(x_hi, "gx", _shift(nx, 1))
     hyp = lax.ppermute(y_lo, "gy", _shift(ny, -1))
     hym = lax.ppermute(y_hi, "gy", _shift(ny, 1))
-    c_lo = jnp.concatenate([hxp[:, :, lo_l], hxm[:, :, lo_l]], axis=1)
-    c_hi = jnp.concatenate([hxp[:, :, hi_l], hxm[:, :, hi_l]], axis=1)
+    nfield = y_lo.shape[0]
+    xp3 = hxp.reshape(nfield, DEPTH, flat)
+    xm3 = hxm.reshape(nfield, DEPTH, flat)
+    c_lo = jnp.concatenate([xp3[:, :, lo_l], xm3[:, :, lo_l]], axis=1).reshape(-1, yw)
+    c_hi = jnp.concatenate([xp3[:, :, hi_l], xm3[:, :, hi_l]], axis=1).reshape(-1, yw)
     cp = lax.ppermute(c_lo, "gy", _shift(ny, -1))
     cm = lax.ppermute(c_hi, "gy", _shift(ny, 1))
     erows = rows + 2 * DEPTH

time: 39.7 us -> 39.8 us (level)
  transfers between devices with their start and end apart: 6 -> 6, of which waited for: 5 -> 5; matrix products, arithmetic and copies ran while one was open for 0% -> 1% of each run, Pallas kernels for 0% -> 0%
where the time goes in v5:
time: 39.8 us; the launch traced here: 39.7 us
  Pallas kernels  14 us (35%)
  starting transfers between devices  12.1 us (30%)
  waiting for transfers between devices  11.9 us (30%)
  local copies, waits for them, and re-layouts  0.86 us (2%)
  between operations  0.72 us (2%)
    pallas_call x1, Pallas kernels, body(): pl.pallas_call(_fused_kernel, grid=(1,), in_specs=[full(a.shape) for a in...  11.3 us
    ppermute x1, waiting for transfers between devices, body(): cm = lax.ppermute(c_hi, 'gy', _shift(ny, 1))  5.29 us
    ppermute x1, starting transfers between devices, body(): hyp = lax.ppermute(y_lo, 'gy', _shift(ny, -1))  4.37 us
    ppermute x1, starting transfers between devices, body(): hxp = lax.ppermute(x_lo, 'gx', _shift(nx, -1))  4.12 us
    ppermute x1, starting transfers between devices, body(): cp = lax.ppermute(c_lo, 'gy', _shift(ny, -1))  3.54 us
    ppermute x1, waiting for transfers between devices, body(): hxm = lax.ppermute(x_hi, 'gx', _shift(nx, 1))  3.2 us
    pallas_call x1, Pallas kernels, _messages(): pl.pallas_call(_prep_kernel, grid=(1,), in_specs=[full(a.shape) for a in...  2.69 us
    ppermute x1, waiting for transfers between devices, body(): cp = lax.ppermute(c_lo, 'gy', _shift(ny, -1))  1.43 us
  transfers between devices with their start and end apart: 6, of which 5 were waited for; matrix products, arithmetic and copies ran while one was open for 1% of the time, Pallas kernels for 0%

profile of v5, /device:TPU:0, one launch (start us, length us, event | category | flops | bytes accessed | tf_op | source)
XLA Modules:
  0.0 39.7 jit_solution(9802922045426680733)
XLA Ops:
  0.6 2.7 %shard_map.68 = (f32[120,512]{1,0:T(8,128)}, f32[120,512]{1,0:T(8,128)}, f32[30,16,128]{2,1,0:T(8,128)}, f32[30,16,128]{2,1,0:T(8,128)}) custom-call(bf16[4,19,16,512]{3,2,1,0:T(8,128)(2,1)} %pops_ref.3, f32[19,16,512]{2,1,0:T(8,128)} %seed_ref.3, s32[16,512]{1,0:T(8,128)} %solid_ref.3, s32[16,512]{1,0:T(8,128)} %mask_ref.3, f32[16,512]{1,0:T(8,128)} %field_ref.3), custom_call_target="tpu_custom_call" | custom-call | tf_op jit(solution)/shard_map/pallas_call | solution.py:275
  3.3 4.1 %collective-permute-start = (f32[120,512]{1,0:T(8,128)}, f32[120,512]{1,0:T(8,128)S(1)}, u32[]{:S(2)}, u32[]{:S(2)}) collective-permute-start(f32[120,512]{1,0:T(8,128)} %get-tuple-element.6), channel_id=1, source_target_pairs={{0,224},{32,0},{64,32},{96,64},{128,96},{160,128},{192,160},{224,1... | collective-permute-start | bytes 737288 | tf_op jit(solution)/shard_map/ppermute | solution.py:296
  7.4 0.0 collective-permute-start.1
  7.4 4.4 %collective-permute-start.2 = (f32[30,16,128]{2,1,0:T(8,128)}, f32[30,16,128]{2,1,0:T(8,128)S(1)}, u32[]{:S(2)}, u32[]{:S(2)}) collective-permute-start(f32[30,16,128]{2,1,0:T(8,128)} %get-tuple-element.8), channel_id=1, source_target_pairs={{0,31},{1,0},{2,1},{3,2},{4,3},{5,4},{6,5},{7,6},{8,7},{9,8},{10,9... | collective-permute-start | bytes 737288 | tf_op jit(solution)/shard_map/ppermute | solution.py:298
  11.8 0.0 collective-permute-start.3
  11.8 1.2 %collective-permute-done.hxp = f32[120,512]{1,0:T(8,128)S(1)} collective-permute-done((f32[120,512]{1,0:T(8,128)}, f32[120,512]{1,0:T(8,128)S(1)}, u32[]{:S(2)}, u32[]{:S(2)}) %collective-permute-start) | collective-permute-done | bytes 245792 | tf_op jit(solution)/shard_map/ppermute | solution.py:296
  13.0 0.1 reshape.16
  13.1 3.2 %collective-permute-done.1.hxm = f32[120,512]{1,0:T(8,128)S(1)} collective-permute-done((f32[120,512]{1,0:T(8,128)}, f32[120,512]{1,0:T(8,128)S(1)}, u32[]{:S(2)}, u32[]{:S(2)}) %collective-permute-start.1) | collective-permute-done | bytes 245792 | tf_op jit(solution)/shard_map/ppermute | solution.py:297
  16.3 0.1 reshape.17
  16.4 3.5 %collective-permute-start.4 = (f32[240,128]{1,0:T(8,128)S(1)}, f32[240,128]{1,0:T(8,128)S(1)}, u32[]{:S(2)}, u32[]{:S(2)}) collective-permute-start(f32[240,128]{1,0:T(8,128)S(1)} %maximum_bitcast_fusion), channel_id=1, source_target_pairs={{0,31},{1,0},{2,1},{3,2},{4,3},{5,4},{6,5},{7,6},{8,7},{9,8},{10,9... | collective-permute-start | bytes 368648 | tf_op jit(solution)/shard_map/ppermute | solution.py:305
  20.0 0.1 collective-permute-start.5
  20.1 0.0 collective-permute-done.2.hyp
  20.1 0.0 copy-start.2
  20.1 0.9 %collective-permute-done.3.hym = f32[30,16,128]{2,1,0:T(8,128)S(1)} collective-permute-done((f32[30,16,128]{2,1,0:T(8,128)}, f32[30,16,128]{2,1,0:T(8,128)S(1)}, u32[]{:S(2)}, u32[]{:S(2)}) %collective-permute-start.3) | collective-permute-done | bytes 245792 | tf_op jit(solution)/shard_map/ppermute | solution.py:299
  21.0 1.4 %collective-permute-done.4.cp = f32[240,128]{1,0:T(8,128)S(1)} collective-permute-done((f32[240,128]{1,0:T(8,128)S(1)}, f32[240,128]{1,0:T(8,128)S(1)}, u32[]{:S(2)}, u32[]{:S(2)}) %collective-permute-start.4) | collective-permute-done | bytes 122912 | tf_op jit(solution)/shard_map/ppermute | solution.py:305
  22.4 5.3 %collective-permute-done.5.cm = f32[240,128]{1,0:T(8,128)S(1)} collective-permute-done((f32[240,128]{1,0:T(8,128)S(1)}, f32[240,128]{1,0:T(8,128)S(1)}, u32[]{:S(2)}, u32[]{:S(2)}) %collective-permute-start.5) | collective-permute-done | bytes 122912 | tf_op jit(solution)/shard_map/ppermute | solution.py:306
  27.7 0.0 copy-done
  27.7 0.0 copy-done.1
  27.7 0.0 copy-done.2
  27.7 0.0 copy-done.3
  27.7 0.0 copy-done.4
  27.7 0.0 copy-start.5
  27.7 0.7 %copy-done.5 = f32[240,128]{1,0:T(8,128)} copy-done((f32[240,128]{1,0:T(8,128)}, f32[240,128]{1,0:T(8,128)S(1)}, u32[]{:S(2)}) %copy-start.5) | copy-done | bytes 122904
  28.4 11.3 %shard_map.69 = (f32[19,16,512]{2,1,0:T(8,128)}, f32[16,512]{1,0:T(8,128)}) custom-call(bf16[4,19,16,512]{3,2,1,0:T(8,128)(2,1)} %pops_ref.3, f32[19,16,512]{2,1,0:T(8,128)} %seed_ref.3, s32[16,512]{1,0:T(8,128)} %solid_ref.3, s32[16,512]{1,0:T(8,128)} %mask_ref.3, f32[16,512]{1,0:T(8,128)} %field_ref.3, f32[120,512]{1,0:T(8,128)} %copy-done, ...), custom_call_target="tpu_custom_call" | custom-call | tf_op jit(solution)/shard_map/pallas_call | solution.py:316
  (8 shorter events, 0.1 us)
Async XLA Ops:
  3.3 9.7 %collective-permute-start = (f32[120,512]{1,0:T(8,128)}, f32[120,512]{1,0:T(8,128)S(1)}, u32[]{:S(2)}, u32[]{:S(2)}) collective-permute-start(f32[120,512]{1,0:T(8,128)} %get-tuple-element.6), channel_id=1, source_target_pairs={{0,224},{32,0},{64,32},{96,64},{128,96},{160,128},{192,160},{224,1... | collective-permute-start | bytes 737288 | tf_op jit(solution)/shard_map/ppermute | solution.py:296
  7.4 8.8 %collective-permute-start.1 = (f32[120,512]{1,0:T(8,128)}, f32[120,512]{1,0:T(8,128)S(1)}, u32[]{:S(2)}, u32[]{:S(2)}) collective-permute-start(f32[120,512]{1,0:T(8,128)} %get-tuple-element.7), channel_id=1, source_target_pairs={{0,32},{32,64},{64,96},{96,128},{128,160},{160,192},{192,224},{224... | collective-permute-start | bytes 737288 | tf_op jit(solution)/shard_map/ppermute | solution.py:297
  7.4 12.6 %collective-permute-start.2 = (f32[30,16,128]{2,1,0:T(8,128)}, f32[30,16,128]{2,1,0:T(8,128)S(1)}, u32[]{:S(2)}, u32[]{:S(2)}) collective-permute-start(f32[30,16,128]{2,1,0:T(8,128)} %get-tuple-element.8), channel_id=1, source_target_pairs={{0,31},{1,0},{2,1},{3,2},{4,3},{5,4},{6,5},{7,6},{8,7},{9,8},{10,9... | collective-permute-start | bytes 737288 | tf_op jit(solution)/shard_map/ppermute | solution.py:298
  11.8 9.2 %collective-permute-start.3 = (f32[30,16,128]{2,1,0:T(8,128)}, f32[30,16,128]{2,1,0:T(8,128)S(1)}, u32[]{:S(2)}, u32[]{:S(2)}) collective-permute-start(f32[30,16,128]{2,1,0:T(8,128)} %get-tuple-element.9), channel_id=1, source_target_pairs={{0,1},{1,2},{2,3},{3,4},{4,5},{5,6},{6,7},{7,8},{8,9},{9,10},{10,1... | collective-permute-start | bytes 737288 | tf_op jit(solution)/shard_map/ppermute | solution.py:299
  13.0 14.7 %copy-start = (f32[120,512]{1,0:T(8,128)}, f32[120,512]{1,0:T(8,128)S(1)}, u32[]{:S(2)}) copy-start(f32[120,512]{1,0:T(8,128)S(1)} %collective-permute-done.hxp) | copy-start | bytes 737284
  16.3 11.4 %copy-start.1 = (f32[120,512]{1,0:T(8,128)}, f32[120,512]{1,0:T(8,128)S(1)}, u32[]{:S(2)}) copy-start(f32[120,512]{1,0:T(8,128)S(1)} %collective-permute-done.1.hxm) | copy-start | bytes 737284
  16.4 6.0 %collective-permute-start.4 = (f32[240,128]{1,0:T(8,128)S(1)}, f32[240,128]{1,0:T(8,128)S(1)}, u32[]{:S(2)}, u32[]{:S(2)}) collective-permute-start(f32[240,128]{1,0:T(8,128)S(1)} %maximum_bitcast_fusion), channel_id=1, source_target_pairs={{0,31},{1,0},{2,1},{3,2},{4,3},{5,4},{6,5},{7,6},{8,7},{9,8},{10,9... | collective-permute-start | bytes 368648 | tf_op jit(solution)/shard_map/ppermute | solution.py:305
  20.0 7.7 %collective-permute-start.5 = (f32[240,128]{1,0:T(8,128)S(1)}, f32[240,128]{1,0:T(8,128)S(1)}, u32[]{:S(2)}, u32[]{:S(2)}) collective-permute-start(f32[240,128]{1,0:T(8,128)S(1)} %maximum_bitcast_fusion.1), channel_id=1, source_target_pairs={{0,1},{1,2},{2,3},{3,4},{4,5},{5,6},{6,7},{7,8},{8,9},{9,10},{10,1... | collective-permute-start | bytes 368648 | tf_op jit(solution)/shard_map/ppermute | solution.py:306
  20.1 7.6 %copy-start.2 = (f32[30,16,128]{2,1,0:T(8,128)}, f32[30,16,128]{2,1,0:T(8,128)S(1)}, u32[]{:S(2)}) copy-start(f32[30,16,128]{2,1,0:T(8,128)S(1)} %collective-permute-done.2.hyp) | copy-start | bytes 737284
  21.0 6.7 %copy-start.3 = (f32[30,16,128]{2,1,0:T(8,128)}, f32[30,16,128]{2,1,0:T(8,128)S(1)}, u32[]{:S(2)}) copy-start(f32[30,16,128]{2,1,0:T(8,128)S(1)} %collective-permute-done.3.hym) | copy-start | bytes 737284
  22.4 5.3 %copy-start.4 = (f32[240,128]{1,0:T(8,128)}, f32[240,128]{1,0:T(8,128)S(1)}, u32[]{:S(2)}) copy-start(f32[240,128]{1,0:T(8,128)S(1)} %collective-permute-done.4.cp) | copy-start | bytes 368644
  27.7 0.7 %copy-start.5 = (f32[240,128]{1,0:T(8,128)}, f32[240,128]{1,0:T(8,128)S(1)}, u32[]{:S(2)}) copy-start(f32[240,128]{1,0:T(8,128)S(1)} %collective-permute-done.5.cm) | copy-start | bytes 368644

commit v6 on v5

--- a/solution.py
+++ b/solution.py
@@ -63,67 +63,71 @@
     return rho, [m / rho for m in mom]
 
 
+PAIRS = [(i, int(OPPOSITE[i])) for i in range(1, 19) if i < OPPOSITE[i]]
+
+
+def _dot_c(i, vec):
+    acc = None
+    for a in range(3):
+        c = int(VELOCITIES[i, a])
+        if c == 0:
+            continue
+        if acc is None:
+            acc = vec[a] if c > 0 else -vec[a]
+        else:
+            acc = acc + vec[a] if c > 0 else acc - vec[a]
+    return acc
+
+
 def _vjp_core(u, g, rate, solid):
     usq = u[0] * u[0] + u[1] * u[1] + u[2] * u[2]
     base = 1.0 - 1.5 * usq
     fluid = solid == 0
-    one_minus = 1.0 - rate
-    esum = None
-    easum = None
+    gw = [g[i] * W32[i] for i in range(19)]
+    e = [rate * x for x in gw]
+    esum = e[0]
+    easum = e[0] * base
     mb = [None, None, None]
-    amp = []
-    gf = []
-    for i in range(19):
-        cvec = [int(c) for c in VELOCITIES[i]]
-        p = None
+    shape = []
+    for i, j in PAIRS:
+        p = _dot_c(i, u)
+        p3 = 3.0 * p
+        q = base + 1.5 * p * p3
+        sm = e[i] + e[j]
+        df = e[i] - e[j]
+        esum = esum + sm
+        easum = easum + (q * sm + p3 * df)
+        ep = 3.0 * df + 3.0 * p3 * sm
         for a in range(3):
-            if cvec[a] == 0:
+            c = int(VELOCITIES[i, a])
+            if c == 0:
                 continue
-            term = u[a] if cvec[a] > 0 else -u[a]
-            p = term if p is None else p + term
-        if p is None:
-            amp_i = base
-        else:
-            amp_i = base + (3.0 + 4.5 * p) * p
-        amp.append(amp_i)
-        gi = jnp.where(fluid, g[i], 0.0)
-        gf.append(gi)
-        e = (rate * W32[i]) * gi
-        esum = e if esum is None else esum + e
-        ea = e * amp_i
-        easum = ea if easum is None else easum + ea
-        if p is not None:
-            ep = e * (3.0 + 9.0 * p)
-            for a in range(3):
-                if cvec[a] == 0:
-                    continue
-                if mb[a] is None:
-                    mb[a] = ep if cvec[a] > 0 else -ep
-                else:
-                    mb[a] = mb[a] + ep if cvec[a] > 0 else mb[a] - ep
+            if mb[a] is None:
+                mb[a] = ep if c > 0 else -ep
+            else:
+                mb[a] = mb[a] + ep if c > 0 else mb[a] - ep
+        shape.append((q, p3))
     mb = [mb[a] - 3.0 * u[a] * esum for a in range(3)]
     rhobar = easum - (mb[0] * u[0] + mb[1] * u[1] + mb[2] * u[2])
-    out = []
-    for i in range(19):
-        cvec = [int(c) for c in VELOCITIES[i]]
-        val = one_minus * gf[i] + rhobar
-        for a in range(3):
-            if cvec[a] > 0:
-                val = val + mb[a]
-            elif cvec[a] < 0:
-                val = val - mb[a]
-        out.append(jnp.where(fluid, val, g[int(OPPOSITE[i])]))
-    return out, amp, gf
+    one_minus = 1.0 - rate
+    out = [None] * 19
+    out[0] = jnp.where(fluid, one_minus * g[0] + rhobar, g[0])
+    for i, j in PAIRS:
+        k = _dot_c(i, mb)
+        out[i] = jnp.where(fluid, one_minus * g[i] + (rhobar + k), g[j])
+        out[j] = jnp.where(fluid, one_minus * g[j] + (rhobar - k), g[i])
+    return out, shape, gw
 
 
 def _collide_vjp(f, g, rate, solid):
     rho, u = _velocity(f)
-    out, amp, gf = _vjp_core(u, g, rate, solid)
-    rbar = None
-    for i in range(19):
-        feq = W32[i] * rho * amp[i]
-        t = gf[i] * (feq - f[i])
-        rbar = t if rbar is None else rbar + t
+    out, shape, gw = _vjp_core(u, g, rate, solid)
+    gwa = gw[0] * (1.0 - 1.5 * (u[0] * u[0] + u[1] * u[1] + u[2] * u[2]))
+    gf = g[0] * f[0]
+    for (i, j), (q, p3) in zip(PAIRS, shape):
+        gwa = gwa + (q * (gw[i] + gw[j]) + p3 * (gw[i] - gw[j]))
+        gf = gf + (g[i] * f[i] + g[j] * f[j])
+    rbar = rho * gwa - gf
     return out, rbar
 
 

time: 39.8 us -> 39.3 us (0.987)
  Pallas kernels: 14 us -> 13.5 us
    pallas_call x1, Pallas kernels: 11.3 us -> 10.8 us  [body(): pl.pallas_call(_fused_kernel, grid=(1,), in_specs=[full(a.shape) for a in...]
where the time goes in v6:
time: 39.3 us; the launch traced here: 39.2 us
  Pallas kernels  13.5 us (34%)
  starting transfers between devices  12.1 us (31%)
  waiting for transfers between devices  11.9 us (30%)
  local copies, waits for them, and re-layouts  0.86 us (2%)
  between operations  0.72 us (2%)
    pallas_call x1, Pallas kernels, body(): pl.pallas_call(_fused_kernel, grid=(1,), in_specs=[full(a.shape) for a in...  10.8 us
    ppermute x1, waiting for transfers between devices, body(): cm = lax.ppermute(c_hi, 'gy', _shift(ny, 1))  5.29 us
    ppermute x1, starting transfers between devices, body(): hyp = lax.ppermute(y_lo, 'gy', _shift(ny, -1))  4.37 us
    ppermute x1, starting transfers between devices, body(): hxp = lax.ppermute(x_lo, 'gx', _shift(nx, -1))  4.12 us
    ppermute x1, starting transfers between devices, body(): cp = lax.ppermute(c_lo, 'gy', _shift(ny, -1))  3.54 us
    ppermute x1, waiting for transfers between devices, body(): hxm = lax.ppermute(x_hi, 'gx', _shift(nx, 1))  3.2 us
    pallas_call x1, Pallas kernels, _messages(): pl.pallas_call(_prep_kernel, grid=(1,), in_specs=[full(a.shape) for a in...  2.69 us
    ppermute x1, waiting for transfers between devices, body(): cp = lax.ppermute(c_lo, 'gy', _shift(ny, -1))  1.43 us
  transfers between devices with their start and end apart: 6, of which 5 were waited for; matrix products, arithmetic and copies ran while one was open for 1% of the time, Pallas kernels for 0%

profile of v6, /device:TPU:0, one launch (start us, length us, event | category | flops | bytes accessed | tf_op | source)
XLA Modules:
  0.0 39.2 jit_solution(15587668447201084850)
XLA Ops:
  0.6 2.7 %shard_map.68 = (f32[120,512]{1,0:T(8,128)}, f32[120,512]{1,0:T(8,128)}, f32[30,16,128]{2,1,0:T(8,128)}, f32[30,16,128]{2,1,0:T(8,128)}) custom-call(bf16[4,19,16,512]{3,2,1,0:T(8,128)(2,1)} %pops_ref.3, f32[19,16,512]{2,1,0:T(8,128)} %seed_ref.3, s32[16,512]{1,0:T(8,128)} %solid_ref.3, s32[16,512]{1,0:T(8,128)} %mask_ref.3, f32[16,512]{1,0:T(8,128)} %field_ref.3), custom_call_target="tpu_custom_call" | custom-call | tf_op jit(solution)/shard_map/pallas_call | solution.py:279
  3.3 4.1 %collective-permute-start = (f32[120,512]{1,0:T(8,128)}, f32[120,512]{1,0:T(8,128)S(1)}, u32[]{:S(2)}, u32[]{:S(2)}) collective-permute-start(f32[120,512]{1,0:T(8,128)} %get-tuple-element.6), channel_id=1, source_target_pairs={{0,224},{32,0},{64,32},{96,64},{128,96},{160,128},{192,160},{224,1... | collective-permute-start | bytes 737288 | tf_op jit(solution)/shard_map/ppermute | solution.py:300
  7.4 0.0 collective-permute-start.1
  7.4 4.4 %collective-permute-start.2 = (f32[30,16,128]{2,1,0:T(8,128)}, f32[30,16,128]{2,1,0:T(8,128)S(1)}, u32[]{:S(2)}, u32[]{:S(2)}) collective-permute-start(f32[30,16,128]{2,1,0:T(8,128)} %get-tuple-element.8), channel_id=1, source_target_pairs={{0,31},{1,0},{2,1},{3,2},{4,3},{5,4},{6,5},{7,6},{8,7},{9,8},{10,9... | collective-permute-start | bytes 737288 | tf_op jit(solution)/shard_map/ppermute | solution.py:302
  11.8 0.0 collective-permute-start.3
  11.8 1.2 %collective-permute-done.hxp = f32[120,512]{1,0:T(8,128)S(1)} collective-permute-done((f32[120,512]{1,0:T(8,128)}, f32[120,512]{1,0:T(8,128)S(1)}, u32[]{:S(2)}, u32[]{:S(2)}) %collective-permute-start) | collective-permute-done | bytes 245792 | tf_op jit(solution)/shard_map/ppermute | solution.py:300
  13.0 0.1 reshape.16
  13.1 3.2 %collective-permute-done.1.hxm = f32[120,512]{1,0:T(8,128)S(1)} collective-permute-done((f32[120,512]{1,0:T(8,128)}, f32[120,512]{1,0:T(8,128)S(1)}, u32[]{:S(2)}, u32[]{:S(2)}) %collective-permute-start.1) | collective-permute-done | bytes 245792 | tf_op jit(solution)/shard_map/ppermute | solution.py:301
  16.3 0.1 reshape.17
  16.4 3.5 %collective-permute-start.4 = (f32[240,128]{1,0:T(8,128)S(1)}, f32[240,128]{1,0:T(8,128)S(1)}, u32[]{:S(2)}, u32[]{:S(2)}) collective-permute-start(f32[240,128]{1,0:T(8,128)S(1)} %maximum_bitcast_fusion), channel_id=1, source_target_pairs={{0,31},{1,0},{2,1},{3,2},{4,3},{5,4},{6,5},{7,6},{8,7},{9,8},{10,9... | collective-permute-start | bytes 368648 | tf_op jit(solution)/shard_map/ppermute | solution.py:309
  20.0 0.1 collective-permute-start.5
  20.1 0.0 collective-permute-done.2.hyp
  20.1 0.0 copy-start.2
  20.1 0.9 %collective-permute-done.3.hym = f32[30,16,128]{2,1,0:T(8,128)S(1)} collective-permute-done((f32[30,16,128]{2,1,0:T(8,128)}, f32[30,16,128]{2,1,0:T(8,128)S(1)}, u32[]{:S(2)}, u32[]{:S(2)}) %collective-permute-start.3) | collective-permute-done | bytes 245792 | tf_op jit(solution)/shard_map/ppermute | solution.py:303
  21.0 1.4 %collective-permute-done.4.cp = f32[240,128]{1,0:T(8,128)S(1)} collective-permute-done((f32[240,128]{1,0:T(8,128)S(1)}, f32[240,128]{1,0:T(8,128)S(1)}, u32[]{:S(2)}, u32[]{:S(2)}) %collective-permute-start.4) | collective-permute-done | bytes 122912 | tf_op jit(solution)/shard_map/ppermute | solution.py:309
  22.4 5.3 %collective-permute-done.5.cm = f32[240,128]{1,0:T(8,128)S(1)} collective-permute-done((f32[240,128]{1,0:T(8,128)S(1)}, f32[240,128]{1,0:T(8,128)S(1)}, u32[]{:S(2)}, u32[]{:S(2)}) %collective-permute-start.5) | collective-permute-done | bytes 122912 | tf_op jit(solution)/shard_map/ppermute | solution.py:310
  27.7 0.0 copy-done
  27.7 0.0 copy-done.1
  27.7 0.0 copy-done.2
  27.7 0.0 copy-done.3
  27.7 0.0 copy-done.4
  27.7 0.0 copy-start.5
  27.7 0.7 %copy-done.5 = f32[240,128]{1,0:T(8,128)} copy-done((f32[240,128]{1,0:T(8,128)}, f32[240,128]{1,0:T(8,128)S(1)}, u32[]{:S(2)}) %copy-start.5) | copy-done | bytes 122904
  28.4 10.8 %shard_map.69 = (f32[19,16,512]{2,1,0:T(8,128)}, f32[16,512]{1,0:T(8,128)}) custom-call(bf16[4,19,16,512]{3,2,1,0:T(8,128)(2,1)} %pops_ref.3, f32[19,16,512]{2,1,0:T(8,128)} %seed_ref.3, s32[16,512]{1,0:T(8,128)} %solid_ref.3, s32[16,512]{1,0:T(8,128)} %mask_ref.3, f32[16,512]{1,0:T(8,128)} %field_ref.3, f32[120,512]{1,0:T(8,128)} %copy-done, ...), custom_call_target="tpu_custom_call" | custom-call | tf_op jit(solution)/shard_map/pallas_call | solution.py:320
  (8 shorter events, 0.1 us)
Async XLA Ops:
  3.3 9.7 %collective-permute-start = (f32[120,512]{1,0:T(8,128)}, f32[120,512]{1,0:T(8,128)S(1)}, u32[]{:S(2)}, u32[]{:S(2)}) collective-permute-start(f32[120,512]{1,0:T(8,128)} %get-tuple-element.6), channel_id=1, source_target_pairs={{0,224},{32,0},{64,32},{96,64},{128,96},{160,128},{192,160},{224,1... | collective-permute-start | bytes 737288 | tf_op jit(solution)/shard_map/ppermute | solution.py:300
  7.4 8.8 %collective-permute-start.1 = (f32[120,512]{1,0:T(8,128)}, f32[120,512]{1,0:T(8,128)S(1)}, u32[]{:S(2)}, u32[]{:S(2)}) collective-permute-start(f32[120,512]{1,0:T(8,128)} %get-tuple-element.7), channel_id=1, source_target_pairs={{0,32},{32,64},{64,96},{96,128},{128,160},{160,192},{192,224},{224... | collective-permute-start | bytes 737288 | tf_op jit(solution)/shard_map/ppermute | solution.py:301
  7.4 12.6 %collective-permute-start.2 = (f32[30,16,128]{2,1,0:T(8,128)}, f32[30,16,128]{2,1,0:T(8,128)S(1)}, u32[]{:S(2)}, u32[]{:S(2)}) collective-permute-start(f32[30,16,128]{2,1,0:T(8,128)} %get-tuple-element.8), channel_id=1, source_target_pairs={{0,31},{1,0},{2,1},{3,2},{4,3},{5,4},{6,5},{7,6},{8,7},{9,8},{10,9... | collective-permute-start | bytes 737288 | tf_op jit(solution)/shard_map/ppermute | solution.py:302
  11.8 9.2 %collective-permute-start.3 = (f32[30,16,128]{2,1,0:T(8,128)}, f32[30,16,128]{2,1,0:T(8,128)S(1)}, u32[]{:S(2)}, u32[]{:S(2)}) collective-permute-start(f32[30,16,128]{2,1,0:T(8,128)} %get-tuple-element.9), channel_id=1, source_target_pairs={{0,1},{1,2},{2,3},{3,4},{4,5},{5,6},{6,7},{7,8},{8,9},{9,10},{10,1... | collective-permute-start | bytes 737288 | tf_op jit(solution)/shard_map/ppermute | solution.py:303
  13.0 14.7 %copy-start = (f32[120,512]{1,0:T(8,128)}, f32[120,512]{1,0:T(8,128)S(1)}, u32[]{:S(2)}) copy-start(f32[120,512]{1,0:T(8,128)S(1)} %collective-permute-done.hxp) | copy-start | bytes 737284
  16.3 11.4 %copy-start.1 = (f32[120,512]{1,0:T(8,128)}, f32[120,512]{1,0:T(8,128)S(1)}, u32[]{:S(2)}) copy-start(f32[120,512]{1,0:T(8,128)S(1)} %collective-permute-done.1.hxm) | copy-start | bytes 737284
  16.4 6.0 %collective-permute-start.4 = (f32[240,128]{1,0:T(8,128)S(1)}, f32[240,128]{1,0:T(8,128)S(1)}, u32[]{:S(2)}, u32[]{:S(2)}) collective-permute-start(f32[240,128]{1,0:T(8,128)S(1)} %maximum_bitcast_fusion), channel_id=1, source_target_pairs={{0,31},{1,0},{2,1},{3,2},{4,3},{5,4},{6,5},{7,6},{8,7},{9,8},{10,9... | collective-permute-start | bytes 368648 | tf_op jit(solution)/shard_map/ppermute | solution.py:309
  20.0 7.7 %collective-permute-start.5 = (f32[240,128]{1,0:T(8,128)S(1)}, f32[240,128]{1,0:T(8,128)S(1)}, u32[]{:S(2)}, u32[]{:S(2)}) collective-permute-start(f32[240,128]{1,0:T(8,128)S(1)} %maximum_bitcast_fusion.1), channel_id=1, source_target_pairs={{0,1},{1,2},{2,3},{3,4},{4,5},{5,6},{6,7},{7,8},{8,9},{9,10},{10,1... | collective-permute-start | bytes 368648 | tf_op jit(solution)/shard_map/ppermute | solution.py:310
  20.1 7.6 %copy-start.2 = (f32[30,16,128]{2,1,0:T(8,128)}, f32[30,16,128]{2,1,0:T(8,128)S(1)}, u32[]{:S(2)}) copy-start(f32[30,16,128]{2,1,0:T(8,128)S(1)} %collective-permute-done.2.hyp) | copy-start | bytes 737284
  21.0 6.7 %copy-start.3 = (f32[30,16,128]{2,1,0:T(8,128)}, f32[30,16,128]{2,1,0:T(8,128)S(1)}, u32[]{:S(2)}) copy-start(f32[30,16,128]{2,1,0:T(8,128)S(1)} %collective-permute-done.3.hym) | copy-start | bytes 737284
  22.4 5.3 %copy-start.4 = (f32[240,128]{1,0:T(8,128)}, f32[240,128]{1,0:T(8,128)S(1)}, u32[]{:S(2)}) copy-start(f32[240,128]{1,0:T(8,128)S(1)} %collective-permute-done.4.cp) | copy-start | bytes 368644
  27.7 0.7 %copy-start.5 = (f32[240,128]{1,0:T(8,128)}, f32[240,128]{1,0:T(8,128)S(1)}, u32[]{:S(2)}) copy-start(f32[240,128]{1,0:T(8,128)S(1)} %collective-permute-done.5.cm) | copy-start | bytes 368644

commit v7 on v6

--- a/solution.py
+++ b/solution.py
@@ -142,12 +142,14 @@
         v = a_ref[i]
         if cx != 0:
             v = pltpu.roll(v, (rows - cx) % rows, 0)
-        if cy != 0:
-            v = pltpu.roll(v, (flat - cy * NZ) % flat, 1)
-        if cz == 1:
-            v = jnp.where(zl == NZ - 1, pltpu.roll(v, NZ - 1, 1), pltpu.roll(v, flat - 1, 1))
-        elif cz == -1:
-            v = jnp.where(zl == 0, pltpu.roll(v, flat - NZ + 1, 1), pltpu.roll(v, 1, 1))
+        main = -(cy * NZ + cz) % flat
+        if cz == 0:
+            if main:
+                v = pltpu.roll(v, main, 1)
+        else:
+            wrap = -(cy * NZ + cz - cz * NZ) % flat
+            edge = NZ - 1 if cz == 1 else 0
+            v = jnp.where(zl == edge, pltpu.roll(v, wrap, 1), pltpu.roll(v, main, 1))
         p_ref[i] = v
 
 

time: 39.3 us -> 38.1 us (0.969)
  Pallas kernels: 13.5 us -> 12.3 us
    pallas_call x1, Pallas kernels: 10.8 us -> 9.6 us  [body(): pl.pallas_call(_fused_kernel, grid=(1,), in_specs=[full(a.shape) for a in...]
where the time goes in v7:
time: 38.1 us; the launch traced here: 38 us
  Pallas kernels  12.3 us (32%)
  starting transfers between devices  12.1 us (32%)
  waiting for transfers between devices  11.9 us (31%)
  local copies, waits for them, and re-layouts  0.86 us (2%)
  between operations  0.72 us (2%)
    pallas_call x1, Pallas kernels, body(): pl.pallas_call(_fused_kernel, grid=(1,), in_specs=[full(a.shape) for a in...  9.6 us
    ppermute x1, waiting for transfers between devices, body(): cm = lax.ppermute(c_hi, 'gy', _shift(ny, 1))  5.29 us
    ppermute x1, starting transfers between devices, body(): hyp = lax.ppermute(y_lo, 'gy', _shift(ny, -1))  4.37 us
    ppermute x1, starting transfers between devices, body(): hxp = lax.ppermute(x_lo, 'gx', _shift(nx, -1))  4.12 us
    ppermute x1, starting transfers between devices, body(): cp = lax.ppermute(c_lo, 'gy', _shift(ny, -1))  3.54 us
    ppermute x1, waiting for transfers between devices, body(): hxm = lax.ppermute(x_hi, 'gx', _shift(nx, 1))  3.2 us
    pallas_call x1, Pallas kernels, _messages(): pl.pallas_call(_prep_kernel, grid=(1,), in_specs=[full(a.shape) for a in...  2.69 us
    ppermute x1, waiting for transfers between devices, body(): cp = lax.ppermute(c_lo, 'gy', _shift(ny, -1))  1.43 us
  transfers between devices with their start and end apart: 6, of which 5 were waited for; matrix products, arithmetic and copies ran while one was open for 1% of the time, Pallas kernels for 0%

profile of v7, /device:TPU:0, one launch (start us, length us, event | category | flops | bytes accessed | tf_op | source)
XLA Modules:
  0.0 38.0 jit_solution(11855587292136916611)
XLA Ops:
  0.6 2.7 %shard_map.68 = (f32[120,512]{1,0:T(8,128)}, f32[120,512]{1,0:T(8,128)}, f32[30,16,128]{2,1,0:T(8,128)}, f32[30,16,128]{2,1,0:T(8,128)}) custom-call(bf16[4,19,16,512]{3,2,1,0:T(8,128)(2,1)} %pops_ref.3, f32[19,16,512]{2,1,0:T(8,128)} %seed_ref.3, s32[16,512]{1,0:T(8,128)} %solid_ref.3, s32[16,512]{1,0:T(8,128)} %mask_ref.3, f32[16,512]{1,0:T(8,128)} %field_ref.3), custom_call_target="tpu_custom_call" | custom-call | tf_op jit(solution)/shard_map/pallas_call | solution.py:281
  3.3 4.1 %collective-permute-start = (f32[120,512]{1,0:T(8,128)}, f32[120,512]{1,0:T(8,128)S(1)}, u32[]{:S(2)}, u32[]{:S(2)}) collective-permute-start(f32[120,512]{1,0:T(8,128)} %get-tuple-element.6), channel_id=1, source_target_pairs={{0,224},{32,0},{64,32},{96,64},{128,96},{160,128},{192,160},{224,1... | collective-permute-start | bytes 737288 | tf_op jit(solution)/shard_map/ppermute | solution.py:302
  7.4 0.0 collective-permute-start.1
  7.4 4.4 %collective-permute-start.2 = (f32[30,16,128]{2,1,0:T(8,128)}, f32[30,16,128]{2,1,0:T(8,128)S(1)}, u32[]{:S(2)}, u32[]{:S(2)}) collective-permute-start(f32[30,16,128]{2,1,0:T(8,128)} %get-tuple-element.8), channel_id=1, source_target_pairs={{0,31},{1,0},{2,1},{3,2},{4,3},{5,4},{6,5},{7,6},{8,7},{9,8},{10,9... | collective-permute-start | bytes 737288 | tf_op jit(solution)/shard_map/ppermute | solution.py:304
  11.8 0.0 collective-permute-start.3
  11.8 1.2 %collective-permute-done.hxp = f32[120,512]{1,0:T(8,128)S(1)} collective-permute-done((f32[120,512]{1,0:T(8,128)}, f32[120,512]{1,0:T(8,128)S(1)}, u32[]{:S(2)}, u32[]{:S(2)}) %collective-permute-start) | collective-permute-done | bytes 245792 | tf_op jit(solution)/shard_map/ppermute | solution.py:302
  13.0 0.1 reshape.16
  13.1 3.2 %collective-permute-done.1.hxm = f32[120,512]{1,0:T(8,128)S(1)} collective-permute-done((f32[120,512]{1,0:T(8,128)}, f32[120,512]{1,0:T(8,128)S(1)}, u32[]{:S(2)}, u32[]{:S(2)}) %collective-permute-start.1) | collective-permute-done | bytes 245792 | tf_op jit(solution)/shard_map/ppermute | solution.py:303
  16.3 0.1 reshape.17
  16.4 3.5 %collective-permute-start.4 = (f32[240,128]{1,0:T(8,128)S(1)}, f32[240,128]{1,0:T(8,128)S(1)}, u32[]{:S(2)}, u32[]{:S(2)}) collective-permute-start(f32[240,128]{1,0:T(8,128)S(1)} %maximum_bitcast_fusion), channel_id=1, source_target_pairs={{0,31},{1,0},{2,1},{3,2},{4,3},{5,4},{6,5},{7,6},{8,7},{9,8},{10,9... | collective-permute-start | bytes 368648 | tf_op jit(solution)/shard_map/ppermute | solution.py:311
  20.0 0.1 collective-permute-start.5
  20.1 0.0 collective-permute-done.2.hyp
  20.1 0.0 copy-start.2
  20.1 0.9 %collective-permute-done.3.hym = f32[30,16,128]{2,1,0:T(8,128)S(1)} collective-permute-done((f32[30,16,128]{2,1,0:T(8,128)}, f32[30,16,128]{2,1,0:T(8,128)S(1)}, u32[]{:S(2)}, u32[]{:S(2)}) %collective-permute-start.3) | collective-permute-done | bytes 245792 | tf_op jit(solution)/shard_map/ppermute | solution.py:305
  21.0 1.4 %collective-permute-done.4.cp = f32[240,128]{1,0:T(8,128)S(1)} collective-permute-done((f32[240,128]{1,0:T(8,128)S(1)}, f32[240,128]{1,0:T(8,128)S(1)}, u32[]{:S(2)}, u32[]{:S(2)}) %collective-permute-start.4) | collective-permute-done | bytes 122912 | tf_op jit(solution)/shard_map/ppermute | solution.py:311
  22.4 5.3 %collective-permute-done.5.cm = f32[240,128]{1,0:T(8,128)S(1)} collective-permute-done((f32[240,128]{1,0:T(8,128)S(1)}, f32[240,128]{1,0:T(8,128)S(1)}, u32[]{:S(2)}, u32[]{:S(2)}) %collective-permute-start.5) | collective-permute-done | bytes 122912 | tf_op jit(solution)/shard_map/ppermute | solution.py:312
  27.7 0.0 copy-done
  27.7 0.0 copy-done.1
  27.7 0.0 copy-done.2
  27.7 0.0 copy-done.3
  27.7 0.0 copy-done.4
  27.7 0.0 copy-start.5
  27.7 0.7 %copy-done.5 = f32[240,128]{1,0:T(8,128)} copy-done((f32[240,128]{1,0:T(8,128)}, f32[240,128]{1,0:T(8,128)S(1)}, u32[]{:S(2)}) %copy-start.5) | copy-done | bytes 122904
  28.4 9.6 %shard_map.69 = (f32[19,16,512]{2,1,0:T(8,128)}, f32[16,512]{1,0:T(8,128)}) custom-call(bf16[4,19,16,512]{3,2,1,0:T(8,128)(2,1)} %pops_ref.3, f32[19,16,512]{2,1,0:T(8,128)} %seed_ref.3, s32[16,512]{1,0:T(8,128)} %solid_ref.3, s32[16,512]{1,0:T(8,128)} %mask_ref.3, f32[16,512]{1,0:T(8,128)} %field_ref.3, f32[120,512]{1,0:T(8,128)} %copy-done, ...), custom_call_target="tpu_custom_call" | custom-call | tf_op jit(solution)/shard_map/pallas_call | solution.py:322
  (8 shorter events, 0.1 us)
Async XLA Ops:
  3.3 9.7 %collective-permute-start = (f32[120,512]{1,0:T(8,128)}, f32[120,512]{1,0:T(8,128)S(1)}, u32[]{:S(2)}, u32[]{:S(2)}) collective-permute-start(f32[120,512]{1,0:T(8,128)} %get-tuple-element.6), channel_id=1, source_target_pairs={{0,224},{32,0},{64,32},{96,64},{128,96},{160,128},{192,160},{224,1... | collective-permute-start | bytes 737288 | tf_op jit(solution)/shard_map/ppermute | solution.py:302
  7.4 8.8 %collective-permute-start.1 = (f32[120,512]{1,0:T(8,128)}, f32[120,512]{1,0:T(8,128)S(1)}, u32[]{:S(2)}, u32[]{:S(2)}) collective-permute-start(f32[120,512]{1,0:T(8,128)} %get-tuple-element.7), channel_id=1, source_target_pairs={{0,32},{32,64},{64,96},{96,128},{128,160},{160,192},{192,224},{224... | collective-permute-start | bytes 737288 | tf_op jit(solution)/shard_map/ppermute | solution.py:303
  7.4 12.6 %collective-permute-start.2 = (f32[30,16,128]{2,1,0:T(8,128)}, f32[30,16,128]{2,1,0:T(8,128)S(1)}, u32[]{:S(2)}, u32[]{:S(2)}) collective-permute-start(f32[30,16,128]{2,1,0:T(8,128)} %get-tuple-element.8), channel_id=1, source_target_pairs={{0,31},{1,0},{2,1},{3,2},{4,3},{5,4},{6,5},{7,6},{8,7},{9,8},{10,9... | collective-permute-start | bytes 737288 | tf_op jit(solution)/shard_map/ppermute | solution.py:304
  11.8 9.2 %collective-permute-start.3 = (f32[30,16,128]{2,1,0:T(8,128)}, f32[30,16,128]{2,1,0:T(8,128)S(1)}, u32[]{:S(2)}, u32[]{:S(2)}) collective-permute-start(f32[30,16,128]{2,1,0:T(8,128)} %get-tuple-element.9), channel_id=1, source_target_pairs={{0,1},{1,2},{2,3},{3,4},{4,5},{5,6},{6,7},{7,8},{8,9},{9,10},{10,1... | collective-permute-start | bytes 737288 | tf_op jit(solution)/shard_map/ppermute | solution.py:305
  13.0 14.7 %copy-start = (f32[120,512]{1,0:T(8,128)}, f32[120,512]{1,0:T(8,128)S(1)}, u32[]{:S(2)}) copy-start(f32[120,512]{1,0:T(8,128)S(1)} %collective-permute-done.hxp) | copy-start | bytes 737284
  16.3 11.4 %copy-start.1 = (f32[120,512]{1,0:T(8,128)}, f32[120,512]{1,0:T(8,128)S(1)}, u32[]{:S(2)}) copy-start(f32[120,512]{1,0:T(8,128)S(1)} %collective-permute-done.1.hxm) | copy-start | bytes 737284
  16.4 6.0 %collective-permute-start.4 = (f32[240,128]{1,0:T(8,128)S(1)}, f32[240,128]{1,0:T(8,128)S(1)}, u32[]{:S(2)}, u32[]{:S(2)}) collective-permute-start(f32[240,128]{1,0:T(8,128)S(1)} %maximum_bitcast_fusion), channel_id=1, source_target_pairs={{0,31},{1,0},{2,1},{3,2},{4,3},{5,4},{6,5},{7,6},{8,7},{9,8},{10,9... | collective-permute-start | bytes 368648 | tf_op jit(solution)/shard_map/ppermute | solution.py:311
  20.0 7.7 %collective-permute-start.5 = (f32[240,128]{1,0:T(8,128)S(1)}, f32[240,128]{1,0:T(8,128)S(1)}, u32[]{:S(2)}, u32[]{:S(2)}) collective-permute-start(f32[240,128]{1,0:T(8,128)S(1)} %maximum_bitcast_fusion.1), channel_id=1, source_target_pairs={{0,1},{1,2},{2,3},{3,4},{4,5},{5,6},{6,7},{7,8},{8,9},{9,10},{10,1... | collective-permute-start | bytes 368648 | tf_op jit(solution)/shard_map/ppermute | solution.py:312
  20.1 7.6 %copy-start.2 = (f32[30,16,128]{2,1,0:T(8,128)}, f32[30,16,128]{2,1,0:T(8,128)S(1)}, u32[]{:S(2)}) copy-start(f32[30,16,128]{2,1,0:T(8,128)S(1)} %collective-permute-done.2.hyp) | copy-start | bytes 737284
  21.0 6.7 %copy-start.3 = (f32[30,16,128]{2,1,0:T(8,128)}, f32[30,16,128]{2,1,0:T(8,128)S(1)}, u32[]{:S(2)}) copy-start(f32[30,16,128]{2,1,0:T(8,128)S(1)} %collective-permute-done.3.hym) | copy-start | bytes 737284
  22.4 5.3 %copy-start.4 = (f32[240,128]{1,0:T(8,128)}, f32[240,128]{1,0:T(8,128)S(1)}, u32[]{:S(2)}) copy-start(f32[240,128]{1,0:T(8,128)S(1)} %collective-permute-done.4.cp) | copy-start | bytes 368644
  27.7 0.7 %copy-start.5 = (f32[240,128]{1,0:T(8,128)}, f32[240,128]{1,0:T(8,128)S(1)}, u32[]{:S(2)}) copy-start(f32[240,128]{1,0:T(8,128)S(1)} %collective-permute-done.5.cm) | copy-start | bytes 368644

commit v8 on v7

--- a/solution.py
+++ b/solution.py
@@ -242,28 +242,43 @@
             lax.fori_loop(0, n_halo, halo_body, 0)
 
 
-def _prep_kernel(pops_ref, seed_ref, solid_ref, mask_ref, field_ref, x_lo, x_hi, y_lo, y_hi, u_ref):
-    steps = pops_ref.shape[0]
+def _prep_kernel(pops_ref, seed_ref, solid_ref, mask_ref, field_ref, x_lo, x_hi, y_lo, y_hi):
+    nsteps = pl.num_programs(0)
     _, rows, flat = seed_ref.shape
     yw = DEPTH * NZ
-    for n, step in enumerate(reversed(range(1, steps))):
-        for t in range(flat // LANES):
+    tiles = flat // LANES
+    pid = pl.program_id(0)
+
+    def put(k, val, sl, t):
+        x_lo[DEPTH * k : DEPTH * (k + 1), sl] = val[0:DEPTH, :]
+        x_hi[DEPTH * k : DEPTH * (k + 1), sl] = val[rows - DEPTH : rows, :]
+        if t == 0:
+            y_lo[k] = val[:, 0:yw]
+        if t == tiles - 1:
+            y_hi[k] = val[:, LANES - yw : LANES]
+
+    @pl.when(pid == 0)
+    def _():
+        nfield = y_lo.shape[0]
+        for t in range(tiles):
             sl = slice(LANES * t, LANES * (t + 1))
-            f = [pops_ref[step, i, :, sl].astype(jnp.float32) * W32[i] for i in range(19)]
-            _, u = _velocity(f)
-            for a in range(3):
-                u_ref[3 * n + a, :, sl] = u[a]
-    nu = 3 * (steps - 1)
-    rate = OMEGA_BASE + OMEGA_SPAN * field_ref[...] * mask_ref[...].astype(jnp.float32)
-    solid = solid_ref[...].astype(jnp.float32)
-    fields = [lambda rs, ls, i=i: seed_ref[i, rs, ls] for i in range(19)]
-    fields += [lambda rs, ls, k=k: u_ref[k, rs, ls] for k in range(nu)]
-    fields += [lambda rs, ls: rate[rs, ls], lambda rs, ls: solid[rs, ls]]
-    for k, get in enumerate(fields):
-        x_lo[DEPTH * k : DEPTH * (k + 1), :] = get(slice(0, DEPTH), slice(0, flat))
-        x_hi[DEPTH * k : DEPTH * (k + 1), :] = get(slice(rows - DEPTH, rows), slice(0, flat))
-        y_lo[k] = get(slice(0, rows), slice(0, yw))
-        y_hi[k] = get(slice(0, rows), slice(flat - yw, flat))
+            mask = mask_ref[:, sl].astype(jnp.float32)
+            rate = OMEGA_BASE + OMEGA_SPAN * field_ref[:, sl] * mask
+            put(nfield - 2, rate, sl, t)
+            put(nfield - 1, solid_ref[:, sl].astype(jnp.float32), sl, t)
+            for i in range(19):
+                put(i, seed_ref[i, :, sl], sl, t)
+
+    for n in range((y_lo.shape[0] - 21) // 3):
+
+        @pl.when(pid == n)
+        def _(n=n):
+            for t in range(tiles):
+                sl = slice(LANES * t, LANES * (t + 1))
+                f = [pops_ref[0, i, :, sl].astype(jnp.float32) * W32[i] for i in range(19)]
+                _, u = _velocity(f)
+                for a in range(3):
+                    put(19 + 3 * n + a, u[a], sl, t)
 
 
 def _messages(saved_pops, seed, solid, mask, field):
@@ -276,15 +291,15 @@
 
     def full(shape):
         nd = len(shape)
-        return pl.BlockSpec(shape, lambda i, _n=nd: (0,) * _n)
-
+        return pl.BlockSpec(shape, lambda n, _n=nd: (0,) * _n)
+
+    pops_spec = pl.BlockSpec((1, 19, rows, flat), lambda n: (steps - 1 - n, 0, 0, 0))
     return pl.pallas_call(
         _prep_kernel,
-        grid=(1,),
-        in_specs=[full(a.shape) for a in args],
+        grid=(steps - 1,),
+        in_specs=[pops_spec] + [full(a.shape) for a in args[1:]],
         out_specs=[full(sh) for sh in shapes],
         out_shape=[jax.ShapeDtypeStruct(sh, jnp.float32) for sh in shapes],
-        scratch_shapes=[pltpu.VMEM((3 * (steps - 1), rows, flat), jnp.float32)],
     )(*args)
 
 

time: 38.1 us -> 38.9 us (1.021)
  Pallas kernels: 12.3 us -> 13 us
    pallas_call x1, Pallas kernels: 2.69 us -> 3.43 us  [_messages(): pl.pallas_call(_prep_kernel, grid=(steps - 1,), in_specs=[pops_spec] + [f...]
where the time goes in v8:
time: 38.9 us; the launch traced here: 38.7 us
  Pallas kernels  13 us (33%)
  starting transfers between devices  12.1 us (31%)
  waiting for transfers between devices  11.9 us (31%)
  local copies, waits for them, and re-layouts  0.86 us (2%)
  between operations  0.72 us (2%)
    pallas_call x1, Pallas kernels, body(): pl.pallas_call(_fused_kernel, grid=(1,), in_specs=[full(a.shape) for a in...  9.6 us
    ppermute x1, waiting for transfers between devices, body(): cm = lax.ppermute(c_hi, 'gy', _shift(ny, 1))  5.29 us
    ppermute x1, starting transfers between devices, body(): hyp = lax.ppermute(y_lo, 'gy', _shift(ny, -1))  4.37 us
    ppermute x1, starting transfers between devices, body(): hxp = lax.ppermute(x_lo, 'gx', _shift(nx, -1))  4.12 us
    ppermute x1, starting transfers between devices, body(): cp = lax.ppermute(c_lo, 'gy', _shift(ny, -1))  3.54 us
    pallas_call x1, Pallas kernels, _messages(): pl.pallas_call(_prep_kernel, grid=(steps - 1,), in_specs=[pops_spec] + [f...  3.43 us
    ppermute x1, waiting for transfers between devices, body(): hxm = lax.ppermute(x_hi, 'gx', _shift(nx, 1))  3.2 us
    ppermute x1, waiting for transfers between devices, body(): cp = lax.ppermute(c_lo, 'gy', _shift(ny, -1))  1.43 us
  transfers between devices with their start and end apart: 6, of which 5 were waited for; matrix products, arithmetic and copies ran while one was open for 1% of the time, Pallas kernels for 0%

profile of v8, /device:TPU:0, one launch (start us, length us, event | category | flops | bytes accessed | tf_op | source)
XLA Modules:
  0.0 38.7 jit_solution(3832832420657975228)
XLA Ops:
  0.6 3.4 %shard_map.68 = (f32[120,512]{1,0:T(8,128)}, f32[120,512]{1,0:T(8,128)}, f32[30,16,128]{2,1,0:T(8,128)}, f32[30,16,128]{2,1,0:T(8,128)}) custom-call(bf16[4,19,16,512]{3,2,1,0:T(8,128)(2,1)} %pops_ref.3, f32[19,16,512]{2,1,0:T(8,128)} %seed_ref.3, s32[16,512]{1,0:T(8,128)} %solid_ref.3, s32[16,512]{1,0:T(8,128)} %mask_ref.3, f32[16,512]{1,0:T(8,128)} %field_ref.3), custom_call_target="tpu_custom_call" | custom-call | tf_op jit(solution)/shard_map/pallas_call | solution.py:297
  4.1 4.1 %collective-permute-start = (f32[120,512]{1,0:T(8,128)}, f32[120,512]{1,0:T(8,128)S(1)}, u32[]{:S(2)}, u32[]{:S(2)}) collective-permute-start(f32[120,512]{1,0:T(8,128)} %get-tuple-element.6), channel_id=1, source_target_pairs={{0,224},{32,0},{64,32},{96,64},{128,96},{160,128},{192,160},{224,1... | collective-permute-start | bytes 737288 | tf_op jit(solution)/shard_map/ppermute | solution.py:317
  8.2 0.0 collective-permute-start.1
  8.2 4.4 %collective-permute-start.2 = (f32[30,16,128]{2,1,0:T(8,128)}, f32[30,16,128]{2,1,0:T(8,128)S(1)}, u32[]{:S(2)}, u32[]{:S(2)}) collective-permute-start(f32[30,16,128]{2,1,0:T(8,128)} %get-tuple-element.8), channel_id=1, source_target_pairs={{0,31},{1,0},{2,1},{3,2},{4,3},{5,4},{6,5},{7,6},{8,7},{9,8},{10,9... | collective-permute-start | bytes 737288 | tf_op jit(solution)/shard_map/ppermute | solution.py:319
  12.6 0.0 collective-permute-start.3
  12.6 1.2 %collective-permute-done.hxp = f32[120,512]{1,0:T(8,128)S(1)} collective-permute-done((f32[120,512]{1,0:T(8,128)}, f32[120,512]{1,0:T(8,128)S(1)}, u32[]{:S(2)}, u32[]{:S(2)}) %collective-permute-start) | collective-permute-done | bytes 245792 | tf_op jit(solution)/shard_map/ppermute | solution.py:317
  13.7 0.1 reshape.16
  13.8 3.2 %collective-permute-done.1.hxm = f32[120,512]{1,0:T(8,128)S(1)} collective-permute-done((f32[120,512]{1,0:T(8,128)}, f32[120,512]{1,0:T(8,128)S(1)}, u32[]{:S(2)}, u32[]{:S(2)}) %collective-permute-start.1) | collective-permute-done | bytes 245792 | tf_op jit(solution)/shard_map/ppermute | solution.py:318
  17.0 0.1 reshape.17
  17.2 3.5 %collective-permute-start.4 = (f32[240,128]{1,0:T(8,128)S(1)}, f32[240,128]{1,0:T(8,128)S(1)}, u32[]{:S(2)}, u32[]{:S(2)}) collective-permute-start(f32[240,128]{1,0:T(8,128)S(1)} %maximum_bitcast_fusion), channel_id=1, source_target_pairs={{0,31},{1,0},{2,1},{3,2},{4,3},{5,4},{6,5},{7,6},{8,7},{9,8},{10,9... | collective-permute-start | bytes 368648 | tf_op jit(solution)/shard_map/ppermute | solution.py:326
  20.7 0.1 collective-permute-start.5
  20.8 0.0 collective-permute-done.2.hyp
  20.8 0.0 copy-start.2
  20.8 0.9 %collective-permute-done.3.hym = f32[30,16,128]{2,1,0:T(8,128)S(1)} collective-permute-done((f32[30,16,128]{2,1,0:T(8,128)}, f32[30,16,128]{2,1,0:T(8,128)S(1)}, u32[]{:S(2)}, u32[]{:S(2)}) %collective-permute-start.3) | collective-permute-done | bytes 245792 | tf_op jit(solution)/shard_map/ppermute | solution.py:320
  21.7 1.4 %collective-permute-done.4.cp = f32[240,128]{1,0:T(8,128)S(1)} collective-permute-done((f32[240,128]{1,0:T(8,128)S(1)}, f32[240,128]{1,0:T(8,128)S(1)}, u32[]{:S(2)}, u32[]{:S(2)}) %collective-permute-start.4) | collective-permute-done | bytes 122912 | tf_op jit(solution)/shard_map/ppermute | solution.py:326
  23.1 5.3 %collective-permute-done.5.cm = f32[240,128]{1,0:T(8,128)S(1)} collective-permute-done((f32[240,128]{1,0:T(8,128)S(1)}, f32[240,128]{1,0:T(8,128)S(1)}, u32[]{:S(2)}, u32[]{:S(2)}) %collective-permute-start.5) | collective-permute-done | bytes 122912 | tf_op jit(solution)/shard_map/ppermute | solution.py:327
  28.4 0.0 copy-done
  28.4 0.0 copy-done.1
  28.4 0.0 copy-done.2
  28.4 0.0 copy-done.3
  28.5 0.0 copy-done.4
  28.5 0.0 copy-start.5
  28.5 0.7 %copy-done.5 = f32[240,128]{1,0:T(8,128)} copy-done((f32[240,128]{1,0:T(8,128)}, f32[240,128]{1,0:T(8,128)S(1)}, u32[]{:S(2)}) %copy-start.5) | copy-done | bytes 122904
  29.1 9.6 %shard_map.69 = (f32[19,16,512]{2,1,0:T(8,128)}, f32[16,512]{1,0:T(8,128)}) custom-call(bf16[4,19,16,512]{3,2,1,0:T(8,128)(2,1)} %pops_ref.3, f32[19,16,512]{2,1,0:T(8,128)} %seed_ref.3, s32[16,512]{1,0:T(8,128)} %solid_ref.3, s32[16,512]{1,0:T(8,128)} %mask_ref.3, f32[16,512]{1,0:T(8,128)} %field_ref.3, f32[120,512]{1,0:T(8,128)} %copy-done, ...), custom_call_target="tpu_custom_call" | custom-call | tf_op jit(solution)/shard_map/pallas_call | solution.py:337
  (8 shorter events, 0.1 us)
Async XLA Ops:
  4.1 9.7 %collective-permute-start = (f32[120,512]{1,0:T(8,128)}, f32[120,512]{1,0:T(8,128)S(1)}, u32[]{:S(2)}, u32[]{:S(2)}) collective-permute-start(f32[120,512]{1,0:T(8,128)} %get-tuple-element.6), channel_id=1, source_target_pairs={{0,224},{32,0},{64,32},{96,64},{128,96},{160,128},{192,160},{224,1... | collective-permute-start | bytes 737288 | tf_op jit(solution)/shard_map/ppermute | solution.py:317
  8.2 8.8 %collective-permute-start.1 = (f32[120,512]{1,0:T(8,128)}, f32[120,512]{1,0:T(8,128)S(1)}, u32[]{:S(2)}, u32[]{:S(2)}) collective-permute-start(f32[120,512]{1,0:T(8,128)} %get-tuple-element.7), channel_id=1, source_target_pairs={{0,32},{32,64},{64,96},{96,128},{128,160},{160,192},{192,224},{224... | collective-permute-start | bytes 737288 | tf_op jit(solution)/shard_map/ppermute | solution.py:318
  8.2 12.6 %collective-permute-start.2 = (f32[30,16,128]{2,1,0:T(8,128)}, f32[30,16,128]{2,1,0:T(8,128)S(1)}, u32[]{:S(2)}, u32[]{:S(2)}) collective-permute-start(f32[30,16,128]{2,1,0:T(8,128)} %get-tuple-element.8), channel_id=1, source_target_pairs={{0,31},{1,0},{2,1},{3,2},{4,3},{5,4},{6,5},{7,6},{8,7},{9,8},{10,9... | collective-permute-start | bytes 737288 | tf_op jit(solution)/shard_map/ppermute | solution.py:319
  12.6 9.2 %collective-permute-start.3 = (f32[30,16,128]{2,1,0:T(8,128)}, f32[30,16,128]{2,1,0:T(8,128)S(1)}, u32[]{:S(2)}, u32[]{:S(2)}) collective-permute-start(f32[30,16,128]{2,1,0:T(8,128)} %get-tuple-element.9), channel_id=1, source_target_pairs={{0,1},{1,2},{2,3},{3,4},{4,5},{5,6},{6,7},{7,8},{8,9},{9,10},{10,1... | collective-permute-start | bytes 737288 | tf_op jit(solution)/shard_map/ppermute | solution.py:320
  13.7 14.7 %copy-start = (f32[120,512]{1,0:T(8,128)}, f32[120,512]{1,0:T(8,128)S(1)}, u32[]{:S(2)}) copy-start(f32[120,512]{1,0:T(8,128)S(1)} %collective-permute-done.hxp) | copy-start | bytes 737284
  17.0 11.4 %copy-start.1 = (f32[120,512]{1,0:T(8,128)}, f32[120,512]{1,0:T(8,128)S(1)}, u32[]{:S(2)}) copy-start(f32[120,512]{1,0:T(8,128)S(1)} %collective-permute-done.1.hxm) | copy-start | bytes 737284
  17.2 6.0 %collective-permute-start.4 = (f32[240,128]{1,0:T(8,128)S(1)}, f32[240,128]{1,0:T(8,128)S(1)}, u32[]{:S(2)}, u32[]{:S(2)}) collective-permute-start(f32[240,128]{1,0:T(8,128)S(1)} %maximum_bitcast_fusion), channel_id=1, source_target_pairs={{0,31},{1,0},{2,1},{3,2},{4,3},{5,4},{6,5},{7,6},{8,7},{9,8},{10,9... | collective-permute-start | bytes 368648 | tf_op jit(solution)/shard_map/ppermute | solution.py:326
  20.7 7.7 %collective-permute-start.5 = (f32[240,128]{1,0:T(8,128)S(1)}, f32[240,128]{1,0:T(8,128)S(1)}, u32[]{:S(2)}, u32[]{:S(2)}) collective-permute-start(f32[240,128]{1,0:T(8,128)S(1)} %maximum_bitcast_fusion.1), channel_id=1, source_target_pairs={{0,1},{1,2},{2,3},{3,4},{4,5},{5,6},{6,7},{7,8},{8,9},{9,10},{10,1... | collective-permute-start | bytes 368648 | tf_op jit(solution)/shard_map/ppermute | solution.py:327
  20.8 7.6 %copy-start.2 = (f32[30,16,128]{2,1,0:T(8,128)}, f32[30,16,128]{2,1,0:T(8,128)S(1)}, u32[]{:S(2)}) copy-start(f32[30,16,128]{2,1,0:T(8,128)S(1)} %collective-permute-done.2.hyp) | copy-start | bytes 737284
  21.7 6.7 %copy-start.3 = (f32[30,16,128]{2,1,0:T(8,128)}, f32[30,16,128]{2,1,0:T(8,128)S(1)}, u32[]{:S(2)}) copy-start(f32[30,16,128]{2,1,0:T(8,128)S(1)} %collective-permute-done.3.hym) | copy-start | bytes 737284
  23.1 5.3 %copy-start.4 = (f32[240,128]{1,0:T(8,128)}, f32[240,128]{1,0:T(8,128)S(1)}, u32[]{:S(2)}) copy-start(f32[240,128]{1,0:T(8,128)S(1)} %collective-permute-done.4.cp) | copy-start | bytes 368644
  28.5 0.7 %copy-start.5 = (f32[240,128]{1,0:T(8,128)}, f32[240,128]{1,0:T(8,128)S(1)}, u32[]{:S(2)}) copy-start(f32[240,128]{1,0:T(8,128)S(1)} %collective-permute-done.5.cm) | copy-start | bytes 368644

commit v9 on v7

--- a/solution.py
+++ b/solution.py
@@ -228,7 +228,7 @@
             chunk(step, r0, l0, write_ref, True)
             return carry
 
-        lax.fori_loop(0, n_own, own_body, 0)
+        lax.fori_loop(0, n_own, own_body, 0, unroll=True)
         if not last:
 
             def halo_body(c, carry):
@@ -239,7 +239,7 @@
                 chunk(step, pl.multiple_of(r * 8, 8), pl.multiple_of(t * LANES, LANES), a_ref, False)
                 return carry
 
-            lax.fori_loop(0, n_halo, halo_body, 0)
+            lax.fori_loop(0, n_halo, halo_body, 0, unroll=True)
 
 
 def _prep_kernel(pops_ref, seed_ref, solid_ref, mask_ref, field_ref, x_lo, x_hi, y_lo, y_hi, u_ref):

time: 38.1 us -> 35.8 us (0.940)
  Pallas kernels: 12.3 us -> 9.97 us
    pallas_call x1, Pallas kernels: 9.6 us -> 7.28 us  [body(): pl.pallas_call(_fused_kernel, grid=(1,), in_specs=[full(a.shape) for a in...]
where the time goes in v9:
time: 35.8 us; the launch traced here: 35.7 us
  starting transfers between devices  12.1 us (34%)
  waiting for transfers between devices  11.9 us (33%)
  Pallas kernels  9.97 us (28%)
  local copies, waits for them, and re-layouts  0.86 us (2%)
  between operations  0.72 us (2%)
    pallas_call x1, Pallas kernels, body(): pl.pallas_call(_fused_kernel, grid=(1,), in_specs=[full(a.shape) for a in...  7.28 us
    ppermute x1, waiting for transfers between devices, body(): cm = lax.ppermute(c_hi, 'gy', _shift(ny, 1))  5.29 us
    ppermute x1, starting transfers between devices, body(): hyp = lax.ppermute(y_lo, 'gy', _shift(ny, -1))  4.37 us
    ppermute x1, starting transfers between devices, body(): hxp = lax.ppermute(x_lo, 'gx', _shift(nx, -1))  4.12 us
    ppermute x1, starting transfers between devices, body(): cp = lax.ppermute(c_lo, 'gy', _shift(ny, -1))  3.54 us
    ppermute x1, waiting for transfers between devices, body(): hxm = lax.ppermute(x_hi, 'gx', _shift(nx, 1))  3.2 us
    pallas_call x1, Pallas kernels, _messages(): pl.pallas_call(_prep_kernel, grid=(1,), in_specs=[full(a.shape) for a in...  2.69 us
    ppermute x1, waiting for transfers between devices, body(): cp = lax.ppermute(c_lo, 'gy', _shift(ny, -1))  1.43 us
  transfers between devices with their start and end apart: 6, of which 5 were waited for; matrix products, arithmetic and copies ran while one was open for 1% of the time, Pallas kernels for 0%

profile of v9, /device:TPU:0, one launch (start us, length us, event | category | flops | bytes accessed | tf_op | source)
XLA Modules:
  0.0 35.7 jit_solution(14476343250291464349)
XLA Ops:
  0.6 2.7 %shard_map.68 = (f32[120,512]{1,0:T(8,128)}, f32[120,512]{1,0:T(8,128)}, f32[30,16,128]{2,1,0:T(8,128)}, f32[30,16,128]{2,1,0:T(8,128)}) custom-call(bf16[4,19,16,512]{3,2,1,0:T(8,128)(2,1)} %pops_ref.3, f32[19,16,512]{2,1,0:T(8,128)} %seed_ref.3, s32[16,512]{1,0:T(8,128)} %solid_ref.3, s32[16,512]{1,0:T(8,128)} %mask_ref.3, f32[16,512]{1,0:T(8,128)} %field_ref.3), custom_call_target="tpu_custom_call" | custom-call | tf_op jit(solution)/shard_map/pallas_call | solution.py:281
  3.3 4.1 %collective-permute-start = (f32[120,512]{1,0:T(8,128)}, f32[120,512]{1,0:T(8,128)S(1)}, u32[]{:S(2)}, u32[]{:S(2)}) collective-permute-start(f32[120,512]{1,0:T(8,128)} %get-tuple-element.6), channel_id=1, source_target_pairs={{0,224},{32,0},{64,32},{96,64},{128,96},{160,128},{192,160},{224,1... | collective-permute-start | bytes 737288 | tf_op jit(solution)/shard_map/ppermute | solution.py:302
  7.4 0.0 collective-permute-start.1
  7.4 4.4 %collective-permute-start.2 = (f32[30,16,128]{2,1,0:T(8,128)}, f32[30,16,128]{2,1,0:T(8,128)S(1)}, u32[]{:S(2)}, u32[]{:S(2)}) collective-permute-start(f32[30,16,128]{2,1,0:T(8,128)} %get-tuple-element.8), channel_id=1, source_target_pairs={{0,31},{1,0},{2,1},{3,2},{4,3},{5,4},{6,5},{7,6},{8,7},{9,8},{10,9... | collective-permute-start | bytes 737288 | tf_op jit(solution)/shard_map/ppermute | solution.py:304
  11.8 0.0 collective-permute-start.3
  11.8 1.2 %collective-permute-done.hxp = f32[120,512]{1,0:T(8,128)S(1)} collective-permute-done((f32[120,512]{1,0:T(8,128)}, f32[120,512]{1,0:T(8,128)S(1)}, u32[]{:S(2)}, u32[]{:S(2)}) %collective-permute-start) | collective-permute-done | bytes 245792 | tf_op jit(solution)/shard_map/ppermute | solution.py:302
  13.0 0.1 reshape.16
  13.1 3.2 %collective-permute-done.1.hxm = f32[120,512]{1,0:T(8,128)S(1)} collective-permute-done((f32[120,512]{1,0:T(8,128)}, f32[120,512]{1,0:T(8,128)S(1)}, u32[]{:S(2)}, u32[]{:S(2)}) %collective-permute-start.1) | collective-permute-done | bytes 245792 | tf_op jit(solution)/shard_map/ppermute | solution.py:303
  16.3 0.1 reshape.17
  16.4 3.5 %collective-permute-start.4 = (f32[240,128]{1,0:T(8,128)S(1)}, f32[240,128]{1,0:T(8,128)S(1)}, u32[]{:S(2)}, u32[]{:S(2)}) collective-permute-start(f32[240,128]{1,0:T(8,128)S(1)} %maximum_bitcast_fusion), channel_id=1, source_target_pairs={{0,31},{1,0},{2,1},{3,2},{4,3},{5,4},{6,5},{7,6},{8,7},{9,8},{10,9... | collective-permute-start | bytes 368648 | tf_op jit(solution)/shard_map/ppermute | solution.py:311
  20.0 0.1 collective-permute-start.5
  20.1 0.0 collective-permute-done.2.hyp
  20.1 0.0 copy-start.2
  20.1 0.9 %collective-permute-done.3.hym = f32[30,16,128]{2,1,0:T(8,128)S(1)} collective-permute-done((f32[30,16,128]{2,1,0:T(8,128)}, f32[30,16,128]{2,1,0:T(8,128)S(1)}, u32[]{:S(2)}, u32[]{:S(2)}) %collective-permute-start.3) | collective-permute-done | bytes 245792 | tf_op jit(solution)/shard_map/ppermute | solution.py:305
  21.0 1.4 %collective-permute-done.4.cp = f32[240,128]{1,0:T(8,128)S(1)} collective-permute-done((f32[240,128]{1,0:T(8,128)S(1)}, f32[240,128]{1,0:T(8,128)S(1)}, u32[]{:S(2)}, u32[]{:S(2)}) %collective-permute-start.4) | collective-permute-done | bytes 122912 | tf_op jit(solution)/shard_map/ppermute | solution.py:311
  22.4 5.3 %collective-permute-done.5.cm = f32[240,128]{1,0:T(8,128)S(1)} collective-permute-done((f32[240,128]{1,0:T(8,128)S(1)}, f32[240,128]{1,0:T(8,128)S(1)}, u32[]{:S(2)}, u32[]{:S(2)}) %collective-permute-start.5) | collective-permute-done | bytes 122912 | tf_op jit(solution)/shard_map/ppermute | solution.py:312
  27.7 0.0 copy-done
  27.7 0.0 copy-done.1
  27.7 0.0 copy-done.2
  27.7 0.0 copy-done.3
  27.7 0.0 copy-done.4
  27.7 0.0 copy-start.5
  27.7 0.7 %copy-done.5 = f32[240,128]{1,0:T(8,128)} copy-done((f32[240,128]{1,0:T(8,128)}, f32[240,128]{1,0:T(8,128)S(1)}, u32[]{:S(2)}) %copy-start.5) | copy-done | bytes 122904
  28.4 7.3 %shard_map.69 = (f32[19,16,512]{2,1,0:T(8,128)}, f32[16,512]{1,0:T(8,128)}) custom-call(bf16[4,19,16,512]{3,2,1,0:T(8,128)(2,1)} %pops_ref.3, f32[19,16,512]{2,1,0:T(8,128)} %seed_ref.3, s32[16,512]{1,0:T(8,128)} %solid_ref.3, s32[16,512]{1,0:T(8,128)} %mask_ref.3, f32[16,512]{1,0:T(8,128)} %field_ref.3, f32[120,512]{1,0:T(8,128)} %copy-done, ...), custom_call_target="tpu_custom_call" | custom-call | tf_op jit(solution)/shard_map/pallas_call | solution.py:322
  (8 shorter events, 0.1 us)
Async XLA Ops:
  3.3 9.7 %collective-permute-start = (f32[120,512]{1,0:T(8,128)}, f32[120,512]{1,0:T(8,128)S(1)}, u32[]{:S(2)}, u32[]{:S(2)}) collective-permute-start(f32[120,512]{1,0:T(8,128)} %get-tuple-element.6), channel_id=1, source_target_pairs={{0,224},{32,0},{64,32},{96,64},{128,96},{160,128},{192,160},{224,1... | collective-permute-start | bytes 737288 | tf_op jit(solution)/shard_map/ppermute | solution.py:302
  7.4 8.8 %collective-permute-start.1 = (f32[120,512]{1,0:T(8,128)}, f32[120,512]{1,0:T(8,128)S(1)}, u32[]{:S(2)}, u32[]{:S(2)}) collective-permute-start(f32[120,512]{1,0:T(8,128)} %get-tuple-element.7), channel_id=1, source_target_pairs={{0,32},{32,64},{64,96},{96,128},{128,160},{160,192},{192,224},{224... | collective-permute-start | bytes 737288 | tf_op jit(solution)/shard_map/ppermute | solution.py:303
  7.4 12.6 %collective-permute-start.2 = (f32[30,16,128]{2,1,0:T(8,128)}, f32[30,16,128]{2,1,0:T(8,128)S(1)}, u32[]{:S(2)}, u32[]{:S(2)}) collective-permute-start(f32[30,16,128]{2,1,0:T(8,128)} %get-tuple-element.8), channel_id=1, source_target_pairs={{0,31},{1,0},{2,1},{3,2},{4,3},{5,4},{6,5},{7,6},{8,7},{9,8},{10,9... | collective-permute-start | bytes 737288 | tf_op jit(solution)/shard_map/ppermute | solution.py:304
  11.8 9.2 %collective-permute-start.3 = (f32[30,16,128]{2,1,0:T(8,128)}, f32[30,16,128]{2,1,0:T(8,128)S(1)}, u32[]{:S(2)}, u32[]{:S(2)}) collective-permute-start(f32[30,16,128]{2,1,0:T(8,128)} %get-tuple-element.9), channel_id=1, source_target_pairs={{0,1},{1,2},{2,3},{3,4},{4,5},{5,6},{6,7},{7,8},{8,9},{9,10},{10,1... | collective-permute-start | bytes 737288 | tf_op jit(solution)/shard_map/ppermute | solution.py:305
  13.0 14.7 %copy-start = (f32[120,512]{1,0:T(8,128)}, f32[120,512]{1,0:T(8,128)S(1)}, u32[]{:S(2)}) copy-start(f32[120,512]{1,0:T(8,128)S(1)} %collective-permute-done.hxp) | copy-start | bytes 737284
  16.3 11.4 %copy-start.1 = (f32[120,512]{1,0:T(8,128)}, f32[120,512]{1,0:T(8,128)S(1)}, u32[]{:S(2)}) copy-start(f32[120,512]{1,0:T(8,128)S(1)} %collective-permute-done.1.hxm) | copy-start | bytes 737284
  16.4 6.0 %collective-permute-start.4 = (f32[240,128]{1,0:T(8,128)S(1)}, f32[240,128]{1,0:T(8,128)S(1)}, u32[]{:S(2)}, u32[]{:S(2)}) collective-permute-start(f32[240,128]{1,0:T(8,128)S(1)} %maximum_bitcast_fusion), channel_id=1, source_target_pairs={{0,31},{1,0},{2,1},{3,2},{4,3},{5,4},{6,5},{7,6},{8,7},{9,8},{10,9... | collective-permute-start | bytes 368648 | tf_op jit(solution)/shard_map/ppermute | solution.py:311
  20.0 7.7 %collective-permute-start.5 = (f32[240,128]{1,0:T(8,128)S(1)}, f32[240,128]{1,0:T(8,128)S(1)}, u32[]{:S(2)}, u32[]{:S(2)}) collective-permute-start(f32[240,128]{1,0:T(8,128)S(1)} %maximum_bitcast_fusion.1), channel_id=1, source_target_pairs={{0,1},{1,2},{2,3},{3,4},{4,5},{5,6},{6,7},{7,8},{8,9},{9,10},{10,1... | collective-permute-start | bytes 368648 | tf_op jit(solution)/shard_map/ppermute | solution.py:312
  20.1 7.6 %copy-start.2 = (f32[30,16,128]{2,1,0:T(8,128)}, f32[30,16,128]{2,1,0:T(8,128)S(1)}, u32[]{:S(2)}) copy-start(f32[30,16,128]{2,1,0:T(8,128)S(1)} %collective-permute-done.2.hyp) | copy-start | bytes 737284
  21.0 6.7 %copy-start.3 = (f32[30,16,128]{2,1,0:T(8,128)}, f32[30,16,128]{2,1,0:T(8,128)S(1)}, u32[]{:S(2)}) copy-start(f32[30,16,128]{2,1,0:T(8,128)S(1)} %collective-permute-done.3.hym) | copy-start | bytes 737284
  22.4 5.3 %copy-start.4 = (f32[240,128]{1,0:T(8,128)}, f32[240,128]{1,0:T(8,128)S(1)}, u32[]{:S(2)}) copy-start(f32[240,128]{1,0:T(8,128)S(1)} %collective-permute-done.4.cp) | copy-start | bytes 368644
  27.7 0.7 %copy-start.5 = (f32[240,128]{1,0:T(8,128)}, f32[240,128]{1,0:T(8,128)S(1)}, u32[]{:S(2)}) copy-start(f32[240,128]{1,0:T(8,128)S(1)} %collective-permute-done.5.cm) | copy-start | bytes 368644

commit v10 on v9

--- a/solution.py
+++ b/solution.py
@@ -242,24 +242,39 @@
             lax.fori_loop(0, n_halo, halo_body, 0, unroll=True)
 
 
-def _prep_kernel(pops_ref, seed_ref, solid_ref, mask_ref, field_ref, x_lo, x_hi, y_lo, y_hi, u_ref):
-    steps = pops_ref.shape[0]
+def _prep_kernel(pops_hbm, seed_ref, solid_ref, mask_ref, field_ref, x_lo, x_hi, y_lo, y_hi, u_ref,
+                 pops_ref, sems):
+    steps = pops_hbm.shape[0]
     _, rows, flat = seed_ref.shape
     yw = DEPTH * NZ
+    copies = [
+        pltpu.make_async_copy(pops_hbm.at[step], pops_ref.at[step - 1], sems.at[step - 1])
+        for step in range(1, steps)
+    ]
+    for c in reversed(copies):
+        c.start()
+    rate = OMEGA_BASE + OMEGA_SPAN * field_ref[...] * mask_ref[...].astype(jnp.float32)
+    solid = solid_ref[...].astype(jnp.float32)
+    nu = 3 * (steps - 1)
+    fields = {i: (lambda rs, ls, i=i: seed_ref[i, rs, ls]) for i in range(19)}
+    fields[19 + nu] = lambda rs, ls: rate[rs, ls]
+    fields[20 + nu] = lambda rs, ls: solid[rs, ls]
+    _put_fields(fields, x_lo, x_hi, y_lo, y_hi, rows, flat)
     for n, step in enumerate(reversed(range(1, steps))):
+        copies[step - 1].wait()
         for t in range(flat // LANES):
             sl = slice(LANES * t, LANES * (t + 1))
-            f = [pops_ref[step, i, :, sl].astype(jnp.float32) * W32[i] for i in range(19)]
+            f = [pops_ref[step - 1, i, :, sl].astype(jnp.float32) * W32[i] for i in range(19)]
             _, u = _velocity(f)
             for a in range(3):
                 u_ref[3 * n + a, :, sl] = u[a]
-    nu = 3 * (steps - 1)
-    rate = OMEGA_BASE + OMEGA_SPAN * field_ref[...] * mask_ref[...].astype(jnp.float32)
-    solid = solid_ref[...].astype(jnp.float32)
-    fields = [lambda rs, ls, i=i: seed_ref[i, rs, ls] for i in range(19)]
-    fields += [lambda rs, ls, k=k: u_ref[k, rs, ls] for k in range(nu)]
-    fields += [lambda rs, ls: rate[rs, ls], lambda rs, ls: solid[rs, ls]]
-    for k, get in enumerate(fields):
+    fields = {19 + k: (lambda rs, ls, k=k: u_ref[k, rs, ls]) for k in range(nu)}
+    _put_fields(fields, x_lo, x_hi, y_lo, y_hi, rows, flat)
+
+
+def _put_fields(fields, x_lo, x_hi, y_lo, y_hi, rows, flat):
+    yw = DEPTH * NZ
+    for k, get in fields.items():
         x_lo[DEPTH * k : DEPTH * (k + 1), :] = get(slice(0, DEPTH), slice(0, flat))
         x_hi[DEPTH * k : DEPTH * (k + 1), :] = get(slice(rows - DEPTH, rows), slice(0, flat))
         y_lo[k] = get(slice(0, rows), slice(0, yw))
@@ -281,10 +296,14 @@
     return pl.pallas_call(
         _prep_kernel,
         grid=(1,),
-        in_specs=[full(a.shape) for a in args],
+        in_specs=[pl.BlockSpec(memory_space=pl.ANY)] + [full(a.shape) for a in args[1:]],
         out_specs=[full(sh) for sh in shapes],
         out_shape=[jax.ShapeDtypeStruct(sh, jnp.float32) for sh in shapes],
-        scratch_shapes=[pltpu.VMEM((3 * (steps - 1), rows, flat), jnp.float32)],
+        scratch_shapes=[
+            pltpu.VMEM((3 * (steps - 1), rows, flat), jnp.float32),
+            pltpu.VMEM((steps - 1,) + saved_pops.shape[1:], saved_pops.dtype),
+            pltpu.SemaphoreType.DMA((steps - 1,)),
+        ],
     )(*args)
 
 

time: 35.8 us -> 36.5 us (1.020)
  Pallas kernels: 9.97 us -> 10.6 us
    pallas_call x1, Pallas kernels: 2.69 us -> 3.33 us  [_messages(): pl.pallas_call(_prep_kernel, grid=(1,), in_specs=[pl.BlockSpec(memory_spa...]
where the time goes in v10:
time: 36.5 us; the launch traced here: 36.4 us
  starting transfers between devices  12.2 us (33%)
  waiting for transfers between devices  11.9 us (33%)
  Pallas kernels  10.6 us (29%)
  local copies, waits for them, and re-layouts  0.86 us (2%)
  between operations  0.73 us (2%)
    pallas_call x1, Pallas kernels, body(): pl.pallas_call(_fused_kernel, grid=(1,), in_specs=[full(a.shape) for a in...  7.28 us
    ppermute x1, waiting for transfers between devices, body(): cm = lax.ppermute(c_hi, 'gy', _shift(ny, 1))  5.29 us
    ppermute x1, starting transfers between devices, body(): hyp = lax.ppermute(y_lo, 'gy', _shift(ny, -1))  4.37 us
    ppermute x1, starting transfers between devices, body(): hxp = lax.ppermute(x_lo, 'gx', _shift(nx, -1))  4.2 us
    ppermute x1, starting transfers between devices, body(): cp = lax.ppermute(c_lo, 'gy', _shift(ny, -1))  3.54 us
    pallas_call x1, Pallas kernels, _messages(): pl.pallas_call(_prep_kernel, grid=(1,), in_specs=[pl.BlockSpec(memory_spa...  3.33 us
    ppermute x1, waiting for transfers between devices, body(): hxm = lax.ppermute(x_hi, 'gx', _shift(nx, 1))  3.2 us
    ppermute x1, waiting for transfers between devices, body(): cp = lax.ppermute(c_lo, 'gy', _shift(ny, -1))  1.43 us
  transfers between devices with their start and end apart: 6, of which 5 were waited for; matrix products, arithmetic and copies ran while one was open for 1% of the time, Pallas kernels for 0%

profile of v10, /device:TPU:0, one launch (start us, length us, event | category | flops | bytes accessed | tf_op | source)
XLA Modules:
  0.0 36.4 jit_solution(14206018893130440979)
XLA Ops:
  0.6 3.3 %shard_map.68 = (f32[120,512]{1,0:T(8,128)}, f32[120,512]{1,0:T(8,128)}, f32[30,16,128]{2,1,0:T(8,128)}, f32[30,16,128]{2,1,0:T(8,128)}) custom-call(bf16[4,19,16,512]{3,2,1,0:T(8,128)(2,1)} %pops_ref.1, f32[19,16,512]{2,1,0:T(8,128)} %seed_ref.3, s32[16,512]{1,0:T(8,128)} %solid_ref.3, s32[16,512]{1,0:T(8,128)} %mask_ref.3, f32[16,512]{1,0:T(8,128)} %field_ref.3), custom_call_target="tpu_custom_call" | custom-call | tf_op jit(solution)/shard_map/pallas_call | solution.py:296
  4.0 4.2 %collective-permute-start = (f32[120,512]{1,0:T(8,128)}, f32[120,512]{1,0:T(8,128)S(1)}, u32[]{:S(2)}, u32[]{:S(2)}) collective-permute-start(f32[120,512]{1,0:T(8,128)} %get-tuple-element.6), channel_id=1, source_target_pairs={{0,224},{32,0},{64,32},{96,64},{128,96},{160,128},{192,160},{224,1... | collective-permute-start | bytes 737288 | tf_op jit(solution)/shard_map/ppermute | solution.py:321
  8.2 0.0 collective-permute-start.1
  8.2 4.4 %collective-permute-start.2 = (f32[30,16,128]{2,1,0:T(8,128)}, f32[30,16,128]{2,1,0:T(8,128)S(1)}, u32[]{:S(2)}, u32[]{:S(2)}) collective-permute-start(f32[30,16,128]{2,1,0:T(8,128)} %get-tuple-element.8), channel_id=1, source_target_pairs={{0,31},{1,0},{2,1},{3,2},{4,3},{5,4},{6,5},{7,6},{8,7},{9,8},{10,9... | collective-permute-start | bytes 737288 | tf_op jit(solution)/shard_map/ppermute | solution.py:323
  12.5 0.0 collective-permute-start.3
  12.5 1.2 %collective-permute-done.hxp = f32[120,512]{1,0:T(8,128)S(1)} collective-permute-done((f32[120,512]{1,0:T(8,128)}, f32[120,512]{1,0:T(8,128)S(1)}, u32[]{:S(2)}, u32[]{:S(2)}) %collective-permute-start) | collective-permute-done | bytes 245792 | tf_op jit(solution)/shard_map/ppermute | solution.py:321
  13.7 0.1 reshape.16
  13.8 3.2 %collective-permute-done.1.hxm = f32[120,512]{1,0:T(8,128)S(1)} collective-permute-done((f32[120,512]{1,0:T(8,128)}, f32[120,512]{1,0:T(8,128)S(1)}, u32[]{:S(2)}, u32[]{:S(2)}) %collective-permute-start.1) | collective-permute-done | bytes 245792 | tf_op jit(solution)/shard_map/ppermute | solution.py:322
  17.0 0.1 reshape.17
  17.1 3.5 %collective-permute-start.4 = (f32[240,128]{1,0:T(8,128)S(1)}, f32[240,128]{1,0:T(8,128)S(1)}, u32[]{:S(2)}, u32[]{:S(2)}) collective-permute-start(f32[240,128]{1,0:T(8,128)S(1)} %maximum_bitcast_fusion), channel_id=1, source_target_pairs={{0,31},{1,0},{2,1},{3,2},{4,3},{5,4},{6,5},{7,6},{8,7},{9,8},{10,9... | collective-permute-start | bytes 368648 | tf_op jit(solution)/shard_map/ppermute | solution.py:330
  20.7 0.1 collective-permute-start.5
  20.8 0.0 collective-permute-done.2.hyp
  20.8 0.0 copy-start.2
  20.8 0.9 %collective-permute-done.3.hym = f32[30,16,128]{2,1,0:T(8,128)S(1)} collective-permute-done((f32[30,16,128]{2,1,0:T(8,128)}, f32[30,16,128]{2,1,0:T(8,128)S(1)}, u32[]{:S(2)}, u32[]{:S(2)}) %collective-permute-start.3) | collective-permute-done | bytes 245792 | tf_op jit(solution)/shard_map/ppermute | solution.py:324
  21.7 1.4 %collective-permute-done.4.cp = f32[240,128]{1,0:T(8,128)S(1)} collective-permute-done((f32[240,128]{1,0:T(8,128)S(1)}, f32[240,128]{1,0:T(8,128)S(1)}, u32[]{:S(2)}, u32[]{:S(2)}) %collective-permute-start.4) | collective-permute-done | bytes 122912 | tf_op jit(solution)/shard_map/ppermute | solution.py:330
  23.1 5.3 %collective-permute-done.5.cm = f32[240,128]{1,0:T(8,128)S(1)} collective-permute-done((f32[240,128]{1,0:T(8,128)S(1)}, f32[240,128]{1,0:T(8,128)S(1)}, u32[]{:S(2)}, u32[]{:S(2)}) %collective-permute-start.5) | collective-permute-done | bytes 122912 | tf_op jit(solution)/shard_map/ppermute | solution.py:331
  28.4 0.0 copy-done
  28.4 0.0 copy-done.1
  28.4 0.0 copy-done.2
  28.4 0.0 copy-done.3
  28.4 0.0 copy-done.4
  28.4 0.0 copy-start.5
  28.5 0.7 %copy-done.5 = f32[240,128]{1,0:T(8,128)} copy-done((f32[240,128]{1,0:T(8,128)}, f32[240,128]{1,0:T(8,128)S(1)}, u32[]{:S(2)}) %copy-start.5) | copy-done | bytes 122904
  29.1 7.3 %shard_map.69 = (f32[19,16,512]{2,1,0:T(8,128)}, f32[16,512]{1,0:T(8,128)}) custom-call(bf16[4,19,16,512]{3,2,1,0:T(8,128)(2,1)} %pops_ref.1, f32[19,16,512]{2,1,0:T(8,128)} %seed_ref.3, s32[16,512]{1,0:T(8,128)} %solid_ref.3, s32[16,512]{1,0:T(8,128)} %mask_ref.3, f32[16,512]{1,0:T(8,128)} %field_ref.3, f32[120,512]{1,0:T(8,128)} %copy-done, ...), custom_call_target="tpu_custom_call" | custom-call | tf_op jit(solution)/shard_map/pallas_call | solution.py:341
  (8 shorter events, 0.1 us)
Async XLA Ops:
  4.0 9.7 %collective-permute-start = (f32[120,512]{1,0:T(8,128)}, f32[120,512]{1,0:T(8,128)S(1)}, u32[]{:S(2)}, u32[]{:S(2)}) collective-permute-start(f32[120,512]{1,0:T(8,128)} %get-tuple-element.6), channel_id=1, source_target_pairs={{0,224},{32,0},{64,32},{96,64},{128,96},{160,128},{192,160},{224,1... | collective-permute-start | bytes 737288 | tf_op jit(solution)/shard_map/ppermute | solution.py:321
  8.2 8.8 %collective-permute-start.1 = (f32[120,512]{1,0:T(8,128)}, f32[120,512]{1,0:T(8,128)S(1)}, u32[]{:S(2)}, u32[]{:S(2)}) collective-permute-start(f32[120,512]{1,0:T(8,128)} %get-tuple-element.7), channel_id=1, source_target_pairs={{0,32},{32,64},{64,96},{96,128},{128,160},{160,192},{192,224},{224... | collective-permute-start | bytes 737288 | tf_op jit(solution)/shard_map/ppermute | solution.py:322
  8.2 12.6 %collective-permute-start.2 = (f32[30,16,128]{2,1,0:T(8,128)}, f32[30,16,128]{2,1,0:T(8,128)S(1)}, u32[]{:S(2)}, u32[]{:S(2)}) collective-permute-start(f32[30,16,128]{2,1,0:T(8,128)} %get-tuple-element.8), channel_id=1, source_target_pairs={{0,31},{1,0},{2,1},{3,2},{4,3},{5,4},{6,5},{7,6},{8,7},{9,8},{10,9... | collective-permute-start | bytes 737288 | tf_op jit(solution)/shard_map/ppermute | solution.py:323
  12.5 9.2 %collective-permute-start.3 = (f32[30,16,128]{2,1,0:T(8,128)}, f32[30,16,128]{2,1,0:T(8,128)S(1)}, u32[]{:S(2)}, u32[]{:S(2)}) collective-permute-start(f32[30,16,128]{2,1,0:T(8,128)} %get-tuple-element.9), channel_id=1, source_target_pairs={{0,1},{1,2},{2,3},{3,4},{4,5},{5,6},{6,7},{7,8},{8,9},{9,10},{10,1... | collective-permute-start | bytes 737288 | tf_op jit(solution)/shard_map/ppermute | solution.py:324
  13.7 14.7 %copy-start = (f32[120,512]{1,0:T(8,128)}, f32[120,512]{1,0:T(8,128)S(1)}, u32[]{:S(2)}) copy-start(f32[120,512]{1,0:T(8,128)S(1)} %collective-permute-done.hxp) | copy-start | bytes 737284
  17.0 11.4 %copy-start.1 = (f32[120,512]{1,0:T(8,128)}, f32[120,512]{1,0:T(8,128)S(1)}, u32[]{:S(2)}) copy-start(f32[120,512]{1,0:T(8,128)S(1)} %collective-permute-done.1.hxm) | copy-start | bytes 737284
  17.1 6.0 %collective-permute-start.4 = (f32[240,128]{1,0:T(8,128)S(1)}, f32[240,128]{1,0:T(8,128)S(1)}, u32[]{:S(2)}, u32[]{:S(2)}) collective-permute-start(f32[240,128]{1,0:T(8,128)S(1)} %maximum_bitcast_fusion), channel_id=1, source_target_pairs={{0,31},{1,0},{2,1},{3,2},{4,3},{5,4},{6,5},{7,6},{8,7},{9,8},{10,9... | collective-permute-start | bytes 368648 | tf_op jit(solution)/shard_map/ppermute | solution.py:330
  20.7 7.7 %collective-permute-start.5 = (f32[240,128]{1,0:T(8,128)S(1)}, f32[240,128]{1,0:T(8,128)S(1)}, u32[]{:S(2)}, u32[]{:S(2)}) collective-permute-start(f32[240,128]{1,0:T(8,128)S(1)} %maximum_bitcast_fusion.1), channel_id=1, source_target_pairs={{0,1},{1,2},{2,3},{3,4},{4,5},{5,6},{6,7},{7,8},{8,9},{9,10},{10,1... | collective-permute-start | bytes 368648 | tf_op jit(solution)/shard_map/ppermute | solution.py:331
  20.8 7.6 %copy-start.2 = (f32[30,16,128]{2,1,0:T(8,128)}, f32[30,16,128]{2,1,0:T(8,128)S(1)}, u32[]{:S(2)}) copy-start(f32[30,16,128]{2,1,0:T(8,128)S(1)} %collective-permute-done.2.hyp) | copy-start | bytes 737284
  21.7 6.7 %copy-start.3 = (f32[30,16,128]{2,1,0:T(8,128)}, f32[30,16,128]{2,1,0:T(8,128)S(1)}, u32[]{:S(2)}) copy-start(f32[30,16,128]{2,1,0:T(8,128)S(1)} %collective-permute-done.3.hym) | copy-start | bytes 737284
  23.1 5.3 %copy-start.4 = (f32[240,128]{1,0:T(8,128)}, f32[240,128]{1,0:T(8,128)S(1)}, u32[]{:S(2)}) copy-start(f32[240,128]{1,0:T(8,128)S(1)} %collective-permute-done.4.cp) | copy-start | bytes 368644
  28.4 0.7 %copy-start.5 = (f32[240,128]{1,0:T(8,128)}, f32[240,128]{1,0:T(8,128)S(1)}, u32[]{:S(2)}) copy-start(f32[240,128]{1,0:T(8,128)S(1)} %collective-permute-done.5.cm) | copy-start | bytes 368644
